TPU v7x, 256 devices: a whole 4x4x8 slice. The times are simulated.
256 devices in a mesh: gz: 32 (over x, z), gx: 8 (over y, core).
Axes of the slice: x: 4, y: 4, z: 8, core: 2. Of those that a mesh axis runs over, the one named last changes fastest.
Arguments:
- u_field: bfloat16 [2, 512, 2048, 128], P(None, 'gx', 'gz'), may hold values from -64 to 64, as said below
- w_field: bfloat16 [2, 512, 2048, 128], P(None, 'gx', 'gz'), may hold values from -64 to 64, as said below
Outputs:
- modes: float32 [2, 512, 2048, 128], P(None, 'gx', 'gz')
- factor_r: float32 [2, 128, 128], replicated
Inputs may be any that keep to these rules, and one draw needn't show every extreme that they name: `u_field`: velocity values of a snapshot. `w_field`: velocity values of a snapshot.
All inputs are finite; a program needn't handle non-finite values.
Results may differ from a plain program's by a relative error of at most 0.0003.
Values may be sent and summed in bfloat16 or wider, within the bound.
No kernel may reach another device: no remote copies, remote signals or barrier semaphores. Data moves between devices by JAX's collectives and lax.ppermute only.
A program may use at most 64 MiB of HBM per device.

v0:
```python
import jax
import jax.numpy as jnp
from jax import lax
from jax.sharding import PartitionSpec as P

span_step = 0.75


def with_halo(cells, sides, width):
    for axis, dim in sides:
        count = lax.axis_size(axis)
        head = lax.slice_in_dim(cells, 0, width, axis=dim)
        tail = lax.slice_in_dim(cells, cells.shape[dim] - width, cells.shape[dim], axis=dim)
        cells = jnp.concatenate(
            [
                lax.ppermute(tail, axis, [(i, (i + 1) % count) for i in range(count)]),
                cells,
                lax.ppermute(head, axis, [((i + 1) % count, i) for i in range(count)]),
            ],
            axis=dim,
        )
    return cells


def local(u_field, w_field):
    planes, rows_x, rows_z, snaps = u_field.shape
    padded_u = with_halo(u_field, (("gz", 2),), 2).astype(jnp.float32)
    padded_w = with_halo(w_field, (("gx", 1),), 2).astype(jnp.float32)
    span_diff = 8.0 * (padded_u[:, :, 3:-1] - padded_u[:, :, 1:-3]) - (
        padded_u[:, :, 4:] - padded_u[:, :, :-4]
    )
    stream_diff = 8.0 * (padded_w[:, 3:-1] - padded_w[:, 1:-3]) - (
        padded_w[:, 4:] - padded_w[:, :-4]
    )
    vorticity = span_diff / (12.0 * span_step) - stream_diff / 12.0
    columns = vorticity.reshape(planes, rows_x * rows_z, snaps)
    gram_local = jnp.einsum(
        "pcs,pct->pst",
        columns,
        columns,
        precision=lax.Precision.HIGHEST,
        preferred_element_type=jnp.float32,
    )
    gram_sum = lax.psum(gram_local, ("gz", "gx"))
    total_cells = rows_x * rows_z * lax.axis_size("gz") * lax.axis_size("gx")
    gram = gram_sum / total_cells
    lower = jnp.linalg.cholesky(gram)
    identity_matrix = jnp.broadcast_to(jnp.eye(snaps, dtype=gram.dtype), lower.shape)
    lower_inverse = lax.linalg.triangular_solve(lower, identity_matrix, left_side=True, lower=True)
    inverse_r = jnp.transpose(lower_inverse, (0, 2, 1))
    modes = jnp.einsum(
        "pcs,pst->pct",
        columns,
        inverse_r,
        precision=lax.Precision.HIGHEST,
        preferred_element_type=jnp.float32,
    )
    modes = modes.reshape(planes, rows_x, rows_z, snaps)
    factor_r = jnp.transpose(lower, (0, 2, 1))
    return (modes, factor_r)


def solution(mesh):
    return jax.shard_map(
        local,
        mesh=mesh,
        in_specs=(P(None, "gx", "gz", None), P(None, "gx", "gz", None)),
        out_specs=(P(None, "gx", "gz", None), P()),
        check_vma=False,
    )
```

profile of v0, /device:TPU:8, one launch (start us, length us, event | category | flops | bytes accessed | tf_op | source)
XLA Modules:
  0.0 339.0 jit_solution(9191449530525586369)
XLA Ops:
  7.2 0.0 copy-start.1
  7.2 0.0 all-reduce.2.cloned.1.call-start
  7.2 1.3 fusion.13
  8.5 2.0 collective-permute-start
  10.5 6.2 %collective-permute-start.1 = (bf16[2,64,2,128]{3,2,1,0:T(2,128)(2,1)S(1)}, bf16[2,64,2,128]{3,2,1,0:T(2,128)(2,1)S(1)}, u32[]{:S(2)}, u32[]{:S(2)}) collective-permute-start(bf16[2,64,2,128]{3,2,1,0:T(2,128)(2,1)S(1)} %get-tuple-element.7), channel_id=1, source_target_pairs={{8,0},{16,8},{24,16},{32,24},{40,32},{48,40},{56,48},{64,56},{72,6... | collective-permute-start | bytes 196616 | tf_op jit(solution)/shard_map/ppermute | solution.py:18
  16.7 0.9 fusion.14
  17.6 0.0 collective-permute-start.2
  17.6 1.7 collective-permute-start.3
  19.4 0.0 collective-permute-done
  19.4 0.0 collective-permute-done.1
  19.4 2.8 maximum_convert_fusion
  22.2 0.0 collective-permute-done.2
  22.2 0.0 collective-permute-done.3
  22.2 0.0 copy-done.1
  22.2 0.3 maximum_convert_fusion.1
  22.6 2.8 fusion.2
  25.4 0.0 copy-start
  25.4 1.9 copy-done
  27.3 7.5 %fusion.15 = f32[2,128,128]{1,2,0:T(8,128)} fusion(f32[2,4096,128]{2,1,0:T(8,128)S(1)} %bitcast.17), kind=kOutput, calls=%fused_computation.29 | convolution fusion | flops 1610612736 | bytes 4325376 | tf_op jit(solution)/shard_map/pcs,pct->pst/dot_general | solution.py:37
  34.8 0.0 all-reduce.2.cloned.1.call-update
  34.9 244.0 %all-reduce.2.cloned.1.call-done = f32[2,128,128]{1,2,0:T(8,128)} async-done(((f32[2,128,128]{1,2,0:T(8,128)}), f32[2,128,128]{1,2,0:T(8,128)}) %all-reduce.2.cloned.1.call-update) | async-done | bytes 131088 | tf_op jit(solution)/shard_map/psum | solution.py:44
  278.9 0.9 broadcast_multiply_fusion
  279.8 0.1 copy.10
  279.9 0.9 fusion.9
  280.9 23.6 %custom-call.7 = f32[2,128,128]{2,1,0:T(8,128)S(1)} custom-call(f32[2,128,128]{2,1,0:T(8,128)S(1)} %fusion.9), custom_call_target="Cholesky" | custom-call | tf_op jit(solution)/shard_map/jit(cholesky)/cholesky | solution.py:47
  304.5 0.1 compare_reduce_fusion
  304.7 0.1 fusion.10
  304.8 19.7 %custom-call.8 = f32[2,1,128,128]{2,3,1,0:T(8,128)S(1)} custom-call(f32[2,1,128,128]{3,2,1,0:T(8,128)S(1)} %get-tuple-element.11), custom_call_target="InvertDiagBlocksLowerTriangular" | custom-call | tf_op jit(solution)/shard_map/triangular_solve | solution.py:49
  324.5 0.4 fusion.7
  324.9 6.5 %fusion.16 = f32[2,4096,128]{2,1,0:T(8,128)} fusion(f32[2,4096,128]{2,1,0:T(8,128)} %bitcast.18, f32[2,128,128]{2,1,0:T(8,128)S(1)} %fusion.7), kind=kOutput, calls=%fused_computation.30 | convolution fusion | flops 1610612736 | bytes 8519680 | tf_op jit(solution)/shard_map/pcs,pst->pct/dot_general | solution.py:51
  331.4 0.8 copy.11
  (4 shorter events, 0.1 us)
Async XLA Ops:
  7.2 15.1 %copy-start.1 = (bf16[2,64,64,128]{3,2,1,0:T(8,128)(2,1)S(1)}, bf16[2,64,64,128]{3,2,1,0:T(8,128)(2,1)}, u32[]{:S(2)}) copy-start(bf16[2,64,64,128]{3,2,1,0:T(8,128)(2,1)} %param.3) | copy-start | bytes 6291460
  7.2 271.8 %all-reduce.2.cloned.1.call-start = ((), (), s32[]{:S(2)}) async-start(), calls=%async_computation | async-start | bytes 262144 | tf_op jit(solution)/shard_map/psum | solution.py:44
  8.5 10.9 %collective-permute-start = (bf16[2,64,2,128]{3,2,1,0:T(2,128)(2,1)S(1)}, bf16[2,64,2,128]{3,2,1,0:T(2,128)(2,1)S(1)}, u32[]{:S(2)}, u32[]{:S(2)}) collective-permute-start(bf16[2,64,2,128]{3,2,1,0:T(2,128)(2,1)S(1)} %get-tuple-element.6), channel_id=1, source_target_pairs={{0,8},{8,16},{16,24},{24,32},{32,40},{40,48},{48,56},{56,64},{64,7... | collective-permute-start | bytes 196616 | tf_op jit(solution)/shard_map/ppermute | solution.py:16
  10.5 8.9 %collective-permute-start.1 = (bf16[2,64,2,128]{3,2,1,0:T(2,128)(2,1)S(1)}, bf16[2,64,2,128]{3,2,1,0:T(2,128)(2,1)S(1)}, u32[]{:S(2)}, u32[]{:S(2)}) collective-permute-start(bf16[2,64,2,128]{3,2,1,0:T(2,128)(2,1)S(1)} %get-tuple-element.7), channel_id=1, source_target_pairs={{8,0},{16,8},{24,16},{32,24},{40,32},{48,40},{56,48},{64,56},{72,6... | collective-permute-start | bytes 196616 | tf_op jit(solution)/shard_map/ppermute | solution.py:18
  17.6 4.6 %collective-permute-start.2 = (bf16[2,2,64,128]{3,2,1,0:T(8,128)(2,1)S(1)}, bf16[2,2,64,128]{3,2,1,0:T(8,128)(2,1)S(1)}, u32[]{:S(2)}, u32[]{:S(2)}) collective-permute-start(bf16[2,2,64,128]{3,2,1,0:T(8,128)(2,1)S(1)} %get-tuple-element.8), channel_id=1, source_target_pairs={{0,1},{1,2},{2,3},{3,4},{4,5},{5,6},{6,7},{7,0},{8,9},{9,10},{10,1... | collective-permute-start | bytes 196616 | tf_op jit(solution)/shard_map/ppermute | solution.py:16
  17.6 4.6 %collective-permute-start.3 = (bf16[2,2,64,128]{3,2,1,0:T(8,128)(2,1)S(1)}, bf16[2,2,64,128]{3,2,1,0:T(8,128)(2,1)S(1)}, u32[]{:S(2)}, u32[]{:S(2)}) collective-permute-start(bf16[2,2,64,128]{3,2,1,0:T(8,128)(2,1)S(1)} %get-tuple-element.9), channel_id=1, source_target_pairs={{1,0},{2,1},{3,2},{4,3},{5,4},{6,5},{7,6},{0,7},{9,8},{10,9},{11,1... | collective-permute-start | bytes 196616 | tf_op jit(solution)/shard_map/ppermute | solution.py:18
  25.4 1.9 copy-start
Sparse Core Ops, SparseCore 0:
  35.0 243.8 all-reduce.1
where the time goes:
time: 339 us
  waiting for transfers between devices  244 us (72%)
  other arithmetic  51.3 us (15%)
  matrix products  14.5 us (4%)
  between operations  14.2 us (4%)
  starting transfers between devices  10 us (3%)
  local copies, waits for them, and re-layouts  4.96 us (1%)
    psum x1, waiting for transfers between devices, local(): gram_sum = lax.psum(gram_local, ('gz', 'gx'))  244 us
    another operation x4, other arithmetic, local(): lower = jnp.linalg.cholesky(gram)  23.8 us
    another operation x2, other arithmetic, local(): lax.linalg.triangular_solve(lower, identity_matrix, left_side=True, lower...  19.7 us
    ppermute x2, starting transfers between devices, with_halo(): lax.ppermute(head, axis, [((i + 1) % count, i) for i in range(count)])  7.96 us
    dot_general x1, matrix products, local(): jnp.einsum('pcs,pct->pst', columns, columns, precision=lax.Precision.HIGH...  7.54 us
  transfers between devices with their start and end apart: 5, of which 1 were waited for; matrix products, arithmetic and copies ran while one was open for 1% of the time, Pallas kernels for 0%

commit v1 on v0

--- a/solution.py
+++ b/solution.py
@@ -22,6 +22,38 @@
     return cells
 
 
+def butterfly_sum(x, axes):
+    for axis in axes:
+        count = lax.axis_size(axis)
+        step = 1
+        while step < count:
+            x = x + lax.ppermute(x, axis, [(i, i ^ step) for i in range(count)])
+            step *= 2
+    return x
+
+
+def pack_pair(gram):
+    n = gram.shape[-1]
+    row = lax.broadcasted_iota(jnp.int32, (n, n), 0)
+    col = lax.broadcasted_iota(jnp.int32, (n, n), 1)
+    square = jnp.where(row <= col, gram[0], gram[1])
+    diag = jnp.diagonal(gram[1])[None, :]
+    pad = jnp.zeros((7, n), gram.dtype)
+    return jnp.concatenate([square, diag, pad], axis=0)
+
+
+def unpack_pair(packed):
+    n = packed.shape[-1]
+    square = packed[:n]
+    diag = packed[n]
+    row = lax.broadcasted_iota(jnp.int32, (n, n), 0)
+    col = lax.broadcasted_iota(jnp.int32, (n, n), 1)
+    flipped = square.T
+    first = jnp.where(row <= col, square, flipped)
+    second = jnp.where(row > col, square, jnp.where(row < col, flipped, jnp.diag(diag)))
+    return jnp.stack([first, second])
+
+
 def local(u_field, w_field):
     planes, rows_x, rows_z, snaps = u_field.shape
     padded_u = with_halo(u_field, (("gz", 2),), 2).astype(jnp.float32)
@@ -41,7 +73,10 @@
         precision=lax.Precision.HIGHEST,
         preferred_element_type=jnp.float32,
     )
-    gram_sum = lax.psum(gram_local, ("gz", "gx"))
+    if planes == 2:
+        gram_sum = unpack_pair(butterfly_sum(pack_pair(gram_local), ("gx", "gz")))
+    else:
+        gram_sum = butterfly_sum(gram_local, ("gx", "gz"))
     total_cells = rows_x * rows_z * lax.axis_size("gz") * lax.axis_size("gx")
     gram = gram_sum / total_cells
     lower = jnp.linalg.cholesky(gram)

time: 339 us -> 127 us (0.37)
  waiting for transfers between devices: 244 us -> 37.5 us
  between operations: 14.2 us -> 0.89 us
  starting transfers between devices: 10 us -> 20.2 us
    psum x1 -> x0, waiting for transfers between devices: 244 us -> none  [local(): gram_sum = lax.psum(gram_local, ('gz', 'gx'))]
    ppermute x0 -> x8, waiting for transfers between devices: none -> 37.4 us  [butterfly_sum(): x = x + lax.ppermute(x, axis, [(i, i ^ step) for i in range(count)])]
    ppermute x0 -> x8, starting transfers between devices: none -> 10.2 us  [butterfly_sum(): x = x + lax.ppermute(x, axis, [(i, i ^ step) for i in range(count)])]
  transfers between devices with their start and end apart: 5 -> 12, of which waited for: 1 -> 8; matrix products, arithmetic and copies ran while one was open for 1% -> 3% of each run, Pallas kernels for 0% -> 0%
where the time goes in v1:
time: 127 us
  other arithmetic  49.5 us (39%)
  waiting for transfers between devices  37.5 us (30%)
  starting transfers between devices  20.2 us (16%)
  matrix products  13.8 us (11%)
  local copies, waits for them, and re-layouts  4.93 us (4%)
    ppermute x8, waiting for transfers between devices, butterfly_sum(): x = x + lax.ppermute(x, axis, [(i, i ^ step) for i in range(count)])  37.4 us
    another operation x4, other arithmetic, local(): lower = jnp.linalg.cholesky(gram)  23.6 us
    another operation x2, other arithmetic, local(): lax.linalg.triangular_solve(lower, identity_matrix, left_side=True, lower...  19.7 us
    ppermute x8, starting transfers between devices, butterfly_sum(): x = x + lax.ppermute(x, axis, [(i, i ^ step) for i in range(count)])  10.2 us
    ppermute x2, starting transfers between devices, with_halo(): lax.ppermute(head, axis, [((i + 1) % count, i) for i in range(count)])  7.96 us
    dot_general x1, matrix products, local(): jnp.einsum('pcs,pct->pst', columns, columns, precision=lax.Precision.HIGH...  6.89 us
    dot_general x1, matrix products, local(): jnp.einsum('pcs,pst->pct', columns, inverse_r, precision=lax.Precision.HI...  6.55 us
    convert_element_type x1, other arithmetic, local(): padded_u = with_halo(u_field, (('gz', 2),), 2).astype(jnp.float32)  2.78 us
  transfers between devices with their start and end apart: 12, of which 8 were waited for; matrix products, arithmetic and copies ran while one was open for 3% of the time, Pallas kernels for 0%

profile of v1, /device:TPU:8, one launch (start us, length us, event | category | flops | bytes accessed | tf_op | source)
XLA Modules:
  0.0 126.8 jit_solution(5239366548244477162)
XLA Ops:
  0.6 1.3 %fusion.17 = (bf16[2,64,2,128]{3,2,1,0:T(2,128)(2,1)S(1)}, bf16[2,64,2,128]{3,2,1,0:T(2,128)(2,1)S(1)}) fusion(bf16[2,64,64,128]{3,2,1,0:T(8,128)(2,1)} %param.2), kind=kLoop, calls=%fused_computation.42 | loop fusion | bytes 262144 | tf_op jit(solution)/shard_map/slice | solution.py:13
  1.9 2.0 %collective-permute-start = (bf16[2,64,2,128]{3,2,1,0:T(2,128)(2,1)S(1)}, bf16[2,64,2,128]{3,2,1,0:T(2,128)(2,1)S(1)}, u32[]{:S(2)}, u32[]{:S(2)}) collective-permute-start(bf16[2,64,2,128]{3,2,1,0:T(2,128)(2,1)S(1)} %get-tuple-element.8), channel_id=1, source_target_pairs={{0,8},{8,16},{16,24},{24,32},{32,40},{40,48},{48,56},{56,64},{64,7... | collective-permute-start | bytes 196616 | tf_op jit(solution)/shard_map/ppermute | solution.py:16
  3.9 6.2 %collective-permute-start.1 = (bf16[2,64,2,128]{3,2,1,0:T(2,128)(2,1)S(1)}, bf16[2,64,2,128]{3,2,1,0:T(2,128)(2,1)S(1)}, u32[]{:S(2)}, u32[]{:S(2)}) collective-permute-start(bf16[2,64,2,128]{3,2,1,0:T(2,128)(2,1)S(1)} %get-tuple-element.9), channel_id=1, source_target_pairs={{8,0},{16,8},{24,16},{32,24},{40,32},{48,40},{56,48},{64,56},{72,6... | collective-permute-start | bytes 196616 | tf_op jit(solution)/shard_map/ppermute | solution.py:18
  10.2 0.9 fusion.18
  11.1 1.7 %collective-permute-start.3 = (bf16[2,2,64,128]{3,2,1,0:T(8,128)(2,1)S(1)}, bf16[2,2,64,128]{3,2,1,0:T(8,128)(2,1)S(1)}, u32[]{:S(2)}, u32[]{:S(2)}) collective-permute-start(bf16[2,2,64,128]{3,2,1,0:T(8,128)(2,1)S(1)} %get-tuple-element.11), channel_id=1, source_target_pairs={{1,0},{2,1},{3,2},{4,3},{5,4},{6,5},{7,6},{0,7},{9,8},{10,9},{11,1... | collective-permute-start | bytes 196616 | tf_op jit(solution)/shard_map/ppermute | solution.py:18
  12.9 2.8 %maximum_convert_fusion = f32[2,64,68,128]{3,2,1,0:T(8,128)S(1)} fusion(bf16[2,64,2,128]{3,2,1,0:T(2,128)(2,1)S(1)} %collective-permute-done.1, bf16[2,64,64,128]{3,2,1,0:T(8,128)(2,1)} %param.2, bf16[2,64,2,128]{3,2,1,0:T(2,128)(2,1)S(1)} %collective-permute-done), kind=kLoop, calls=%fused_computation.12 | loop fusion | flops 6684672 | bytes 6684672 | tf_op jit(solution)/shard_map/convert_element_type | solution.py:59
  15.7 0.3 maximum_convert_fusion.1
  16.1 2.8 %fusion.2 = f32[2,64,64,128]{3,2,1,0:T(8,128)S(1)} fusion(f32[2,68,64,128]{3,2,1,0:T(8,128)S(1)} %maximum_convert_fusion.1, f32[2,64,68,128]{3,2,1,0:T(8,128)S(1)} %maximum_convert_fusion), kind=kLoop, calls=%fused_computation.4 | loop fusion | flops 11534336 | bytes 37748736 | tf_op jit(solution)/shard_map/sub | solution.py:67
  18.9 6.9 %fusion.19 = f32[2,128,128]{1,2,0:T(8,128)S(1)} fusion(f32[2,4096,128]{2,1,0:T(8,128)S(1)} %bitcast.41), kind=kOutput, calls=%fused_computation.44 | convolution fusion | flops 1610612736 | bytes 4325376 | tf_op jit(solution)/shard_map/pcs,pct->pst/dot_general | solution.py:69
  25.8 1.3 %gather_fusion = f32[128]{0:T(128)S(1)} fusion(f32[128,128]{0,1:T(8,128)S(1)} %slice_bitcast_fusion, s32[128]{0:T(128)S(1)} %or_bitcast_fusion), kind=kCustom, calls=%fused_computation | custom fusion | bytes 2048 | tf_op jit(solution)/shard_map/jit(diagonal)/cond/branch_0_fun/gather | solution.py:40
  27.2 0.8 collective-permute-start.4
  28.0 1.0 collective-permute-done.4
  29.0 1.4 %collective-permute-start.5 = (f32[136,128]{0,1:T(8,128)S(1)}, f32[136,128]{0,1:T(8,128)S(1)}, u32[]{:S(2)}, u32[]{:S(2)}) collective-permute-start(f32[136,128]{0,1:T(8,128)S(1)} %fusion.25), channel_id=1, source_target_pairs={{0,2},{1,3},{2,0},{3,1},{4,6},{5,7},{6,4},{7,5},{8,10},{9,11},{10,... | collective-permute-start | bytes 208904 | tf_op jit(solution)/shard_map/ppermute | solution.py:30
  30.4 4.5 %collective-permute-done.5 = f32[136,128]{0,1:T(8,128)S(1)} collective-permute-done((f32[136,128]{0,1:T(8,128)S(1)}, f32[136,128]{0,1:T(8,128)S(1)}, u32[]{:S(2)}, u32[]{:S(2)}) %collective-permute-start.5) | collective-permute-done | bytes 69664 | tf_op jit(solution)/shard_map/ppermute | solution.py:30
  34.9 2.4 %collective-permute-start.6 = (f32[136,128]{0,1:T(8,128)S(1)}, f32[136,128]{0,1:T(8,128)S(1)}, u32[]{:S(2)}, u32[]{:S(2)}) collective-permute-start(f32[136,128]{0,1:T(8,128)S(1)} %add.40), channel_id=1, source_target_pairs={{0,4},{1,5},{2,6},{3,7},{4,0},{5,1},{6,2},{7,3},{8,12},{9,13},{10,... | collective-permute-start | bytes 208904 | tf_op jit(solution)/shard_map/ppermute | solution.py:30
  37.3 4.3 %collective-permute-done.6 = f32[136,128]{0,1:T(8,128)S(1)} collective-permute-done((f32[136,128]{0,1:T(8,128)S(1)}, f32[136,128]{0,1:T(8,128)S(1)}, u32[]{:S(2)}, u32[]{:S(2)}) %collective-permute-start.6) | collective-permute-done | bytes 69664 | tf_op jit(solution)/shard_map/ppermute | solution.py:30
  41.8 5.0 %collective-permute-done.7 = f32[136,128]{0,1:T(8,128)S(1)} collective-permute-done((f32[136,128]{0,1:T(8,128)S(1)}, f32[136,128]{0,1:T(8,128)S(1)}, u32[]{:S(2)}, u32[]{:S(2)}) %collective-permute-start.7) | collective-permute-done | bytes 69664 | tf_op jit(solution)/shard_map/ppermute | solution.py:30
  46.7 0.4 collective-permute-start.8
  47.1 6.5 %collective-permute-done.8 = f32[136,128]{0,1:T(8,128)S(1)} collective-permute-done((f32[136,128]{0,1:T(8,128)S(1)}, f32[136,128]{0,1:T(8,128)S(1)}, u32[]{:S(2)}, u32[]{:S(2)}) %collective-permute-start.8) | collective-permute-done | bytes 69664 | tf_op jit(solution)/shard_map/ppermute | solution.py:30
  53.6 2.3 %collective-permute-start.9 = (f32[136,128]{0,1:T(8,128)S(1)}, f32[136,128]{0,1:T(8,128)S(1)}, u32[]{:S(2)}, u32[]{:S(2)}) collective-permute-start(f32[136,128]{0,1:T(8,128)S(1)} %add.43), channel_id=1, source_target_pairs={{0,32},{8,40},{16,48},{24,56},{32,0},{40,8},{48,16},{56,24},{64,96... | collective-permute-start | bytes 208904 | tf_op jit(solution)/shard_map/ppermute | solution.py:30
  55.9 0.1 copy.22
  56.1 7.6 %collective-permute-done.9 = f32[136,128]{0,1:T(8,128)S(1)} collective-permute-done((f32[136,128]{0,1:T(8,128)S(1)}, f32[136,128]{0,1:T(8,128)S(1)}, u32[]{:S(2)}, u32[]{:S(2)}) %collective-permute-start.9) | collective-permute-done | bytes 69664 | tf_op jit(solution)/shard_map/ppermute | solution.py:30
  63.7 0.2 collective-permute-start.10
  64.0 4.8 %collective-permute-done.10 = f32[136,128]{0,1:T(8,128)S(1)} collective-permute-done((f32[136,128]{0,1:T(8,128)S(1)}, f32[136,128]{0,1:T(8,128)S(1)}, u32[]{:S(2)}, u32[]{:S(2)}) %collective-permute-start.10) | collective-permute-done | bytes 69664 | tf_op jit(solution)/shard_map/ppermute | solution.py:30
  68.7 2.6 %collective-permute-start.11 = (f32[136,128]{0,1:T(8,128)S(1)}, f32[136,128]{0,1:T(8,128)S(1)}, u32[]{:S(2)}, u32[]{:S(2)}) collective-permute-start(f32[136,128]{0,1:T(8,128)S(1)} %add.45), channel_id=1, source_target_pairs={{0,128},{8,136},{16,144},{24,152},{32,160},{40,168},{48,176},{56,1... | collective-permute-start | bytes 208904 | tf_op jit(solution)/shard_map/ppermute | solution.py:30
  71.4 3.9 %collective-permute-done.11 = f32[136,128]{0,1:T(8,128)S(1)} collective-permute-done((f32[136,128]{0,1:T(8,128)S(1)}, f32[136,128]{0,1:T(8,128)S(1)}, u32[]{:S(2)}, u32[]{:S(2)}) %collective-permute-start.11) | collective-permute-done | bytes 69664 | tf_op jit(solution)/shard_map/ppermute | solution.py:30
  75.7 23.5 %custom-call.7 = f32[2,128,128]{2,1,0:T(8,128)S(1)} custom-call(f32[2,128,128]{2,1,0:T(8,128)S(1)} %fusion.9), custom_call_target="Cholesky" | custom-call | tf_op jit(solution)/shard_map/jit(cholesky)/cholesky | solution.py:82
  99.2 0.1 compare_reduce_fusion
  99.4 19.7 %custom-call.8 = f32[2,1,128,128]{2,3,1,0:T(8,128)S(1)} custom-call(f32[2,1,128,128]{3,2,1,0:T(8,128)S(1)} %get-tuple-element.15), custom_call_target="InvertDiagBlocksLowerTriangular" | custom-call | tf_op jit(solution)/shard_map/triangular_solve | solution.py:84
  119.1 0.4 fusion.7
  119.5 6.5 %fusion.20 = f32[2,4096,128]{2,1,0:T(8,128)} fusion(f32[2,4096,128]{2,1,0:T(8,128)} %bitcast.42, f32[2,128,128]{2,1,0:T(8,128)S(1)} %fusion.7), kind=kOutput, calls=%fused_computation.45 | convolution fusion | flops 1610612736 | bytes 8519680 | tf_op jit(solution)/shard_map/pcs,pst->pct/dot_general | solution.py:86
  126.1 0.8 copy.31
  (38 shorter events, 1.1 us)
Async XLA Ops:
  0.6 15.1 %copy-start.1 = (bf16[2,64,64,128]{3,2,1,0:T(8,128)(2,1)S(1)}, bf16[2,64,64,128]{3,2,1,0:T(8,128)(2,1)}, u32[]{:S(2)}) copy-start(bf16[2,64,64,128]{3,2,1,0:T(8,128)(2,1)} %param.3) | copy-start | bytes 6291460
  1.9 11.0 %collective-permute-start = (bf16[2,64,2,128]{3,2,1,0:T(2,128)(2,1)S(1)}, bf16[2,64,2,128]{3,2,1,0:T(2,128)(2,1)S(1)}, u32[]{:S(2)}, u32[]{:S(2)}) collective-permute-start(bf16[2,64,2,128]{3,2,1,0:T(2,128)(2,1)S(1)} %get-tuple-element.8), channel_id=1, source_target_pairs={{0,8},{8,16},{16,24},{24,32},{32,40},{40,48},{48,56},{56,64},{64,7... | collective-permute-start | bytes 196616 | tf_op jit(solution)/shard_map/ppermute | solution.py:16
  3.9 9.0 %collective-permute-start.1 = (bf16[2,64,2,128]{3,2,1,0:T(2,128)(2,1)S(1)}, bf16[2,64,2,128]{3,2,1,0:T(2,128)(2,1)S(1)}, u32[]{:S(2)}, u32[]{:S(2)}) collective-permute-start(bf16[2,64,2,128]{3,2,1,0:T(2,128)(2,1)S(1)} %get-tuple-element.9), channel_id=1, source_target_pairs={{8,0},{16,8},{24,16},{32,24},{40,32},{48,40},{56,48},{64,56},{72,6... | collective-permute-start | bytes 196616 | tf_op jit(solution)/shard_map/ppermute | solution.py:18
  11.0 4.7 %collective-permute-start.2 = (bf16[2,2,64,128]{3,2,1,0:T(8,128)(2,1)S(1)}, bf16[2,2,64,128]{3,2,1,0:T(8,128)(2,1)S(1)}, u32[]{:S(2)}, u32[]{:S(2)}) collective-permute-start(bf16[2,2,64,128]{3,2,1,0:T(8,128)(2,1)S(1)} %get-tuple-element.10), channel_id=1, source_target_pairs={{0,1},{1,2},{2,3},{3,4},{4,5},{5,6},{6,7},{7,0},{8,9},{9,10},{10,1... | collective-permute-start | bytes 196616 | tf_op jit(solution)/shard_map/ppermute | solution.py:16
  11.1 4.6 %collective-permute-start.3 = (bf16[2,2,64,128]{3,2,1,0:T(8,128)(2,1)S(1)}, bf16[2,2,64,128]{3,2,1,0:T(8,128)(2,1)S(1)}, u32[]{:S(2)}, u32[]{:S(2)}) collective-permute-start(bf16[2,2,64,128]{3,2,1,0:T(8,128)(2,1)S(1)} %get-tuple-element.11), channel_id=1, source_target_pairs={{1,0},{2,1},{3,2},{4,3},{5,4},{6,5},{7,6},{0,7},{9,8},{10,9},{11,1... | collective-permute-start | bytes 196616 | tf_op jit(solution)/shard_map/ppermute | solution.py:18
  18.8 6.9 %copy-start = (f32[2,64,64,128]{3,2,1,0:T(8,128)}, f32[2,64,64,128]{3,2,1,0:T(8,128)S(1)}, u32[]{:S(2)}) copy-start(f32[2,64,64,128]{3,2,1,0:T(8,128)S(1)} %fusion.2) | copy-start | bytes 12582916
  27.2 1.8 %collective-permute-start.4 = (f32[136,128]{0,1:T(8,128)S(1)}, f32[136,128]{0,1:T(8,128)S(1)}, u32[]{:S(2)}, u32[]{:S(2)}) collective-permute-start(f32[136,128]{0,1:T(8,128)S(1)} %maximum_maximum_fusion), channel_id=1, source_target_pairs={{0,1},{1,0},{2,3},{3,2},{4,5},{5,4},{6,7},{7,6},{8,9},{9,8},{10,11... | collective-permute-start | bytes 208904 | tf_op jit(solution)/shard_map/ppermute | solution.py:30
  29.0 5.9 %collective-permute-start.5 = (f32[136,128]{0,1:T(8,128)S(1)}, f32[136,128]{0,1:T(8,128)S(1)}, u32[]{:S(2)}, u32[]{:S(2)}) collective-permute-start(f32[136,128]{0,1:T(8,128)S(1)} %fusion.25), channel_id=1, source_target_pairs={{0,2},{1,3},{2,0},{3,1},{4,6},{5,7},{6,4},{7,5},{8,10},{9,11},{10,... | collective-permute-start | bytes 208904 | tf_op jit(solution)/shard_map/ppermute | solution.py:30
  34.9 6.7 %collective-permute-start.6 = (f32[136,128]{0,1:T(8,128)S(1)}, f32[136,128]{0,1:T(8,128)S(1)}, u32[]{:S(2)}, u32[]{:S(2)}) collective-permute-start(f32[136,128]{0,1:T(8,128)S(1)} %add.40), channel_id=1, source_target_pairs={{0,4},{1,5},{2,6},{3,7},{4,0},{5,1},{6,2},{7,3},{8,12},{9,13},{10,... | collective-permute-start | bytes 208904 | tf_op jit(solution)/shard_map/ppermute | solution.py:30
  41.7 5.1 %collective-permute-start.7 = (f32[136,128]{0,1:T(8,128)S(1)}, f32[136,128]{0,1:T(8,128)S(1)}, u32[]{:S(2)}, u32[]{:S(2)}) collective-permute-start(f32[136,128]{0,1:T(8,128)S(1)} %add.41), channel_id=1, source_target_pairs={{0,8},{8,0},{16,24},{24,16},{32,40},{40,32},{48,56},{56,48},{64,72... | collective-permute-start | bytes 208904 | tf_op jit(solution)/shard_map/ppermute | solution.py:30
  46.7 6.9 %collective-permute-start.8 = (f32[136,128]{0,1:T(8,128)S(1)}, f32[136,128]{0,1:T(8,128)S(1)}, u32[]{:S(2)}, u32[]{:S(2)}) collective-permute-start(f32[136,128]{0,1:T(8,128)S(1)} %add.42), channel_id=1, source_target_pairs={{0,16},{8,24},{16,0},{24,8},{32,48},{40,56},{48,32},{56,40},{64,80... | collective-permute-start | bytes 208904 | tf_op jit(solution)/shard_map/ppermute | solution.py:30
  53.6 10.0 %collective-permute-start.9 = (f32[136,128]{0,1:T(8,128)S(1)}, f32[136,128]{0,1:T(8,128)S(1)}, u32[]{:S(2)}, u32[]{:S(2)}) collective-permute-start(f32[136,128]{0,1:T(8,128)S(1)} %add.43), channel_id=1, source_target_pairs={{0,32},{8,40},{16,48},{24,56},{32,0},{40,8},{48,16},{56,24},{64,96... | collective-permute-start | bytes 208904 | tf_op jit(solution)/shard_map/ppermute | solution.py:30
  63.7 5.1 %collective-permute-start.10 = (f32[136,128]{0,1:T(8,128)S(1)}, f32[136,128]{0,1:T(8,128)S(1)}, u32[]{:S(2)}, u32[]{:S(2)}) collective-permute-start(f32[136,128]{0,1:T(8,128)S(1)} %add.44), channel_id=1, source_target_pairs={{0,64},{8,72},{16,80},{24,88},{32,96},{40,104},{48,112},{56,120},{... | collective-permute-start | bytes 208904 | tf_op jit(solution)/shard_map/ppermute | solution.py:30
  68.7 6.6 %collective-permute-start.11 = (f32[136,128]{0,1:T(8,128)S(1)}, f32[136,128]{0,1:T(8,128)S(1)}, u32[]{:S(2)}, u32[]{:S(2)}) collective-permute-start(f32[136,128]{0,1:T(8,128)S(1)} %add.45), channel_id=1, source_target_pairs={{0,128},{8,136},{16,144},{24,152},{32,160},{40,168},{48,176},{56,1... | collective-permute-start | bytes 208904 | tf_op jit(solution)/shard_map/ppermute | solution.py:30

commit v2 on v1

--- a/solution.py
+++ b/solution.py
@@ -1,6 +1,8 @@
 import jax
 import jax.numpy as jnp
 from jax import lax
+from jax.experimental import pallas as pl
+from jax.experimental.pallas import tpu as pltpu
 from jax.sharding import PartitionSpec as P
 
 span_step = 0.75
@@ -54,6 +56,43 @@
     return jnp.stack([first, second])
 
 
+def chol_inv_kernel(g_ref, rt_ref, x_ref, s_ref):
+    planes, n, _ = g_ref.shape
+    s_ref[...] = g_ref[...]
+    rr = lax.broadcasted_iota(jnp.int32, (n, n), 0)
+    cc = lax.broadcasted_iota(jnp.int32, (n, n), 1)
+    eye = jnp.where(rr == cc, 1.0, 0.0).astype(jnp.float32)
+    for p in range(planes):
+        x_ref[p] = eye
+    rt_ref[...] = jnp.zeros(rt_ref.shape, jnp.float32)
+    lane = lax.broadcasted_iota(jnp.int32, (1, n), 1)
+    for j in range(n):
+        lo = (j // 8) * 8
+        rows = lax.broadcasted_iota(jnp.int32, (n - lo, 1), 0) + lo
+        for p in range(planes):
+            rowj = s_ref[p, j:j + 1, :]
+            root = jnp.sqrt(rowj[:, j:j + 1])
+            inv = 1.0 / root
+            lrow = jnp.where(lane > j, rowj * inv, jnp.where(lane == j, root, 0.0))
+            rt_ref[p, j:j + 1, :] = lrow
+            blk = s_ref[p, lo:, :]
+            lcol = jnp.where(rows > j, blk[:, j:j + 1] * inv, 0.0)
+            s_ref[p, lo:, :] = blk - lcol * lrow
+            xrow = x_ref[p, j:j + 1, :] * inv
+            xblk = x_ref[p, lo:, :]
+            x_ref[p, lo:, :] = jnp.where(rows == j, xrow, xblk - lcol * xrow)
+
+def chol_inv(gram):
+    planes, n, _ = gram.shape
+    return pl.pallas_call(
+        chol_inv_kernel,
+        out_shape=(jax.ShapeDtypeStruct(gram.shape, jnp.float32),) * 2,
+        in_specs=[pl.BlockSpec(memory_space=pltpu.VMEM)],
+        out_specs=(pl.BlockSpec(memory_space=pltpu.VMEM),) * 2,
+        scratch_shapes=[pltpu.VMEM(gram.shape, jnp.float32)],
+    )(gram)
+
+
 def local(u_field, w_field):
     planes, rows_x, rows_z, snaps = u_field.shape
     padded_u = with_halo(u_field, (("gz", 2),), 2).astype(jnp.float32)
@@ -79,19 +118,15 @@
         gram_sum = butterfly_sum(gram_local, ("gx", "gz"))
     total_cells = rows_x * rows_z * lax.axis_size("gz") * lax.axis_size("gx")
     gram = gram_sum / total_cells
-    lower = jnp.linalg.cholesky(gram)
-    identity_matrix = jnp.broadcast_to(jnp.eye(snaps, dtype=gram.dtype), lower.shape)
-    lower_inverse = lax.linalg.triangular_solve(lower, identity_matrix, left_side=True, lower=True)
-    inverse_r = jnp.transpose(lower_inverse, (0, 2, 1))
+    factor_r, lower_inverse = chol_inv(gram)
     modes = jnp.einsum(
-        "pcs,pst->pct",
+        "pcs,pts->pct",
         columns,
-        inverse_r,
+        lower_inverse,
         precision=lax.Precision.HIGHEST,
         preferred_element_type=jnp.float32,
     )
     modes = modes.reshape(planes, rows_x, rows_z, snaps)
-    factor_r = jnp.transpose(lower, (0, 2, 1))
     return (modes, factor_r)
 
 

time: 127 us -> 90.5 us (0.71)
  other arithmetic: 49.5 us -> 6.9 us
  Pallas kernels: 0 us -> 14.2 us
  waiting for transfers between devices: 37.5 us -> 32.9 us
  starting transfers between devices: 20.2 us -> 18.3 us
  local copies, waits for them, and re-layouts: 4.93 us -> 3.61 us
    another operation x6 -> x0, other arithmetic: 43.3 us -> none  [the longest x4 23.6 us: local(): lower = jnp.linalg.cholesky(gram)]
    pallas_call x0 -> x1, Pallas kernels: none -> 14.2 us  [chol_inv(): pl.pallas_call(chol_inv_kernel, out_shape=(jax.ShapeDtypeStruct(gram.shap...]
    ppermute x8, waiting for transfers between devices: 37.4 us -> 32.9 us  [butterfly_sum(): x = x + lax.ppermute(x, axis, [(i, i ^ step) for i in range(count)])]
    ppermute x8, starting transfers between devices: 10.2 us -> 8.3 us  [butterfly_sum(): x = x + lax.ppermute(x, axis, [(i, i ^ step) for i in range(count)])]
  transfers between devices with their start and end apart: 12 -> 12, of which waited for: 8 -> 8; matrix products, arithmetic and copies ran while one was open for 3% -> 4% of each run, Pallas kernels for 0% -> 0%
where the time goes in v2:
time: 90.5 us; the launch traced here: 90.3 us
  waiting for transfers between devices  32.9 us (36%)
  starting transfers between devices  18.3 us (20%)
  Pallas kernels  14.2 us (16%)
  matrix products  13.6 us (15%)
  other arithmetic  6.9 us (8%)
  local copies, waits for them, and re-layouts  3.61 us (4%)
    ppermute x8, waiting for transfers between devices, butterfly_sum(): x = x + lax.ppermute(x, axis, [(i, i ^ step) for i in range(count)])  32.9 us
    pallas_call x1, Pallas kernels, chol_inv(): pl.pallas_call(chol_inv_kernel, out_shape=(jax.ShapeDtypeStruct(gram.shap...  14.2 us
    ppermute x8, starting transfers between devices, butterfly_sum(): x = x + lax.ppermute(x, axis, [(i, i ^ step) for i in range(count)])  8.3 us
    ppermute x2, starting transfers between devices, with_halo(): lax.ppermute(head, axis, [((i + 1) % count, i) for i in range(count)])  7.96 us
    dot_general x1, matrix products, local(): jnp.einsum('pcs,pct->pst', columns, columns, precision=lax.Precision.HIGH...  6.96 us
    dot_general x1, matrix products, local(): jnp.einsum('pcs,pts->pct', columns, lower_inverse, precision=lax.Precisio...  6.67 us
    convert_element_type x1, other arithmetic, local(): padded_u = with_halo(u_field, (('gz', 2),), 2).astype(jnp.float32)  2.78 us
    sub x1, other arithmetic, local(): vorticity = span_diff / (12.0 * span_step) - stream_diff / 12.0  2.77 us
  transfers between devices with their start and end apart: 12, of which 8 were waited for; matrix products, arithmetic and copies ran while one was open for 4% of the time, Pallas kernels for 0%

profile of v2, /device:TPU:8, one launch (start us, length us, event | category | flops | bytes accessed | tf_op | source)
XLA Modules:
  0.0 90.3 jit_solution(1926979491244097673)
XLA Ops:
  0.6 1.3 %fusion.12 = (bf16[2,64,2,128]{3,2,1,0:T(2,128)(2,1)S(1)}, bf16[2,64,2,128]{3,2,1,0:T(2,128)(2,1)S(1)}) fusion(bf16[2,64,64,128]{3,2,1,0:T(8,128)(2,1)} %param.2), kind=kLoop, calls=%fused_computation.31 | loop fusion | bytes 262144 | tf_op jit(solution)/shard_map/slice | solution.py:15
  1.9 2.0 %collective-permute-start = (bf16[2,64,2,128]{3,2,1,0:T(2,128)(2,1)S(1)}, bf16[2,64,2,128]{3,2,1,0:T(2,128)(2,1)S(1)}, u32[]{:S(2)}, u32[]{:S(2)}) collective-permute-start(bf16[2,64,2,128]{3,2,1,0:T(2,128)(2,1)S(1)} %get-tuple-element.6), channel_id=1, source_target_pairs={{0,8},{8,16},{16,24},{24,32},{32,40},{40,48},{48,56},{56,64},{64,7... | collective-permute-start | bytes 196616 | tf_op jit(solution)/shard_map/ppermute | solution.py:18
  3.9 6.2 %collective-permute-start.1 = (bf16[2,64,2,128]{3,2,1,0:T(2,128)(2,1)S(1)}, bf16[2,64,2,128]{3,2,1,0:T(2,128)(2,1)S(1)}, u32[]{:S(2)}, u32[]{:S(2)}) collective-permute-start(bf16[2,64,2,128]{3,2,1,0:T(2,128)(2,1)S(1)} %get-tuple-element.7), channel_id=1, source_target_pairs={{8,0},{16,8},{24,16},{32,24},{40,32},{48,40},{56,48},{64,56},{72,6... | collective-permute-start | bytes 196616 | tf_op jit(solution)/shard_map/ppermute | solution.py:20
  10.2 0.9 fusion.13
  11.1 1.7 %collective-permute-start.3 = (bf16[2,2,64,128]{3,2,1,0:T(8,128)(2,1)S(1)}, bf16[2,2,64,128]{3,2,1,0:T(8,128)(2,1)S(1)}, u32[]{:S(2)}, u32[]{:S(2)}) collective-permute-start(bf16[2,2,64,128]{3,2,1,0:T(8,128)(2,1)S(1)} %get-tuple-element.9), channel_id=1, source_target_pairs={{1,0},{2,1},{3,2},{4,3},{5,4},{6,5},{7,6},{0,7},{9,8},{10,9},{11,1... | collective-permute-start | bytes 196616 | tf_op jit(solution)/shard_map/ppermute | solution.py:20
  12.9 2.8 %maximum_convert_fusion = f32[2,64,68,128]{3,2,1,0:T(8,128)S(1)} fusion(bf16[2,64,2,128]{3,2,1,0:T(2,128)(2,1)S(1)} %collective-permute-done.1, bf16[2,64,64,128]{3,2,1,0:T(8,128)(2,1)} %param.2, bf16[2,64,2,128]{3,2,1,0:T(2,128)(2,1)S(1)} %collective-permute-done), kind=kLoop, calls=%fused_computation.12 | loop fusion | flops 6684672 | bytes 6684672 | tf_op jit(solution)/shard_map/convert_element_type | solution.py:98
  15.7 0.3 maximum_convert_fusion.1
  16.1 2.8 %fusion.2 = f32[2,64,64,128]{3,2,1,0:T(8,128)S(1)} fusion(f32[2,68,64,128]{3,2,1,0:T(8,128)S(1)} %maximum_convert_fusion.1, f32[2,64,68,128]{3,2,1,0:T(8,128)S(1)} %maximum_convert_fusion), kind=kLoop, calls=%fused_computation.4 | loop fusion | flops 11534336 | bytes 37748736 | tf_op jit(solution)/shard_map/sub | solution.py:106
  18.9 7.0 %fusion.14 = f32[2,128,128]{2,1,0:T(8,128)S(1)} fusion(f32[2,4096,128]{2,1,0:T(8,128)S(1)} %bitcast.32), kind=kOutput, calls=%fused_computation.33 | convolution fusion | flops 1610612736 | bytes 4325376 | tf_op jit(solution)/shard_map/pcs,pct->pst/dot_general | solution.py:108
  25.9 1.2 %gather_fusion = f32[128]{0:T(128)S(1)} fusion(f32[128,128]{1,0:T(8,128)S(1)} %slice_bitcast_fusion, s32[128]{0:T(128)S(1)} %or_bitcast_fusion), kind=kCustom, calls=%fused_computation | custom fusion | bytes 2048 | tf_op jit(solution)/shard_map/jit(diagonal)/cond/branch_0_fun/gather | solution.py:42
  27.2 0.8 collective-permute-start.4
  28.0 0.9 %collective-permute-done.4 = f32[136,128]{1,0:T(8,128)S(1)} collective-permute-done((f32[136,128]{1,0:T(8,128)S(1)}, f32[136,128]{1,0:T(8,128)S(1)}, u32[]{:S(2)}, u32[]{:S(2)}) %collective-permute-start.4) | collective-permute-done | bytes 69664 | tf_op jit(solution)/shard_map/ppermute | solution.py:32
  28.9 0.1 fusion.11
  29.0 1.4 %collective-permute-start.5 = (f32[136,128]{1,0:T(8,128)S(1)}, f32[136,128]{1,0:T(8,128)S(1)}, u32[]{:S(2)}, u32[]{:S(2)}) collective-permute-start(f32[136,128]{1,0:T(8,128)S(1)} %fusion.11), channel_id=1, source_target_pairs={{0,2},{1,3},{2,0},{3,1},{4,6},{5,7},{6,4},{7,5},{8,10},{9,11},{10,... | collective-permute-start | bytes 208904 | tf_op jit(solution)/shard_map/ppermute | solution.py:32
  30.4 3.1 %collective-permute-done.5 = f32[136,128]{1,0:T(8,128)S(1)} collective-permute-done((f32[136,128]{1,0:T(8,128)S(1)}, f32[136,128]{1,0:T(8,128)S(1)}, u32[]{:S(2)}, u32[]{:S(2)}) %collective-permute-start.5) | collective-permute-done | bytes 69664 | tf_op jit(solution)/shard_map/ppermute | solution.py:32
  33.5 2.4 %collective-permute-start.6 = (f32[136,128]{1,0:T(8,128)S(1)}, f32[136,128]{1,0:T(8,128)S(1)}, u32[]{:S(2)}, u32[]{:S(2)}) collective-permute-start(f32[136,128]{1,0:T(8,128)S(1)} %add.29), channel_id=1, source_target_pairs={{0,4},{1,5},{2,6},{3,7},{4,0},{5,1},{6,2},{7,3},{8,12},{9,13},{10,... | collective-permute-start | bytes 208904 | tf_op jit(solution)/shard_map/ppermute | solution.py:32
  36.0 3.7 %collective-permute-done.6 = f32[136,128]{1,0:T(8,128)S(1)} collective-permute-done((f32[136,128]{1,0:T(8,128)S(1)}, f32[136,128]{1,0:T(8,128)S(1)}, u32[]{:S(2)}, u32[]{:S(2)}) %collective-permute-start.6) | collective-permute-done | bytes 69664 | tf_op jit(solution)/shard_map/ppermute | solution.py:32
  39.6 0.1 collective-permute-start.7
  39.7 4.3 %collective-permute-done.7 = f32[136,128]{1,0:T(8,128)S(1)} collective-permute-done((f32[136,128]{1,0:T(8,128)S(1)}, f32[136,128]{1,0:T(8,128)S(1)}, u32[]{:S(2)}, u32[]{:S(2)}) %collective-permute-start.7) | collective-permute-done | bytes 69664 | tf_op jit(solution)/shard_map/ppermute | solution.py:32
  44.0 0.5 collective-permute-start.8
  44.5 5.1 %collective-permute-done.8 = f32[136,128]{1,0:T(8,128)S(1)} collective-permute-done((f32[136,128]{1,0:T(8,128)S(1)}, f32[136,128]{1,0:T(8,128)S(1)}, u32[]{:S(2)}, u32[]{:S(2)}) %collective-permute-start.8) | collective-permute-done | bytes 69664 | tf_op jit(solution)/shard_map/ppermute | solution.py:32
  49.6 2.3 %collective-permute-start.9 = (f32[136,128]{1,0:T(8,128)S(1)}, f32[136,128]{1,0:T(8,128)S(1)}, u32[]{:S(2)}, u32[]{:S(2)}) collective-permute-start(f32[136,128]{1,0:T(8,128)S(1)} %add.32), channel_id=1, source_target_pairs={{0,32},{8,40},{16,48},{24,56},{32,0},{40,8},{48,16},{56,24},{64,96... | collective-permute-start | bytes 208904 | tf_op jit(solution)/shard_map/ppermute | solution.py:32
  51.9 6.3 %collective-permute-done.9 = f32[136,128]{1,0:T(8,128)S(1)} collective-permute-done((f32[136,128]{1,0:T(8,128)S(1)}, f32[136,128]{1,0:T(8,128)S(1)}, u32[]{:S(2)}, u32[]{:S(2)}) %collective-permute-start.9) | collective-permute-done | bytes 69664 | tf_op jit(solution)/shard_map/ppermute | solution.py:32
  58.2 0.1 collective-permute-start.10
  58.3 4.3 %collective-permute-done.10 = f32[136,128]{1,0:T(8,128)S(1)} collective-permute-done((f32[136,128]{1,0:T(8,128)S(1)}, f32[136,128]{1,0:T(8,128)S(1)}, u32[]{:S(2)}, u32[]{:S(2)}) %collective-permute-start.10) | collective-permute-done | bytes 69664 | tf_op jit(solution)/shard_map/ppermute | solution.py:32
  62.7 0.8 collective-permute-start.11
  63.4 5.1 %collective-permute-done.11 = f32[136,128]{1,0:T(8,128)S(1)} collective-permute-done((f32[136,128]{1,0:T(8,128)S(1)}, f32[136,128]{1,0:T(8,128)S(1)}, u32[]{:S(2)}, u32[]{:S(2)}) %collective-permute-start.11) | collective-permute-done | bytes 69664 | tf_op jit(solution)/shard_map/ppermute | solution.py:32
  68.6 0.1 copy.7
  68.7 0.1 fusion.8
  68.8 0.7 maximum_multiply_fusion.g_ref
  69.5 14.2 %shard_map.41 = (f32[2,128,128]{2,1,0:T(8,128)}, f32[2,128,128]{2,1,0:T(8,128)}) custom-call(f32[2,128,128]{2,1,0:T(8,128)} %maximum_multiply_fusion.g_ref), custom_call_target="tpu_custom_call" | custom-call | tf_op jit(solution)/shard_map/pallas_call | solution.py:87
  83.6 6.7 %fusion.15 = f32[2,4096,128]{2,1,0:T(8,128)} fusion(f32[2,4096,128]{2,1,0:T(8,128)} %bitcast.33, f32[2,128,128]{2,1,0:T(8,128)} %get-tuple-element.4), kind=kOutput, calls=%fused_computation.34 | convolution fusion | flops 1610612736 | bytes 8519680 | tf_op jit(solution)/shard_map/pcs,pts->pct/dot_general | solution.py:122
  (24 shorter events, 0.3 us)
Async XLA Ops:
  0.6 15.1 %copy-start.1 = (bf16[2,64,64,128]{3,2,1,0:T(8,128)(2,1)S(1)}, bf16[2,64,64,128]{3,2,1,0:T(8,128)(2,1)}, u32[]{:S(2)}) copy-start(bf16[2,64,64,128]{3,2,1,0:T(8,128)(2,1)} %param.3) | copy-start | bytes 6291460
  1.9 11.0 %collective-permute-start = (bf16[2,64,2,128]{3,2,1,0:T(2,128)(2,1)S(1)}, bf16[2,64,2,128]{3,2,1,0:T(2,128)(2,1)S(1)}, u32[]{:S(2)}, u32[]{:S(2)}) collective-permute-start(bf16[2,64,2,128]{3,2,1,0:T(2,128)(2,1)S(1)} %get-tuple-element.6), channel_id=1, source_target_pairs={{0,8},{8,16},{16,24},{24,32},{32,40},{40,48},{48,56},{56,64},{64,7... | collective-permute-start | bytes 196616 | tf_op jit(solution)/shard_map/ppermute | solution.py:18
  3.9 9.0 %collective-permute-start.1 = (bf16[2,64,2,128]{3,2,1,0:T(2,128)(2,1)S(1)}, bf16[2,64,2,128]{3,2,1,0:T(2,128)(2,1)S(1)}, u32[]{:S(2)}, u32[]{:S(2)}) collective-permute-start(bf16[2,64,2,128]{3,2,1,0:T(2,128)(2,1)S(1)} %get-tuple-element.7), channel_id=1, source_target_pairs={{8,0},{16,8},{24,16},{32,24},{40,32},{48,40},{56,48},{64,56},{72,6... | collective-permute-start | bytes 196616 | tf_op jit(solution)/shard_map/ppermute | solution.py:20
  11.0 4.7 %collective-permute-start.2 = (bf16[2,2,64,128]{3,2,1,0:T(8,128)(2,1)S(1)}, bf16[2,2,64,128]{3,2,1,0:T(8,128)(2,1)S(1)}, u32[]{:S(2)}, u32[]{:S(2)}) collective-permute-start(bf16[2,2,64,128]{3,2,1,0:T(8,128)(2,1)S(1)} %get-tuple-element.8), channel_id=1, source_target_pairs={{0,1},{1,2},{2,3},{3,4},{4,5},{5,6},{6,7},{7,0},{8,9},{9,10},{10,1... | collective-permute-start | bytes 196616 | tf_op jit(solution)/shard_map/ppermute | solution.py:18
  11.1 4.6 %collective-permute-start.3 = (bf16[2,2,64,128]{3,2,1,0:T(8,128)(2,1)S(1)}, bf16[2,2,64,128]{3,2,1,0:T(8,128)(2,1)S(1)}, u32[]{:S(2)}, u32[]{:S(2)}) collective-permute-start(bf16[2,2,64,128]{3,2,1,0:T(8,128)(2,1)S(1)} %get-tuple-element.9), channel_id=1, source_target_pairs={{1,0},{2,1},{3,2},{4,3},{5,4},{6,5},{7,6},{0,7},{9,8},{10,9},{11,1... | collective-permute-start | bytes 196616 | tf_op jit(solution)/shard_map/ppermute | solution.py:20
  18.8 7.0 %copy-start = (f32[2,64,64,128]{3,2,1,0:T(8,128)}, f32[2,64,64,128]{3,2,1,0:T(8,128)S(1)}, u32[]{:S(2)}) copy-start(f32[2,64,64,128]{3,2,1,0:T(8,128)S(1)} %fusion.2) | copy-start | bytes 12582916
  27.2 1.7 %collective-permute-start.4 = (f32[136,128]{1,0:T(8,128)S(1)}, f32[136,128]{1,0:T(8,128)S(1)}, u32[]{:S(2)}, u32[]{:S(2)}) collective-permute-start(f32[136,128]{1,0:T(8,128)S(1)} %maximum_maximum_fusion), channel_id=1, source_target_pairs={{0,1},{1,0},{2,3},{3,2},{4,5},{5,4},{6,7},{7,6},{8,9},{9,8},{10,11... | collective-permute-start | bytes 208904 | tf_op jit(solution)/shard_map/ppermute | solution.py:32
  29.0 4.5 %collective-permute-start.5 = (f32[136,128]{1,0:T(8,128)S(1)}, f32[136,128]{1,0:T(8,128)S(1)}, u32[]{:S(2)}, u32[]{:S(2)}) collective-permute-start(f32[136,128]{1,0:T(8,128)S(1)} %fusion.11), channel_id=1, source_target_pairs={{0,2},{1,3},{2,0},{3,1},{4,6},{5,7},{6,4},{7,5},{8,10},{9,11},{10,... | collective-permute-start | bytes 208904 | tf_op jit(solution)/shard_map/ppermute | solution.py:32
  33.5 6.1 %collective-permute-start.6 = (f32[136,128]{1,0:T(8,128)S(1)}, f32[136,128]{1,0:T(8,128)S(1)}, u32[]{:S(2)}, u32[]{:S(2)}) collective-permute-start(f32[136,128]{1,0:T(8,128)S(1)} %add.29), channel_id=1, source_target_pairs={{0,4},{1,5},{2,6},{3,7},{4,0},{5,1},{6,2},{7,3},{8,12},{9,13},{10,... | collective-permute-start | bytes 208904 | tf_op jit(solution)/shard_map/ppermute | solution.py:32
  39.6 4.4 %collective-permute-start.7 = (f32[136,128]{1,0:T(8,128)S(1)}, f32[136,128]{1,0:T(8,128)S(1)}, u32[]{:S(2)}, u32[]{:S(2)}) collective-permute-start(f32[136,128]{1,0:T(8,128)S(1)} %add.30), channel_id=1, source_target_pairs={{0,8},{8,0},{16,24},{24,16},{32,40},{40,32},{48,56},{56,48},{64,72... | collective-permute-start | bytes 208904 | tf_op jit(solution)/shard_map/ppermute | solution.py:32
  44.0 5.6 %collective-permute-start.8 = (f32[136,128]{1,0:T(8,128)S(1)}, f32[136,128]{1,0:T(8,128)S(1)}, u32[]{:S(2)}, u32[]{:S(2)}) collective-permute-start(f32[136,128]{1,0:T(8,128)S(1)} %add.31), channel_id=1, source_target_pairs={{0,16},{8,24},{16,0},{24,8},{32,48},{40,56},{48,32},{56,40},{64,80... | collective-permute-start | bytes 208904 | tf_op jit(solution)/shard_map/ppermute | solution.py:32
  49.6 8.6 %collective-permute-start.9 = (f32[136,128]{1,0:T(8,128)S(1)}, f32[136,128]{1,0:T(8,128)S(1)}, u32[]{:S(2)}, u32[]{:S(2)}) collective-permute-start(f32[136,128]{1,0:T(8,128)S(1)} %add.32), channel_id=1, source_target_pairs={{0,32},{8,40},{16,48},{24,56},{32,0},{40,8},{48,16},{56,24},{64,96... | collective-permute-start | bytes 208904 | tf_op jit(solution)/shard_map/ppermute | solution.py:32
  58.2 4.4 %collective-permute-start.10 = (f32[136,128]{1,0:T(8,128)S(1)}, f32[136,128]{1,0:T(8,128)S(1)}, u32[]{:S(2)}, u32[]{:S(2)}) collective-permute-start(f32[136,128]{1,0:T(8,128)S(1)} %add.33), channel_id=1, source_target_pairs={{0,64},{8,72},{16,80},{24,88},{32,96},{40,104},{48,112},{56,120},{... | collective-permute-start | bytes 208904 | tf_op jit(solution)/shard_map/ppermute | solution.py:32
  62.7 5.9 %collective-permute-start.11 = (f32[136,128]{1,0:T(8,128)S(1)}, f32[136,128]{1,0:T(8,128)S(1)}, u32[]{:S(2)}, u32[]{:S(2)}) collective-permute-start(f32[136,128]{1,0:T(8,128)S(1)} %add.34), channel_id=1, source_target_pairs={{0,128},{8,136},{16,144},{24,152},{32,160},{40,168},{48,176},{56,1... | collective-permute-start | bytes 208904 | tf_op jit(solution)/shard_map/ppermute | solution.py:32

commit v3 on v2

--- a/solution.py
+++ b/solution.py
@@ -34,12 +34,24 @@
     return x
 
 
+def split_gram(columns):
+    head32 = lax.reduce_precision(columns, exponent_bits=8, mantissa_bits=7)
+    head = head32.astype(jnp.bfloat16)
+    tail = (columns - head32).astype(jnp.bfloat16)
+
+    def dot(a, b):
+        return jnp.einsum("pcs,pct->pst", a, b, preferred_element_type=jnp.float32)
+
+    cross = dot(head, tail)
+    return dot(head, head) + (cross + jnp.swapaxes(cross, 1, 2)) + dot(tail, tail)
+
+
 def pack_pair(gram):
     n = gram.shape[-1]
     row = lax.broadcasted_iota(jnp.int32, (n, n), 0)
     col = lax.broadcasted_iota(jnp.int32, (n, n), 1)
     square = jnp.where(row <= col, gram[0], gram[1])
-    diag = jnp.diagonal(gram[1])[None, :]
+    diag = jnp.sum(jnp.where(row == col, gram[1], 0.0), axis=0, keepdims=True)
     pad = jnp.zeros((7, n), gram.dtype)
     return jnp.concatenate([square, diag, pad], axis=0)
 
@@ -105,13 +117,7 @@
     )
     vorticity = span_diff / (12.0 * span_step) - stream_diff / 12.0
     columns = vorticity.reshape(planes, rows_x * rows_z, snaps)
-    gram_local = jnp.einsum(
-        "pcs,pct->pst",
-        columns,
-        columns,
-        precision=lax.Precision.HIGHEST,
-        preferred_element_type=jnp.float32,
-    )
+    gram_local = split_gram(columns)
     if planes == 2:
         gram_sum = unpack_pair(butterfly_sum(pack_pair(gram_local), ("gx", "gz")))
     else:
@@ -123,7 +129,7 @@
         "pcs,pts->pct",
         columns,
         lower_inverse,
-        precision=lax.Precision.HIGHEST,
+        precision=lax.Precision.HIGH,
         preferred_element_type=jnp.float32,
     )
     modes = modes.reshape(planes, rows_x, rows_z, snaps)

time: 90.5 us -> 90.6 us (level)
  local copies, waits for them, and re-layouts: 3.61 us -> 4.57 us
    unnamed x4 -> x6, local copies, waits for them, and re-layouts: 0.01 us -> 2.12 us
    gather x1 -> x0, local copies, waits for them, and re-layouts: 1.25 us -> none  [pack_pair(): diag = jnp.diagonal(gram[1])[None, :]]
    dot_general x1 -> x3, matrix products: 6.96 us -> 6.73 us  [dot(): return jnp.einsum('pcs,pct->pst', a, b, preferred_element_type=jnp.float32)]
where the time goes in v3:
time: 90.6 us; the launch traced here: 90.4 us
  waiting for transfers between devices  32.7 us (36%)
  starting transfers between devices  18.5 us (20%)
  Pallas kernels  14.2 us (16%)
  matrix products  12.7 us (14%)
  other arithmetic  6.91 us (8%)
  local copies, waits for them, and re-layouts  4.57 us (5%)
    ppermute x8, waiting for transfers between devices, butterfly_sum(): x = x + lax.ppermute(x, axis, [(i, i ^ step) for i in range(count)])  32.7 us
    pallas_call x1, Pallas kernels, chol_inv(): pl.pallas_call(chol_inv_kernel, out_shape=(jax.ShapeDtypeStruct(gram.shap...  14.2 us
    ppermute x8, starting transfers between devices, butterfly_sum(): x = x + lax.ppermute(x, axis, [(i, i ^ step) for i in range(count)])  8.49 us
    ppermute x2, starting transfers between devices, with_halo(): lax.ppermute(head, axis, [((i + 1) % count, i) for i in range(count)])  7.96 us
    dot_general x3, matrix products, dot(): return jnp.einsum('pcs,pct->pst', a, b, preferred_element_type=jnp.float32)  6.73 us
    dot_general x1, matrix products, local(): jnp.einsum('pcs,pts->pct', columns, lower_inverse, precision=lax.Precisio...  6.01 us
    convert_element_type x1, other arithmetic, local(): padded_u = with_halo(u_field, (('gz', 2),), 2).astype(jnp.float32)  2.78 us
    sub x1, other arithmetic, local(): vorticity = span_diff / (12.0 * span_step) - stream_diff / 12.0  2.77 us
  transfers between devices with their start and end apart: 12, of which 8 were waited for; matrix products, arithmetic and copies ran while one was open for 4% of the time, Pallas kernels for 0%

profile of v3, /device:TPU:8, one launch (start us, length us, event | category | flops | bytes accessed | tf_op | source)
XLA Modules:
  0.0 90.4 jit_solution(5799062423706212824)
XLA Ops:
  0.6 1.3 %fusion.16 = (bf16[2,64,2,128]{3,2,1,0:T(2,128)(2,1)S(1)}, bf16[2,64,2,128]{3,2,1,0:T(2,128)(2,1)S(1)}) fusion(bf16[2,64,64,128]{3,2,1,0:T(8,128)(2,1)} %param.2), kind=kLoop, calls=%fused_computation.37 | loop fusion | bytes 262144 | tf_op jit(solution)/shard_map/slice | solution.py:15
  1.9 2.0 %collective-permute-start = (bf16[2,64,2,128]{3,2,1,0:T(2,128)(2,1)S(1)}, bf16[2,64,2,128]{3,2,1,0:T(2,128)(2,1)S(1)}, u32[]{:S(2)}, u32[]{:S(2)}) collective-permute-start(bf16[2,64,2,128]{3,2,1,0:T(2,128)(2,1)S(1)} %get-tuple-element.6), channel_id=1, source_target_pairs={{0,8},{8,16},{16,24},{24,32},{32,40},{40,48},{48,56},{56,64},{64,7... | collective-permute-start | bytes 196616 | tf_op jit(solution)/shard_map/ppermute | solution.py:18
  3.9 6.2 %collective-permute-start.1 = (bf16[2,64,2,128]{3,2,1,0:T(2,128)(2,1)S(1)}, bf16[2,64,2,128]{3,2,1,0:T(2,128)(2,1)S(1)}, u32[]{:S(2)}, u32[]{:S(2)}) collective-permute-start(bf16[2,64,2,128]{3,2,1,0:T(2,128)(2,1)S(1)} %get-tuple-element.7), channel_id=1, source_target_pairs={{8,0},{16,8},{24,16},{32,24},{40,32},{48,40},{56,48},{64,56},{72,6... | collective-permute-start | bytes 196616 | tf_op jit(solution)/shard_map/ppermute | solution.py:20
  10.2 0.9 fusion.17
  11.1 1.7 %collective-permute-start.3 = (bf16[2,2,64,128]{3,2,1,0:T(8,128)(2,1)S(1)}, bf16[2,2,64,128]{3,2,1,0:T(8,128)(2,1)S(1)}, u32[]{:S(2)}, u32[]{:S(2)}) collective-permute-start(bf16[2,2,64,128]{3,2,1,0:T(8,128)(2,1)S(1)} %get-tuple-element.9), channel_id=1, source_target_pairs={{1,0},{2,1},{3,2},{4,3},{5,4},{6,5},{7,6},{0,7},{9,8},{10,9},{11,1... | collective-permute-start | bytes 196616 | tf_op jit(solution)/shard_map/ppermute | solution.py:20
  12.9 2.8 %maximum_convert_fusion = f32[2,64,68,128]{3,2,1,0:T(8,128)S(1)} fusion(bf16[2,64,2,128]{3,2,1,0:T(2,128)(2,1)S(1)} %collective-permute-done.1, bf16[2,64,64,128]{3,2,1,0:T(8,128)(2,1)} %param.2, bf16[2,64,2,128]{3,2,1,0:T(2,128)(2,1)S(1)} %collective-permute-done), kind=kLoop, calls=%fused_computation.14 | loop fusion | flops 6684672 | bytes 6684672 | tf_op jit(solution)/shard_map/convert_element_type | solution.py:110
  15.7 0.3 maximum_convert_fusion.1
  16.0 2.8 %fusion.3 = f32[2,64,64,128]{3,2,1,0:T(8,128)S(1)} fusion(f32[2,68,64,128]{3,2,1,0:T(8,128)S(1)} %maximum_convert_fusion.1, f32[2,64,68,128]{3,2,1,0:T(8,128)S(1)} %maximum_convert_fusion), kind=kLoop, calls=%fused_computation.6 | loop fusion | flops 11534336 | bytes 37748736 | tf_op jit(solution)/shard_map/sub | solution.py:118
  18.8 2.0 %copy-done = f32[2,64,64,128]{3,2,1,0:T(8,128)} copy-done((f32[2,64,64,128]{3,2,1,0:T(8,128)}, f32[2,64,64,128]{3,2,1,0:T(8,128)S(1)}, u32[]{:S(2)}) %copy-start) | copy-done | bytes 4194328
  20.8 1.1 %fusion.8 = f32[2,128,128]{2,1,0:T(8,128)S(1)} fusion(f32[2,4096,128]{2,1,0:T(8,128)S(1)} %bitcast.34), kind=kOutput, calls=%fused_computation.18 | convolution fusion | flops 273678336 | bytes 4325376 | tf_op jit(solution)/shard_map/pcs,pct->pst/dot_general | solution.py:43
  21.9 0.1 copy.6
  22.0 4.5 %convolution_add_fusion.1 = f32[2,128,128]{2,1,0:T(8,128)S(1)} fusion(f32[2,4096,128]{2,1,0:T(8,128)} %bitcast.35, f32[2,128,128]{2,1,0:T(8,128)S(1)} %fusion.8, f32[2,128,128]{1,2,0:T(8,128)S(1)} %copy.6), kind=kOutput, calls=%fused_computation.17 | convolution fusion | flops 270598144 | bytes 4587520 | tf_op jit(solution)/shard_map/pcs,pct->pst/dot_general | solution.py:43
  26.5 0.2 copy-done.1
  26.6 1.2 %convolution_add_fusion = f32[2,128,128]{2,1,0:T(8,128)S(1)} fusion(f32[2,128,128]{2,1,0:T(8,128)S(1)} %convolution_add_fusion.1, f32[2,4096,128]{2,1,0:T(8,128)S(1)} %bitcast.37), kind=kOutput, calls=%fused_computation.16 | convolution fusion | flops 271613952 | bytes 4456448 | tf_op jit(solution)/shard_map/pcs,pct->pst/dot_general | solution.py:43
  27.9 0.8 collective-permute-start.4
  28.7 0.9 %collective-permute-done.4 = f32[136,128]{1,0:T(8,128)S(1)} collective-permute-done((f32[136,128]{1,0:T(8,128)S(1)}, f32[136,128]{1,0:T(8,128)S(1)}, u32[]{:S(2)}, u32[]{:S(2)}) %collective-permute-start.4) | collective-permute-done | bytes 69664 | tf_op jit(solution)/shard_map/ppermute | solution.py:32
  29.7 1.4 %collective-permute-start.5 = (f32[136,128]{1,0:T(8,128)S(1)}, f32[136,128]{1,0:T(8,128)S(1)}, u32[]{:S(2)}, u32[]{:S(2)}) collective-permute-start(f32[136,128]{1,0:T(8,128)S(1)} %fusion.15), channel_id=1, source_target_pairs={{0,2},{1,3},{2,0},{3,1},{4,6},{5,7},{6,4},{7,5},{8,10},{9,11},{10,... | collective-permute-start | bytes 208904 | tf_op jit(solution)/shard_map/ppermute | solution.py:32
  31.1 3.2 %collective-permute-done.5 = f32[136,128]{1,0:T(8,128)S(1)} collective-permute-done((f32[136,128]{1,0:T(8,128)S(1)}, f32[136,128]{1,0:T(8,128)S(1)}, u32[]{:S(2)}, u32[]{:S(2)}) %collective-permute-start.5) | collective-permute-done | bytes 69664 | tf_op jit(solution)/shard_map/ppermute | solution.py:32
  34.3 2.2 %collective-permute-start.6 = (f32[136,128]{1,0:T(8,128)S(1)}, f32[136,128]{1,0:T(8,128)S(1)}, u32[]{:S(2)}, u32[]{:S(2)}) collective-permute-start(f32[136,128]{1,0:T(8,128)S(1)} %add.37), channel_id=1, source_target_pairs={{0,4},{1,5},{2,6},{3,7},{4,0},{5,1},{6,2},{7,3},{8,12},{9,13},{10,... | collective-permute-start | bytes 208904 | tf_op jit(solution)/shard_map/ppermute | solution.py:32
  36.5 3.7 %collective-permute-done.6 = f32[136,128]{1,0:T(8,128)S(1)} collective-permute-done((f32[136,128]{1,0:T(8,128)S(1)}, f32[136,128]{1,0:T(8,128)S(1)}, u32[]{:S(2)}, u32[]{:S(2)}) %collective-permute-start.6) | collective-permute-done | bytes 69664 | tf_op jit(solution)/shard_map/ppermute | solution.py:32
  40.2 0.1 collective-permute-start.7
  40.3 4.3 %collective-permute-done.7 = f32[136,128]{1,0:T(8,128)S(1)} collective-permute-done((f32[136,128]{1,0:T(8,128)S(1)}, f32[136,128]{1,0:T(8,128)S(1)}, u32[]{:S(2)}, u32[]{:S(2)}) %collective-permute-start.7) | collective-permute-done | bytes 69664 | tf_op jit(solution)/shard_map/ppermute | solution.py:32
  44.6 0.5 collective-permute-start.8
  45.1 5.1 %collective-permute-done.8 = f32[136,128]{1,0:T(8,128)S(1)} collective-permute-done((f32[136,128]{1,0:T(8,128)S(1)}, f32[136,128]{1,0:T(8,128)S(1)}, u32[]{:S(2)}, u32[]{:S(2)}) %collective-permute-start.8) | collective-permute-done | bytes 69664 | tf_op jit(solution)/shard_map/ppermute | solution.py:32
  50.2 2.3 %collective-permute-start.9 = (f32[136,128]{1,0:T(8,128)S(1)}, f32[136,128]{1,0:T(8,128)S(1)}, u32[]{:S(2)}, u32[]{:S(2)}) collective-permute-start(f32[136,128]{1,0:T(8,128)S(1)} %add.40), channel_id=1, source_target_pairs={{0,32},{8,40},{16,48},{24,56},{32,0},{40,8},{48,16},{56,24},{64,96... | collective-permute-start | bytes 208904 | tf_op jit(solution)/shard_map/ppermute | solution.py:32
  52.5 6.3 %collective-permute-done.9 = f32[136,128]{1,0:T(8,128)S(1)} collective-permute-done((f32[136,128]{1,0:T(8,128)S(1)}, f32[136,128]{1,0:T(8,128)S(1)}, u32[]{:S(2)}, u32[]{:S(2)}) %collective-permute-start.9) | collective-permute-done | bytes 69664 | tf_op jit(solution)/shard_map/ppermute | solution.py:32
  58.9 4.3 %collective-permute-done.10 = f32[136,128]{1,0:T(8,128)S(1)} collective-permute-done((f32[136,128]{1,0:T(8,128)S(1)}, f32[136,128]{1,0:T(8,128)S(1)}, u32[]{:S(2)}, u32[]{:S(2)}) %collective-permute-start.10) | collective-permute-done | bytes 69664 | tf_op jit(solution)/shard_map/ppermute | solution.py:32
  63.2 1.1 %collective-permute-start.11 = (f32[136,128]{1,0:T(8,128)S(1)}, f32[136,128]{1,0:T(8,128)S(1)}, u32[]{:S(2)}, u32[]{:S(2)}) collective-permute-start(f32[136,128]{1,0:T(8,128)S(1)} %add.42), channel_id=1, source_target_pairs={{0,128},{8,136},{16,144},{24,152},{32,160},{40,168},{48,176},{56,1... | collective-permute-start | bytes 208904 | tf_op jit(solution)/shard_map/ppermute | solution.py:32
  64.3 5.0 %collective-permute-done.11 = f32[136,128]{1,0:T(8,128)S(1)} collective-permute-done((f32[136,128]{1,0:T(8,128)S(1)}, f32[136,128]{1,0:T(8,128)S(1)}, u32[]{:S(2)}, u32[]{:S(2)}) %collective-permute-start.11) | collective-permute-done | bytes 69664 | tf_op jit(solution)/shard_map/ppermute | solution.py:32
  69.5 0.7 maximum_multiply_fusion.g_ref
  70.2 14.2 %shard_map.41 = (f32[2,128,128]{2,1,0:T(8,128)}, f32[2,128,128]{2,1,0:T(8,128)}) custom-call(f32[2,128,128]{2,1,0:T(8,128)} %maximum_multiply_fusion.g_ref), custom_call_target="tpu_custom_call" | custom-call | tf_op jit(solution)/shard_map/pallas_call | solution.py:99
  84.4 6.0 %fusion.18 = f32[2,4096,128]{2,1,0:T(8,128)} fusion(f32[2,4096,128]{2,1,0:T(8,128)} %bitcast.36, f32[2,128,128]{2,1,0:T(8,128)} %get-tuple-element.4), kind=kOutput, calls=%fused_computation.39 | convolution fusion | flops 805306368 | bytes 8519680 | tf_op jit(solution)/shard_map/pcs,pts->pct/dot_general | solution.py:128
  (26 shorter events, 0.7 us)
Async XLA Ops:
  0.6 15.1 %copy-start.2 = (bf16[2,64,64,128]{3,2,1,0:T(8,128)(2,1)S(1)}, bf16[2,64,64,128]{3,2,1,0:T(8,128)(2,1)}, u32[]{:S(2)}) copy-start(bf16[2,64,64,128]{3,2,1,0:T(8,128)(2,1)} %param.3) | copy-start | bytes 6291460
  1.9 10.9 %collective-permute-start = (bf16[2,64,2,128]{3,2,1,0:T(2,128)(2,1)S(1)}, bf16[2,64,2,128]{3,2,1,0:T(2,128)(2,1)S(1)}, u32[]{:S(2)}, u32[]{:S(2)}) collective-permute-start(bf16[2,64,2,128]{3,2,1,0:T(2,128)(2,1)S(1)} %get-tuple-element.6), channel_id=1, source_target_pairs={{0,8},{8,16},{16,24},{24,32},{32,40},{40,48},{48,56},{56,64},{64,7... | collective-permute-start | bytes 196616 | tf_op jit(solution)/shard_map/ppermute | solution.py:18
  3.9 9.0 %collective-permute-start.1 = (bf16[2,64,2,128]{3,2,1,0:T(2,128)(2,1)S(1)}, bf16[2,64,2,128]{3,2,1,0:T(2,128)(2,1)S(1)}, u32[]{:S(2)}, u32[]{:S(2)}) collective-permute-start(bf16[2,64,2,128]{3,2,1,0:T(2,128)(2,1)S(1)} %get-tuple-element.7), channel_id=1, source_target_pairs={{8,0},{16,8},{24,16},{32,24},{40,32},{48,40},{56,48},{64,56},{72,6... | collective-permute-start | bytes 196616 | tf_op jit(solution)/shard_map/ppermute | solution.py:20
  11.0 4.6 %collective-permute-start.2 = (bf16[2,2,64,128]{3,2,1,0:T(8,128)(2,1)S(1)}, bf16[2,2,64,128]{3,2,1,0:T(8,128)(2,1)S(1)}, u32[]{:S(2)}, u32[]{:S(2)}) collective-permute-start(bf16[2,2,64,128]{3,2,1,0:T(8,128)(2,1)S(1)} %get-tuple-element.8), channel_id=1, source_target_pairs={{0,1},{1,2},{2,3},{3,4},{4,5},{5,6},{6,7},{7,0},{8,9},{9,10},{10,1... | collective-permute-start | bytes 196616 | tf_op jit(solution)/shard_map/ppermute | solution.py:18
  11.1 4.6 %collective-permute-start.3 = (bf16[2,2,64,128]{3,2,1,0:T(8,128)(2,1)S(1)}, bf16[2,2,64,128]{3,2,1,0:T(8,128)(2,1)S(1)}, u32[]{:S(2)}, u32[]{:S(2)}) collective-permute-start(bf16[2,2,64,128]{3,2,1,0:T(8,128)(2,1)S(1)} %get-tuple-element.9), channel_id=1, source_target_pairs={{1,0},{2,1},{3,2},{4,3},{5,4},{6,5},{7,6},{0,7},{9,8},{10,9},{11,1... | collective-permute-start | bytes 196616 | tf_op jit(solution)/shard_map/ppermute | solution.py:20
  18.8 2.0 %copy-start = (f32[2,64,64,128]{3,2,1,0:T(8,128)}, f32[2,64,64,128]{3,2,1,0:T(8,128)S(1)}, u32[]{:S(2)}) copy-start(f32[2,64,64,128]{3,2,1,0:T(8,128)S(1)} %fusion.3) | copy-start | bytes 12582916
  22.0 4.6 %copy-start.1 = (f32[2,64,64,128]{3,2,1,0:T(8,128)S(1)}, f32[2,64,64,128]{3,2,1,0:T(8,128)}, u32[]{:S(2)}) copy-start(f32[2,64,64,128]{3,2,1,0:T(8,128)} %copy-done) | copy-start | bytes 12582916
  27.9 1.7 %collective-permute-start.4 = (f32[136,128]{1,0:T(8,128)S(1)}, f32[136,128]{1,0:T(8,128)S(1)}, u32[]{:S(2)}, u32[]{:S(2)}) collective-permute-start(f32[136,128]{1,0:T(8,128)S(1)} %maximum_maximum_fusion), channel_id=1, source_target_pairs={{0,1},{1,0},{2,3},{3,2},{4,5},{5,4},{6,7},{7,6},{8,9},{9,8},{10,11... | collective-permute-start | bytes 208904 | tf_op jit(solution)/shard_map/ppermute | solution.py:32
  29.7 4.5 %collective-permute-start.5 = (f32[136,128]{1,0:T(8,128)S(1)}, f32[136,128]{1,0:T(8,128)S(1)}, u32[]{:S(2)}, u32[]{:S(2)}) collective-permute-start(f32[136,128]{1,0:T(8,128)S(1)} %fusion.15), channel_id=1, source_target_pairs={{0,2},{1,3},{2,0},{3,1},{4,6},{5,7},{6,4},{7,5},{8,10},{9,11},{10,... | collective-permute-start | bytes 208904 | tf_op jit(solution)/shard_map/ppermute | solution.py:32
  34.3 5.9 %collective-permute-start.6 = (f32[136,128]{1,0:T(8,128)S(1)}, f32[136,128]{1,0:T(8,128)S(1)}, u32[]{:S(2)}, u32[]{:S(2)}) collective-permute-start(f32[136,128]{1,0:T(8,128)S(1)} %add.37), channel_id=1, source_target_pairs={{0,4},{1,5},{2,6},{3,7},{4,0},{5,1},{6,2},{7,3},{8,12},{9,13},{10,... | collective-permute-start | bytes 208904 | tf_op jit(solution)/shard_map/ppermute | solution.py:32
  40.2 4.4 %collective-permute-start.7 = (f32[136,128]{1,0:T(8,128)S(1)}, f32[136,128]{1,0:T(8,128)S(1)}, u32[]{:S(2)}, u32[]{:S(2)}) collective-permute-start(f32[136,128]{1,0:T(8,128)S(1)} %add.38), channel_id=1, source_target_pairs={{0,8},{8,0},{16,24},{24,16},{32,40},{40,32},{48,56},{56,48},{64,72... | collective-permute-start | bytes 208904 | tf_op jit(solution)/shard_map/ppermute | solution.py:32
  44.6 5.6 %collective-permute-start.8 = (f32[136,128]{1,0:T(8,128)S(1)}, f32[136,128]{1,0:T(8,128)S(1)}, u32[]{:S(2)}, u32[]{:S(2)}) collective-permute-start(f32[136,128]{1,0:T(8,128)S(1)} %add.39), channel_id=1, source_target_pairs={{0,16},{8,24},{16,0},{24,8},{32,48},{40,56},{48,32},{56,40},{64,80... | collective-permute-start | bytes 208904 | tf_op jit(solution)/shard_map/ppermute | solution.py:32
  50.2 8.6 %collective-permute-start.9 = (f32[136,128]{1,0:T(8,128)S(1)}, f32[136,128]{1,0:T(8,128)S(1)}, u32[]{:S(2)}, u32[]{:S(2)}) collective-permute-start(f32[136,128]{1,0:T(8,128)S(1)} %add.40), channel_id=1, source_target_pairs={{0,32},{8,40},{16,48},{24,56},{32,0},{40,8},{48,16},{56,24},{64,96... | collective-permute-start | bytes 208904 | tf_op jit(solution)/shard_map/ppermute | solution.py:32
  58.8 4.4 %collective-permute-start.10 = (f32[136,128]{1,0:T(8,128)S(1)}, f32[136,128]{1,0:T(8,128)S(1)}, u32[]{:S(2)}, u32[]{:S(2)}) collective-permute-start(f32[136,128]{1,0:T(8,128)S(1)} %add.41), channel_id=1, source_target_pairs={{0,64},{8,72},{16,80},{24,88},{32,96},{40,104},{48,112},{56,120},{... | collective-permute-start | bytes 208904 | tf_op jit(solution)/shard_map/ppermute | solution.py:32
  63.2 6.1 %collective-permute-start.11 = (f32[136,128]{1,0:T(8,128)S(1)}, f32[136,128]{1,0:T(8,128)S(1)}, u32[]{:S(2)}, u32[]{:S(2)}) collective-permute-start(f32[136,128]{1,0:T(8,128)S(1)} %add.42), channel_id=1, source_target_pairs={{0,128},{8,136},{16,144},{24,152},{32,160},{40,168},{48,176},{56,1... | collective-permute-start | bytes 208904 | tf_op jit(solution)/shard_map/ppermute | solution.py:32

commit v4 on v3

--- a/solution.py
+++ b/solution.py
@@ -46,28 +46,6 @@
     return dot(head, head) + (cross + jnp.swapaxes(cross, 1, 2)) + dot(tail, tail)
 
 
-def pack_pair(gram):
-    n = gram.shape[-1]
-    row = lax.broadcasted_iota(jnp.int32, (n, n), 0)
-    col = lax.broadcasted_iota(jnp.int32, (n, n), 1)
-    square = jnp.where(row <= col, gram[0], gram[1])
-    diag = jnp.sum(jnp.where(row == col, gram[1], 0.0), axis=0, keepdims=True)
-    pad = jnp.zeros((7, n), gram.dtype)
-    return jnp.concatenate([square, diag, pad], axis=0)
-
-
-def unpack_pair(packed):
-    n = packed.shape[-1]
-    square = packed[:n]
-    diag = packed[n]
-    row = lax.broadcasted_iota(jnp.int32, (n, n), 0)
-    col = lax.broadcasted_iota(jnp.int32, (n, n), 1)
-    flipped = square.T
-    first = jnp.where(row <= col, square, flipped)
-    second = jnp.where(row > col, square, jnp.where(row < col, flipped, jnp.diag(diag)))
-    return jnp.stack([first, second])
-
-
 def chol_inv_kernel(g_ref, rt_ref, x_ref, s_ref):
     planes, n, _ = g_ref.shape
     s_ref[...] = g_ref[...]
@@ -76,17 +54,20 @@
     eye = jnp.where(rr == cc, 1.0, 0.0).astype(jnp.float32)
     for p in range(planes):
         x_ref[p] = eye
-    rt_ref[...] = jnp.zeros(rt_ref.shape, jnp.float32)
     lane = lax.broadcasted_iota(jnp.int32, (1, n), 1)
+    pivot = [g_ref[p, 0:1, :] for p in range(planes)]
     for j in range(n):
         lo = (j // 8) * 8
         rows = lax.broadcasted_iota(jnp.int32, (n - lo, 1), 0) + lo
         for p in range(planes):
-            rowj = s_ref[p, j:j + 1, :]
+            rowj = pivot[p]
             root = jnp.sqrt(rowj[:, j:j + 1])
             inv = 1.0 / root
             lrow = jnp.where(lane > j, rowj * inv, jnp.where(lane == j, root, 0.0))
             rt_ref[p, j:j + 1, :] = lrow
+            if j + 1 < n:
+                nxt = s_ref[p, j + 1:j + 2, :]
+                pivot[p] = nxt - (nxt[:, j:j + 1] * inv) * lrow
             blk = s_ref[p, lo:, :]
             lcol = jnp.where(rows > j, blk[:, j:j + 1] * inv, 0.0)
             s_ref[p, lo:, :] = blk - lcol * lrow
@@ -105,10 +86,9 @@
     )(gram)
 
 
-def local(u_field, w_field):
-    planes, rows_x, rows_z, snaps = u_field.shape
-    padded_u = with_halo(u_field, (("gz", 2),), 2).astype(jnp.float32)
-    padded_w = with_halo(w_field, (("gx", 1),), 2).astype(jnp.float32)
+def vorticity_of(padded_u, padded_w):
+    padded_u = padded_u.astype(jnp.float32)
+    padded_w = padded_w.astype(jnp.float32)
     span_diff = 8.0 * (padded_u[:, :, 3:-1] - padded_u[:, :, 1:-3]) - (
         padded_u[:, :, 4:] - padded_u[:, :, :-4]
     )
@@ -116,25 +96,43 @@
         padded_w[:, 4:] - padded_w[:, :-4]
     )
     vorticity = span_diff / (12.0 * span_step) - stream_diff / 12.0
-    columns = vorticity.reshape(planes, rows_x * rows_z, snaps)
-    gram_local = split_gram(columns)
-    if planes == 2:
-        gram_sum = unpack_pair(butterfly_sum(pack_pair(gram_local), ("gx", "gz")))
-    else:
-        gram_sum = butterfly_sum(gram_local, ("gx", "gz"))
+    planes, rows_x, rows_z, snaps = vorticity.shape
+    return vorticity.reshape(planes, rows_x * rows_z, snaps)
+
+
+def symmetric(gram):
+    n = gram.shape[-1]
+    row = lax.broadcasted_iota(jnp.int32, (n, n), 0)
+    col = lax.broadcasted_iota(jnp.int32, (n, n), 1)
+    return jnp.where(row <= col, gram, jnp.swapaxes(gram, 1, 2))
+
+
+def local(u_field, w_field):
+    planes, rows_x, rows_z, snaps = u_field.shape
+    padded_u = with_halo(u_field, (("gz", 2),), 2)
+    padded_w = with_halo(w_field, (("gx", 1),), 2)
     total_cells = rows_x * rows_z * lax.axis_size("gz") * lax.axis_size("gx")
-    gram = gram_sum / total_cells
-    factor_r, lower_inverse = chol_inv(gram)
-    modes = jnp.einsum(
-        "pcs,pts->pct",
-        columns,
-        lower_inverse,
-        precision=lax.Precision.HIGH,
-        preferred_element_type=jnp.float32,
-    )
-    modes = modes.reshape(planes, rows_x, rows_z, snaps)
+    modes, factor_r = [], []
+    later_u, later_w = padded_u, padded_w
+    for plane in range(planes):
+        part = vorticity_of(later_u[plane:plane + 1], later_w[plane:plane + 1])
+        gram_local = symmetric(split_gram(part))
+        gram_local, later_u, later_w = lax.optimization_barrier((gram_local, later_u, later_w))
+        gram = butterfly_sum(gram_local, ("gx", "gz")) / total_cells
+        upper, lower_inverse = chol_inv(gram)
+        factor_r.append(upper)
+        modes.append(
+            jnp.einsum(
+                "pcs,pts->pct",
+                part,
+                lower_inverse,
+                precision=lax.Precision.HIGH,
+                preferred_element_type=jnp.float32,
+            )
+        )
+    modes = jnp.concatenate(modes, axis=0).reshape(planes, rows_x, rows_z, snaps)
+    factor_r = jnp.concatenate(factor_r, axis=0)
     return (modes, factor_r)
-
 
 def solution(mesh):
     return jax.shard_map(

time: 90.6 us -> 110 us (1.21)
  starting transfers between devices: 18.5 us -> 30.8 us
  waiting for transfers between devices: 32.7 us -> 20.8 us
  Pallas kernels: 14.2 us -> 25.8 us
  local copies, waits for them, and re-layouts: 4.57 us -> 8.58 us
  other arithmetic: 6.91 us -> 10.8 us
    ppermute x8 -> x16, starting transfers between devices: 8.49 us -> 21.1 us  [butterfly_sum(): x = x + lax.ppermute(x, axis, [(i, i ^ step) for i in range(count)])]
    ppermute x8 -> x16, waiting for transfers between devices: 32.7 us -> 20.8 us  [butterfly_sum(): x = x + lax.ppermute(x, axis, [(i, i ^ step) for i in range(count)])]
    pallas_call x1 -> x2, Pallas kernels: 14.2 us -> 25.8 us  [chol_inv(): pl.pallas_call(chol_inv_kernel, out_shape=(jax.ShapeDtypeStruct(gram.shap...]
    concatenate x1 -> x3, other arithmetic: 0.08 us -> 4.68 us  [the longest x1 2.45 us: local(): jnp.concatenate(modes, axis=0).reshape(planes, rows_x, rows_z, snaps)]
    unnamed x6 -> x20, local copies, waits for them, and re-layouts: 2.12 us -> 6.18 us
    convert_element_type x2 -> x4, other arithmetic: 3.12 us -> 2.09 us  [the longest x2 1.77 us: vorticity_of(): padded_w = padded_w.astype(jnp.float32)]
    dot_general x3 -> x6, matrix products: 6.73 us -> 5.71 us  [dot(): return jnp.einsum('pcs,pct->pst', a, b, preferred_element_type=jnp.float32)]
    sub x1 -> x2, other arithmetic: 2.77 us -> 2.6 us  [vorticity_of(): vorticity = span_diff / (12.0 * span_step) - stream_diff / 12.0]
  transfers between devices with their start and end apart: 12 -> 20, of which waited for: 8 -> 10; matrix products, arithmetic and copies ran while one was open for 4% -> 13% of each run, Pallas kernels for 0% -> 12%
where the time goes in v4:
time: 110 us; the launch traced here: 109 us
  starting transfers between devices  30.8 us (28%)
  Pallas kernels  25.8 us (23%)
  waiting for transfers between devices  20.8 us (19%)
  matrix products  11.6 us (11%)
  other arithmetic  10.8 us (10%)
  local copies, waits for them, and re-layouts  8.58 us (8%)
    pallas_call x2, Pallas kernels, chol_inv(): pl.pallas_call(chol_inv_kernel, out_shape=(jax.ShapeDtypeStruct(gram.shap...  25.8 us
    ppermute x16, starting transfers between devices, butterfly_sum(): x = x + lax.ppermute(x, axis, [(i, i ^ step) for i in range(count)])  21.1 us
    ppermute x16, waiting for transfers between devices, butterfly_sum(): x = x + lax.ppermute(x, axis, [(i, i ^ step) for i in range(count)])  20.8 us
    ppermute x2, starting transfers between devices, with_halo(): lax.ppermute(head, axis, [((i + 1) % count, i) for i in range(count)])  7.67 us
    unnamed x20, local copies, waits for them, and re-layouts  6.18 us
    dot_general x2, matrix products, local(): jnp.einsum('pcs,pts->pct', part, lower_inverse, precision=lax.Precision.H...  5.93 us
    dot_general x6, matrix products, dot(): return jnp.einsum('pcs,pct->pst', a, b, preferred_element_type=jnp.float32)  5.71 us
    sub x2, other arithmetic, vorticity_of(): vorticity = span_diff / (12.0 * span_step) - stream_diff / 12.0  2.6 us
  transfers between devices with their start and end apart: 20, of which 10 were waited for; matrix products, arithmetic and copies ran while one was open for 13% of the time, Pallas kernels for 12%

profile of v4, /device:TPU:8, one launch (start us, length us, event | category | flops | bytes accessed | tf_op | source)
XLA Modules:
  0.0 109.4 jit_solution(14749877903515965799)
XLA Ops:
  1.5 1.1 %fusion.46 = (bf16[2,64,2,128]{3,2,1,0:T(2,128)(2,1)S(1)}, bf16[2,64,2,128]{3,2,1,0:T(2,128)(2,1)S(1)}) fusion(bf16[2,64,64,128]{3,2,1,0:T(8,128)(2,1)} %param.2), kind=kLoop, calls=%fused_computation.67 | loop fusion | bytes 262144 | tf_op jit(solution)/shard_map/slice | solution.py:15
  2.7 2.0 %collective-permute-start = (bf16[2,64,2,128]{3,2,1,0:T(2,128)(2,1)S(1)}, bf16[2,64,2,128]{3,2,1,0:T(2,128)(2,1)S(1)}, u32[]{:S(2)}, u32[]{:S(2)}) collective-permute-start(bf16[2,64,2,128]{3,2,1,0:T(2,128)(2,1)S(1)} %get-tuple-element.18), channel_id=1, source_target_pairs={{0,8},{8,16},{16,24},{24,32},{32,40},{40,48},{48,56},{56,64},{64,7... | collective-permute-start | bytes 196616 | tf_op jit(solution)/shard_map/ppermute | solution.py:18
  4.7 6.2 %collective-permute-start.1 = (bf16[2,64,2,128]{3,2,1,0:T(2,128)(2,1)S(1)}, bf16[2,64,2,128]{3,2,1,0:T(2,128)(2,1)S(1)}, u32[]{:S(2)}, u32[]{:S(2)}) collective-permute-start(bf16[2,64,2,128]{3,2,1,0:T(2,128)(2,1)S(1)} %get-tuple-element.19), channel_id=1, source_target_pairs={{8,0},{16,8},{24,16},{32,24},{40,32},{48,40},{56,48},{64,56},{72,6... | collective-permute-start | bytes 196616 | tf_op jit(solution)/shard_map/ppermute | solution.py:20
  10.9 1.4 %collective-permute-start.3 = (bf16[2,2,64,128]{3,2,1,0:T(8,128)(2,1)S(1)}, bf16[2,2,64,128]{3,2,1,0:T(8,128)(2,1)S(1)}, u32[]{:S(2)}, u32[]{:S(2)}) collective-permute-start(bf16[2,2,64,128]{3,2,1,0:T(8,128)(2,1)S(1)} %get-tuple-element.20), channel_id=1, source_target_pairs={{1,0},{2,1},{3,2},{4,3},{5,4},{6,5},{7,6},{0,7},{9,8},{10,9},{11,1... | collective-permute-start | bytes 196616 | tf_op jit(solution)/shard_map/ppermute | solution.py:20
  12.4 1.9 %constant_dynamic-update-slice_fusion.1 = bf16[2,68,64,128]{3,2,1,0:T(8,128)(2,1)S(1)} fusion(bf16[2,68,64,128]{3,2,1,0:T(8,128)(2,1)S(1)} %constant_dynamic-update-slice_fusion.2, bf16[2,64,64,128]{3,2,1,0:T(8,128)(2,1)} %param.3), kind=kLoop, calls=%fused_computation.65 | loop fusion | bytes 4194304
  16.7 1.6 %pad_maximum_fusion.1 = bf16[2,64,68,128]{3,2,1,0:T(8,128)(2,1)S(1)} fusion(bf16[2,64,2,128]{3,2,1,0:T(2,128)(2,1)S(1)} %collective-permute-done.1, bf16[2,64,64,128]{3,2,1,0:T(8,128)(2,1)S(1)} %copy-done.5, bf16[2,64,2,128]{3,2,1,0:T(2,128)(2,1)S(1)} %collective-permute-done), kind=kLoop, calls=%fused_computation.5 | loop fusion | flops 6684672 | bytes 4456448 | tf_op jit(solution)/shard_map/concatenate | solution.py:16
  18.3 1.4 %copy-done.2 = bf16[2,64,68,128]{3,2,1,0:T(8,128)(2,1)} copy-done((bf16[2,64,68,128]{3,2,1,0:T(8,128)(2,1)}, bf16[2,64,68,128]{3,2,1,0:T(8,128)(2,1)S(1)}, u32[]{:S(2)}) %copy-start.2) | copy-done | bytes 2228248
  19.8 1.3 %fusion.11 = f32[1,64,64,128]{3,2,1,0:T(8,128)S(1)} fusion(f32[1,68,64,128]{3,2,1,0:T(8,128)S(1)} %slice_convert_fusion.2, f32[1,64,68,128]{3,2,1,0:T(8,128)S(1)} %slice_convert_fusion), kind=kLoop, calls=%fused_computation.22 | loop fusion | flops 5767168 | bytes 18874368 | tf_op jit(solution)/shard_map/sub | solution.py:98
  23.8 1.5 %slice_convert_fusion.3 = f32[1,68,64,128]{3,2,1,0:T(8,128)S(1)} fusion(bf16[2,68,64,128]{3,2,1,0:T(8,128)(2,1)} %copy-done.6), kind=kLoop, calls=%fused_computation.47 | loop fusion | flops 557056 | bytes 3342336 | tf_op jit(solution)/shard_map/convert_element_type | solution.py:91
  25.5 1.3 %fusion.4 = f32[1,64,64,128]{3,2,1,0:T(8,128)S(1)} fusion(f32[1,68,64,128]{3,2,1,0:T(8,128)S(1)} %slice_convert_fusion.3, f32[1,64,68,128]{3,2,1,0:T(8,128)S(1)} %slice_convert_fusion.1), kind=kLoop, calls=%fused_computation.11 | loop fusion | flops 5767168 | bytes 18874368 | tf_op jit(solution)/shard_map/sub | solution.py:98
  28.3 2.9 %fusion.27 = f32[1,128,128]{1,2,0:T(8,128)S(1)} fusion(f32[1,64,64,128]{3,2,1,0:T(8,128)} %copy-done, f32[1,128,128]{1,2,0:T(8,128)S(1)} %copy.9, f32[128,128,1]{1,0,2:T(8,128)S(1)} %fusion.34), kind=kOutput, calls=%fused_computation.41 | convolution fusion | flops 135299072 | bytes 2293760 | tf_op jit(solution)/shard_map/pcs,pct->pst/dot_general | solution.py:43
  32.4 1.2 %collective-permute-start.5 = (f32[1,128,128]{2,1,0:T(8,128)S(1)}, f32[1,128,128]{2,1,0:T(8,128)S(1)}, u32[]{:S(2)}, u32[]{:S(2)}) collective-permute-start(f32[1,128,128]{2,1,0:T(8,128)S(1)} %add.69), channel_id=1, source_target_pairs={{0,2},{1,3},{2,0},{3,1},{4,6},{5,7},{6,4},{7,5},{8,10},{9,11},{10,... | collective-permute-start | bytes 196616 | tf_op jit(solution)/shard_map/ppermute | solution.py:32
  34.7 2.5 %collective-permute-done.5 = f32[1,128,128]{2,1,0:T(8,128)S(1)} collective-permute-done((f32[1,128,128]{2,1,0:T(8,128)S(1)}, f32[1,128,128]{2,1,0:T(8,128)S(1)}, u32[]{:S(2)}, u32[]{:S(2)}) %collective-permute-start.5) | collective-permute-done | bytes 65568 | tf_op jit(solution)/shard_map/ppermute | solution.py:32
  37.2 2.3 %collective-permute-start.6 = (f32[1,128,128]{2,1,0:T(8,128)S(1)}, f32[1,128,128]{2,1,0:T(8,128)S(1)}, u32[]{:S(2)}, u32[]{:S(2)}) collective-permute-start(f32[1,128,128]{2,1,0:T(8,128)S(1)} %add.70), channel_id=1, source_target_pairs={{0,4},{1,5},{2,6},{3,7},{4,0},{5,1},{6,2},{7,3},{8,12},{9,13},{10,... | collective-permute-start | bytes 196616 | tf_op jit(solution)/shard_map/ppermute | solution.py:32
  39.4 1.6 %collective-permute-start.14 = (f32[1,128,128]{2,1,0:T(8,128)S(1)}, f32[1,128,128]{2,1,0:T(8,128)S(1)}, u32[]{:S(2)}, u32[]{:S(2)}) collective-permute-start(f32[1,128,128]{2,1,0:T(8,128)S(1)} %add.81), channel_id=1, source_target_pairs={{0,4},{1,5},{2,6},{3,7},{4,0},{5,1},{6,2},{7,3},{8,12},{9,13},{10,... | collective-permute-start | bytes 196616 | tf_op jit(solution)/shard_map/ppermute | solution.py:32
  41.1 2.5 %collective-permute-done.6 = f32[1,128,128]{2,1,0:T(8,128)S(1)} collective-permute-done((f32[1,128,128]{2,1,0:T(8,128)S(1)}, f32[1,128,128]{2,1,0:T(8,128)S(1)}, u32[]{:S(2)}, u32[]{:S(2)}) %collective-permute-start.6) | collective-permute-done | bytes 65568 | tf_op jit(solution)/shard_map/ppermute | solution.py:32
  43.7 1.8 %collective-permute-done.14 = f32[1,128,128]{2,1,0:T(8,128)S(1)} collective-permute-done((f32[1,128,128]{2,1,0:T(8,128)S(1)}, f32[1,128,128]{2,1,0:T(8,128)S(1)}, u32[]{:S(2)}, u32[]{:S(2)}) %collective-permute-start.14) | collective-permute-done | bytes 65568 | tf_op jit(solution)/shard_map/ppermute | solution.py:32
  45.8 2.8 %collective-permute-done.7 = f32[1,128,128]{2,1,0:T(8,128)S(1)} collective-permute-done((f32[1,128,128]{2,1,0:T(8,128)S(1)}, f32[1,128,128]{2,1,0:T(8,128)S(1)}, u32[]{:S(2)}, u32[]{:S(2)}) %collective-permute-start.7) | collective-permute-done | bytes 65568 | tf_op jit(solution)/shard_map/ppermute | solution.py:32
  49.8 1.9 %collective-permute-start.16 = (f32[1,128,128]{2,1,0:T(8,128)S(1)}, f32[1,128,128]{2,1,0:T(8,128)S(1)}, u32[]{:S(2)}, u32[]{:S(2)}) collective-permute-start(f32[1,128,128]{2,1,0:T(8,128)S(1)} %add.83), channel_id=1, source_target_pairs={{0,16},{8,24},{16,0},{24,8},{32,48},{40,56},{48,32},{56,40},{64,80... | collective-permute-start | bytes 196616 | tf_op jit(solution)/shard_map/ppermute | solution.py:32
  51.7 2.5 %collective-permute-done.8 = f32[1,128,128]{2,1,0:T(8,128)S(1)} collective-permute-done((f32[1,128,128]{2,1,0:T(8,128)S(1)}, f32[1,128,128]{2,1,0:T(8,128)S(1)}, u32[]{:S(2)}, u32[]{:S(2)}) %collective-permute-start.8) | collective-permute-done | bytes 65568 | tf_op jit(solution)/shard_map/ppermute | solution.py:32
  54.2 1.8 %collective-permute-start.9 = (f32[1,128,128]{2,1,0:T(8,128)S(1)}, f32[1,128,128]{2,1,0:T(8,128)S(1)}, u32[]{:S(2)}, u32[]{:S(2)}) collective-permute-start(f32[1,128,128]{2,1,0:T(8,128)S(1)} %add.73), channel_id=1, source_target_pairs={{0,32},{8,40},{16,48},{24,56},{32,0},{40,8},{48,16},{56,24},{64,96... | collective-permute-start | bytes 196616 | tf_op jit(solution)/shard_map/ppermute | solution.py:32
  56.1 1.1 %collective-permute-done.16 = f32[1,128,128]{2,1,0:T(8,128)S(1)} collective-permute-done((f32[1,128,128]{2,1,0:T(8,128)S(1)}, f32[1,128,128]{2,1,0:T(8,128)S(1)}, u32[]{:S(2)}, u32[]{:S(2)}) %collective-permute-start.16) | collective-permute-done | bytes 65568 | tf_op jit(solution)/shard_map/ppermute | solution.py:32
  57.2 3.2 %collective-permute-start.17 = (f32[1,128,128]{2,1,0:T(8,128)S(1)}, f32[1,128,128]{2,1,0:T(8,128)S(1)}, u32[]{:S(2)}, u32[]{:S(2)}) collective-permute-start(f32[1,128,128]{2,1,0:T(8,128)S(1)} %add.84), channel_id=1, source_target_pairs={{0,32},{8,40},{16,48},{24,56},{32,0},{40,8},{48,16},{56,24},{64,96... | collective-permute-start | bytes 196616 | tf_op jit(solution)/shard_map/ppermute | solution.py:32
  60.4 2.2 %collective-permute-done.9 = f32[1,128,128]{2,1,0:T(8,128)S(1)} collective-permute-done((f32[1,128,128]{2,1,0:T(8,128)S(1)}, f32[1,128,128]{2,1,0:T(8,128)S(1)}, u32[]{:S(2)}, u32[]{:S(2)}) %collective-permute-start.9) | collective-permute-done | bytes 65568 | tf_op jit(solution)/shard_map/ppermute | solution.py:32
  62.7 3.5 %collective-permute-done.17 = f32[1,128,128]{2,1,0:T(8,128)S(1)} collective-permute-done((f32[1,128,128]{2,1,0:T(8,128)S(1)}, f32[1,128,128]{2,1,0:T(8,128)S(1)}, u32[]{:S(2)}, u32[]{:S(2)}) %collective-permute-start.17) | collective-permute-done | bytes 65568 | tf_op jit(solution)/shard_map/ppermute | solution.py:32
  67.3 2.6 %collective-permute-start.11 = (f32[1,128,128]{2,1,0:T(8,128)S(1)}, f32[1,128,128]{2,1,0:T(8,128)S(1)}, u32[]{:S(2)}, u32[]{:S(2)}) collective-permute-start(f32[1,128,128]{2,1,0:T(8,128)S(1)} %add.75), channel_id=1, source_target_pairs={{0,128},{8,136},{16,144},{24,152},{32,160},{40,168},{48,176},{56,1... | collective-permute-start | bytes 196616 | tf_op jit(solution)/shard_map/ppermute | solution.py:32
  70.5 2.6 %collective-permute-start.19 = (f32[1,128,128]{2,1,0:T(8,128)S(1)}, f32[1,128,128]{2,1,0:T(8,128)S(1)}, u32[]{:S(2)}, u32[]{:S(2)}) collective-permute-start(f32[1,128,128]{2,1,0:T(8,128)S(1)} %add.86), channel_id=1, source_target_pairs={{0,128},{8,136},{16,144},{24,152},{32,160},{40,168},{48,176},{56,1... | collective-permute-start | bytes 196616 | tf_op jit(solution)/shard_map/ppermute | solution.py:32
  73.8 12.9 %shard_map.41 = (f32[1,128,128]{2,1,0:T(8,128)}, f32[1,128,128]{2,1,0:T(8,128)}) custom-call(f32[1,128,128]{2,1,0:T(8,128)} %add_multiply_fusion.1.g_ref), custom_call_target="tpu_custom_call" | custom-call | tf_op jit(solution)/shard_map/pallas_call | solution.py:80
  86.7 3.2 %fusion.20 = f32[1,64,64,128]{3,2,1,0:T(8,128)} fusion(f32[1,64,64,128]{3,2,1,0:T(8,128)S(1)} %fusion.11, f32[1,128,128]{2,1,0:T(8,128)} %get-tuple-element.11), kind=kOutput, calls=%fused_computation.34 | convolution fusion | flops 402653184 | bytes 4259840 | tf_op jit(solution)/shard_map/pcs,pts->pct/dot_general | solution.py:125
  90.5 12.9 %shard_map.42 = (f32[1,128,128]{2,1,0:T(8,128)}, f32[1,128,128]{2,1,0:T(8,128)}) custom-call(f32[1,128,128]{2,1,0:T(8,128)} %add_multiply_fusion.g_ref), custom_call_target="tpu_custom_call" | custom-call | tf_op jit(solution)/shard_map/pallas_call | solution.py:80
  103.5 2.7 %fusion.23 = f32[1,64,64,128]{3,2,1,0:T(8,128)S(1)} fusion(f32[1,64,64,128]{3,2,1,0:T(8,128)} %copy-done, f32[1,128,128]{2,1,0:T(8,128)} %get-tuple-element.15), kind=kOutput, calls=%fused_computation.35 | convolution fusion | flops 402653184 | bytes 4259840 | tf_op jit(solution)/shard_map/pcs,pts->pct/dot_general | solution.py:125
  106.2 2.5 %pad_maximum_fusion = f32[2,64,64,128]{3,2,1,0:T(8,128)} fusion(f32[1,64,64,128]{3,2,1,0:T(8,128)S(1)} %fusion.23, f32[1,64,64,128]{3,2,1,0:T(8,128)S(1)} %copy-done.4), kind=kLoop, calls=%fused_computation | loop fusion | flops 1048576 | bytes 8388608 | tf_op jit(solution)/shard_map/concatenate | solution.py:133
  (72 shorter events, 15.5 us)
Async XLA Ops:
  1.5 10.8 %collective-permute-start.2 = (bf16[2,2,64,128]{3,2,1,0:T(8,128)(2,1)S(1)}, bf16[2,2,64,128]{3,2,1,0:T(8,128)(2,1)S(1)}, u32[]{:S(2)}, u32[]{:S(2)}) collective-permute-start(bf16[2,2,64,128]{3,2,1,0:T(8,128)(2,1)S(1)} %get-tuple-element.21), channel_id=1, source_target_pairs={{0,1},{1,2},{2,3},{3,4},{4,5},{5,6},{6,7},{7,0},{8,9},{9,10},{10,1... | collective-permute-start | bytes 196616 | tf_op jit(solution)/shard_map/ppermute | solution.py:18
  2.7 11.9 %collective-permute-start = (bf16[2,64,2,128]{3,2,1,0:T(2,128)(2,1)S(1)}, bf16[2,64,2,128]{3,2,1,0:T(2,128)(2,1)S(1)}, u32[]{:S(2)}, u32[]{:S(2)}) collective-permute-start(bf16[2,64,2,128]{3,2,1,0:T(2,128)(2,1)S(1)} %get-tuple-element.18), channel_id=1, source_target_pairs={{0,8},{8,16},{16,24},{24,32},{32,40},{40,48},{48,56},{56,64},{64,7... | collective-permute-start | bytes 196616 | tf_op jit(solution)/shard_map/ppermute | solution.py:18
  4.7 11.0 %collective-permute-start.1 = (bf16[2,64,2,128]{3,2,1,0:T(2,128)(2,1)S(1)}, bf16[2,64,2,128]{3,2,1,0:T(2,128)(2,1)S(1)}, u32[]{:S(2)}, u32[]{:S(2)}) collective-permute-start(bf16[2,64,2,128]{3,2,1,0:T(2,128)(2,1)S(1)} %get-tuple-element.19), channel_id=1, source_target_pairs={{8,0},{16,8},{24,16},{32,24},{40,32},{48,40},{56,48},{64,56},{72,6... | collective-permute-start | bytes 196616 | tf_op jit(solution)/shard_map/ppermute | solution.py:20
  10.9 3.4 %collective-permute-start.3 = (bf16[2,2,64,128]{3,2,1,0:T(8,128)(2,1)S(1)}, bf16[2,2,64,128]{3,2,1,0:T(8,128)(2,1)S(1)}, u32[]{:S(2)}, u32[]{:S(2)}) collective-permute-start(bf16[2,2,64,128]{3,2,1,0:T(8,128)(2,1)S(1)} %get-tuple-element.20), channel_id=1, source_target_pairs={{1,0},{2,1},{3,2},{4,3},{5,4},{6,5},{7,6},{0,7},{9,8},{10,9},{11,1... | collective-permute-start | bytes 196616 | tf_op jit(solution)/shard_map/ppermute | solution.py:20
  14.3 2.4 %copy-start.5 = (bf16[2,64,64,128]{3,2,1,0:T(8,128)(2,1)S(1)}, bf16[2,64,64,128]{3,2,1,0:T(8,128)(2,1)}, u32[]{:S(2)}) copy-start(bf16[2,64,64,128]{3,2,1,0:T(8,128)(2,1)} %param.2) | copy-start | bytes 6291460
  14.3 1.4 %copy-start.6 = (bf16[2,68,64,128]{3,2,1,0:T(8,128)(2,1)}, bf16[2,68,64,128]{3,2,1,0:T(8,128)(2,1)S(1)}, u32[]{:S(2)}) copy-start(bf16[2,68,64,128]{3,2,1,0:T(8,128)(2,1)S(1)} %constant_dynamic-update-slice_fusion) | copy-start | bytes 6684676
  18.2 1.4 %copy-start.2 = (bf16[2,64,68,128]{3,2,1,0:T(8,128)(2,1)}, bf16[2,64,68,128]{3,2,1,0:T(8,128)(2,1)S(1)}, u32[]{:S(2)}) copy-start(bf16[2,64,68,128]{3,2,1,0:T(8,128)(2,1)S(1)} %pad_maximum_fusion.1) | copy-start | bytes 6684676
  22.9 2.4 %copy-start.3 = (bf16[2,64,68,128]{3,2,1,0:T(8,128)(2,1)S(1)}, bf16[2,64,68,128]{3,2,1,0:T(8,128)(2,1)}, u32[]{:S(2)}) copy-start(bf16[2,64,68,128]{3,2,1,0:T(8,128)(2,1)} %copy-done.2) | copy-start | bytes 6684676
  23.0 9.4 %collective-permute-start.4 = (f32[1,128,128]{2,1,0:T(8,128)S(1)}, f32[1,128,128]{2,1,0:T(8,128)S(1)}, u32[]{:S(2)}, u32[]{:S(2)}) collective-permute-start(f32[1,128,128]{2,1,0:T(8,128)S(1)} %bitcast_select_fusion.1), channel_id=1, source_target_pairs={{0,1},{1,0},{2,3},{3,2},{4,5},{5,4},{6,7},{7,6},{8,9},{9,8},{10,11... | collective-permute-start | bytes 196616 | tf_op jit(solution)/shard_map/ppermute | solution.py:32
  26.8 1.3 %copy-start = (f32[1,64,64,128]{3,2,1,0:T(8,128)}, f32[1,64,64,128]{3,2,1,0:T(8,128)S(1)}, u32[]{:S(2)}) copy-start(f32[1,64,64,128]{3,2,1,0:T(8,128)S(1)} %fusion.4) | copy-start | bytes 6291460
  28.3 2.9 %copy-start.1 = (f32[1,64,64,128]{3,2,1,0:T(8,128)S(1)}, f32[1,64,64,128]{3,2,1,0:T(8,128)}, u32[]{:S(2)}) copy-start(f32[1,64,64,128]{3,2,1,0:T(8,128)} %copy-done) | copy-start | bytes 6291460
  31.9 1.6 %collective-permute-start.12 = (f32[1,128,128]{2,1,0:T(8,128)S(1)}, f32[1,128,128]{2,1,0:T(8,128)S(1)}, u32[]{:S(2)}, u32[]{:S(2)}) collective-permute-start(f32[1,128,128]{2,1,0:T(8,128)S(1)} %bitcast_select_fusion), channel_id=1, source_target_pairs={{0,1},{1,0},{2,3},{3,2},{4,5},{5,4},{6,7},{7,6},{8,9},{9,8},{10,11... | collective-permute-start | bytes 196616 | tf_op jit(solution)/shard_map/ppermute | solution.py:32
  32.4 4.8 %collective-permute-start.5 = (f32[1,128,128]{2,1,0:T(8,128)S(1)}, f32[1,128,128]{2,1,0:T(8,128)S(1)}, u32[]{:S(2)}, u32[]{:S(2)}) collective-permute-start(f32[1,128,128]{2,1,0:T(8,128)S(1)} %add.69), channel_id=1, source_target_pairs={{0,2},{1,3},{2,0},{3,1},{4,6},{5,7},{6,4},{7,5},{8,10},{9,11},{10,... | collective-permute-start | bytes 196616 | tf_op jit(solution)/shard_map/ppermute | solution.py:32
  33.6 5.8 %collective-permute-start.13 = (f32[1,128,128]{2,1,0:T(8,128)S(1)}, f32[1,128,128]{2,1,0:T(8,128)S(1)}, u32[]{:S(2)}, u32[]{:S(2)}) collective-permute-start(f32[1,128,128]{2,1,0:T(8,128)S(1)} %add.80), channel_id=1, source_target_pairs={{0,2},{1,3},{2,0},{3,1},{4,6},{5,7},{6,4},{7,5},{8,10},{9,11},{10,... | collective-permute-start | bytes 196616 | tf_op jit(solution)/shard_map/ppermute | solution.py:32
  37.2 6.4 %collective-permute-start.6 = (f32[1,128,128]{2,1,0:T(8,128)S(1)}, f32[1,128,128]{2,1,0:T(8,128)S(1)}, u32[]{:S(2)}, u32[]{:S(2)}) collective-permute-start(f32[1,128,128]{2,1,0:T(8,128)S(1)} %add.70), channel_id=1, source_target_pairs={{0,4},{1,5},{2,6},{3,7},{4,0},{5,1},{6,2},{7,3},{8,12},{9,13},{10,... | collective-permute-start | bytes 196616 | tf_op jit(solution)/shard_map/ppermute | solution.py:32
  39.4 6.0 %collective-permute-start.14 = (f32[1,128,128]{2,1,0:T(8,128)S(1)}, f32[1,128,128]{2,1,0:T(8,128)S(1)}, u32[]{:S(2)}, u32[]{:S(2)}) collective-permute-start(f32[1,128,128]{2,1,0:T(8,128)S(1)} %add.81), channel_id=1, source_target_pairs={{0,4},{1,5},{2,6},{3,7},{4,0},{5,1},{6,2},{7,3},{8,12},{9,13},{10,... | collective-permute-start | bytes 196616 | tf_op jit(solution)/shard_map/ppermute | solution.py:32
  43.6 5.1 %collective-permute-start.7 = (f32[1,128,128]{2,1,0:T(8,128)S(1)}, f32[1,128,128]{2,1,0:T(8,128)S(1)}, u32[]{:S(2)}, u32[]{:S(2)}) collective-permute-start(f32[1,128,128]{2,1,0:T(8,128)S(1)} %add.71), channel_id=1, source_target_pairs={{0,8},{8,0},{16,24},{24,16},{32,40},{40,32},{48,56},{56,48},{64,72... | collective-permute-start | bytes 196616 | tf_op jit(solution)/shard_map/ppermute | solution.py:32
  45.5 4.4 %collective-permute-start.15 = (f32[1,128,128]{2,1,0:T(8,128)S(1)}, f32[1,128,128]{2,1,0:T(8,128)S(1)}, u32[]{:S(2)}, u32[]{:S(2)}) collective-permute-start(f32[1,128,128]{2,1,0:T(8,128)S(1)} %add.82), channel_id=1, source_target_pairs={{0,8},{8,0},{16,24},{24,16},{32,40},{40,32},{48,56},{56,48},{64,72... | collective-permute-start | bytes 196616 | tf_op jit(solution)/shard_map/ppermute | solution.py:32
  48.6 5.6 %collective-permute-start.8 = (f32[1,128,128]{2,1,0:T(8,128)S(1)}, f32[1,128,128]{2,1,0:T(8,128)S(1)}, u32[]{:S(2)}, u32[]{:S(2)}) collective-permute-start(f32[1,128,128]{2,1,0:T(8,128)S(1)} %add.72), channel_id=1, source_target_pairs={{0,16},{8,24},{16,0},{24,8},{32,48},{40,56},{48,32},{56,40},{64,80... | collective-permute-start | bytes 196616 | tf_op jit(solution)/shard_map/ppermute | solution.py:32
  49.8 7.4 %collective-permute-start.16 = (f32[1,128,128]{2,1,0:T(8,128)S(1)}, f32[1,128,128]{2,1,0:T(8,128)S(1)}, u32[]{:S(2)}, u32[]{:S(2)}) collective-permute-start(f32[1,128,128]{2,1,0:T(8,128)S(1)} %add.83), channel_id=1, source_target_pairs={{0,16},{8,24},{16,0},{24,8},{32,48},{40,56},{48,32},{56,40},{64,80... | collective-permute-start | bytes 196616 | tf_op jit(solution)/shard_map/ppermute | solution.py:32
  54.2 8.3 %collective-permute-start.9 = (f32[1,128,128]{2,1,0:T(8,128)S(1)}, f32[1,128,128]{2,1,0:T(8,128)S(1)}, u32[]{:S(2)}, u32[]{:S(2)}) collective-permute-start(f32[1,128,128]{2,1,0:T(8,128)S(1)} %add.73), channel_id=1, source_target_pairs={{0,32},{8,40},{16,48},{24,56},{32,0},{40,8},{48,16},{56,24},{64,96... | collective-permute-start | bytes 196616 | tf_op jit(solution)/shard_map/ppermute | solution.py:32
  57.2 9.0 %collective-permute-start.17 = (f32[1,128,128]{2,1,0:T(8,128)S(1)}, f32[1,128,128]{2,1,0:T(8,128)S(1)}, u32[]{:S(2)}, u32[]{:S(2)}) collective-permute-start(f32[1,128,128]{2,1,0:T(8,128)S(1)} %add.84), channel_id=1, source_target_pairs={{0,32},{8,40},{16,48},{24,56},{32,0},{40,8},{48,16},{56,24},{64,96... | collective-permute-start | bytes 196616 | tf_op jit(solution)/shard_map/ppermute | solution.py:32
  62.5 4.7 %collective-permute-start.10 = (f32[1,128,128]{2,1,0:T(8,128)S(1)}, f32[1,128,128]{2,1,0:T(8,128)S(1)}, u32[]{:S(2)}, u32[]{:S(2)}) collective-permute-start(f32[1,128,128]{2,1,0:T(8,128)S(1)} %add.74), channel_id=1, source_target_pairs={{0,64},{8,72},{16,80},{24,88},{32,96},{40,104},{48,112},{56,120},{... | collective-permute-start | bytes 196616 | tf_op jit(solution)/shard_map/ppermute | solution.py:32
  66.2 4.4 %collective-permute-start.18 = (f32[1,128,128]{2,1,0:T(8,128)S(1)}, f32[1,128,128]{2,1,0:T(8,128)S(1)}, u32[]{:S(2)}, u32[]{:S(2)}) collective-permute-start(f32[1,128,128]{2,1,0:T(8,128)S(1)} %add.85), channel_id=1, source_target_pairs={{0,64},{8,72},{16,80},{24,88},{32,96},{40,104},{48,112},{56,120},{... | collective-permute-start | bytes 196616 | tf_op jit(solution)/shard_map/ppermute | solution.py:32
  67.3 5.9 %collective-permute-start.11 = (f32[1,128,128]{2,1,0:T(8,128)S(1)}, f32[1,128,128]{2,1,0:T(8,128)S(1)}, u32[]{:S(2)}, u32[]{:S(2)}) collective-permute-start(f32[1,128,128]{2,1,0:T(8,128)S(1)} %add.75), channel_id=1, source_target_pairs={{0,128},{8,136},{16,144},{24,152},{32,160},{40,168},{48,176},{56,1... | collective-permute-start | bytes 196616 | tf_op jit(solution)/shard_map/ppermute | solution.py:32
  70.5 19.4 %collective-permute-start.19 = (f32[1,128,128]{2,1,0:T(8,128)S(1)}, f32[1,128,128]{2,1,0:T(8,128)S(1)}, u32[]{:S(2)}, u32[]{:S(2)}) collective-permute-start(f32[1,128,128]{2,1,0:T(8,128)S(1)} %add.86), channel_id=1, source_target_pairs={{0,128},{8,136},{16,144},{24,152},{32,160},{40,168},{48,176},{56,1... | collective-permute-start | bytes 196616 | tf_op jit(solution)/shard_map/ppermute | solution.py:32
  103.5 2.7 %copy-start.4 = (f32[1,64,64,128]{3,2,1,0:T(8,128)S(1)}, f32[1,64,64,128]{3,2,1,0:T(8,128)}, u32[]{:S(2)}) copy-start(f32[1,64,64,128]{3,2,1,0:T(8,128)} %fusion.20) | copy-start | bytes 6291460
  106.2 2.5 %copy-start.7 = (f32[1,128,128]{2,1,0:T(8,128)S(1)}, f32[1,128,128]{2,1,0:T(8,128)}, u32[]{:S(2)}) copy-start(f32[1,128,128]{2,1,0:T(8,128)} %get-tuple-element.16) | copy-start | bytes 196612
  106.2 2.5 %copy-start.8 = (f32[1,128,128]{2,1,0:T(8,128)S(1)}, f32[1,128,128]{2,1,0:T(8,128)}, u32[]{:S(2)}) copy-start(f32[1,128,128]{2,1,0:T(8,128)} %get-tuple-element.17) | copy-start | bytes 196612

commit v5 on v3

--- a/solution.py
+++ b/solution.py
@@ -76,17 +76,20 @@
     eye = jnp.where(rr == cc, 1.0, 0.0).astype(jnp.float32)
     for p in range(planes):
         x_ref[p] = eye
-    rt_ref[...] = jnp.zeros(rt_ref.shape, jnp.float32)
     lane = lax.broadcasted_iota(jnp.int32, (1, n), 1)
+    pivot = [g_ref[p, 0:1, :] for p in range(planes)]
     for j in range(n):
         lo = (j // 8) * 8
         rows = lax.broadcasted_iota(jnp.int32, (n - lo, 1), 0) + lo
         for p in range(planes):
-            rowj = s_ref[p, j:j + 1, :]
+            rowj = pivot[p]
             root = jnp.sqrt(rowj[:, j:j + 1])
-            inv = 1.0 / root
+            inv = lax.rsqrt(rowj[:, j:j + 1])
             lrow = jnp.where(lane > j, rowj * inv, jnp.where(lane == j, root, 0.0))
             rt_ref[p, j:j + 1, :] = lrow
+            if j + 1 < n:
+                nxt = s_ref[p, j + 1:j + 2, :]
+                pivot[p] = nxt - (nxt[:, j:j + 1] * inv) * lrow
             blk = s_ref[p, lo:, :]
             lcol = jnp.where(rows > j, blk[:, j:j + 1] * inv, 0.0)
             s_ref[p, lo:, :] = blk - lcol * lrow

time: 90.6 us -> 89.2 us (0.985)
  Pallas kernels: 14.2 us -> 12.8 us
    pallas_call x1, Pallas kernels: 14.2 us -> 12.8 us  [chol_inv(): pl.pallas_call(chol_inv_kernel, out_shape=(jax.ShapeDtypeStruct(gram.shap...]
where the time goes in v5:
time: 89.2 us; the launch traced here: 89 us
  waiting for transfers between devices  32.7 us (37%)
  starting transfers between devices  18.5 us (21%)
  Pallas kernels  12.8 us (14%)
  matrix products  12.7 us (14%)
  other arithmetic  6.91 us (8%)
  local copies, waits for them, and re-layouts  4.57 us (5%)
    ppermute x8, waiting for transfers between devices, butterfly_sum(): x = x + lax.ppermute(x, axis, [(i, i ^ step) for i in range(count)])  32.7 us
    pallas_call x1, Pallas kernels, chol_inv(): pl.pallas_call(chol_inv_kernel, out_shape=(jax.ShapeDtypeStruct(gram.shap...  12.8 us
    ppermute x8, starting transfers between devices, butterfly_sum(): x = x + lax.ppermute(x, axis, [(i, i ^ step) for i in range(count)])  8.49 us
    ppermute x2, starting transfers between devices, with_halo(): lax.ppermute(head, axis, [((i + 1) % count, i) for i in range(count)])  7.96 us
    dot_general x3, matrix products, dot(): return jnp.einsum('pcs,pct->pst', a, b, preferred_element_type=jnp.float32)  6.73 us
    dot_general x1, matrix products, local(): jnp.einsum('pcs,pts->pct', columns, lower_inverse, precision=lax.Precisio...  6 us
    convert_element_type x1, other arithmetic, local(): padded_u = with_halo(u_field, (('gz', 2),), 2).astype(jnp.float32)  2.78 us
    sub x1, other arithmetic, local(): vorticity = span_diff / (12.0 * span_step) - stream_diff / 12.0  2.77 us
  transfers between devices with their start and end apart: 12, of which 8 were waited for; matrix products, arithmetic and copies ran while one was open for 4% of the time, Pallas kernels for 0%

profile of v5, /device:TPU:8, one launch (start us, length us, event | category | flops | bytes accessed | tf_op | source)
XLA Modules:
  0.0 89.0 jit_solution(8098568246609209682)
XLA Ops:
  0.6 1.3 %fusion.16 = (bf16[2,64,2,128]{3,2,1,0:T(2,128)(2,1)S(1)}, bf16[2,64,2,128]{3,2,1,0:T(2,128)(2,1)S(1)}) fusion(bf16[2,64,64,128]{3,2,1,0:T(8,128)(2,1)} %param.2), kind=kLoop, calls=%fused_computation.37 | loop fusion | bytes 262144 | tf_op jit(solution)/shard_map/slice | solution.py:15
  1.9 2.0 %collective-permute-start = (bf16[2,64,2,128]{3,2,1,0:T(2,128)(2,1)S(1)}, bf16[2,64,2,128]{3,2,1,0:T(2,128)(2,1)S(1)}, u32[]{:S(2)}, u32[]{:S(2)}) collective-permute-start(bf16[2,64,2,128]{3,2,1,0:T(2,128)(2,1)S(1)} %get-tuple-element.6), channel_id=1, source_target_pairs={{0,8},{8,16},{16,24},{24,32},{32,40},{40,48},{48,56},{56,64},{64,7... | collective-permute-start | bytes 196616 | tf_op jit(solution)/shard_map/ppermute | solution.py:18
  3.9 6.2 %collective-permute-start.1 = (bf16[2,64,2,128]{3,2,1,0:T(2,128)(2,1)S(1)}, bf16[2,64,2,128]{3,2,1,0:T(2,128)(2,1)S(1)}, u32[]{:S(2)}, u32[]{:S(2)}) collective-permute-start(bf16[2,64,2,128]{3,2,1,0:T(2,128)(2,1)S(1)} %get-tuple-element.7), channel_id=1, source_target_pairs={{8,0},{16,8},{24,16},{32,24},{40,32},{48,40},{56,48},{64,56},{72,6... | collective-permute-start | bytes 196616 | tf_op jit(solution)/shard_map/ppermute | solution.py:20
  10.2 0.9 fusion.17
  11.1 1.7 %collective-permute-start.3 = (bf16[2,2,64,128]{3,2,1,0:T(8,128)(2,1)S(1)}, bf16[2,2,64,128]{3,2,1,0:T(8,128)(2,1)S(1)}, u32[]{:S(2)}, u32[]{:S(2)}) collective-permute-start(bf16[2,2,64,128]{3,2,1,0:T(8,128)(2,1)S(1)} %get-tuple-element.9), channel_id=1, source_target_pairs={{1,0},{2,1},{3,2},{4,3},{5,4},{6,5},{7,6},{0,7},{9,8},{10,9},{11,1... | collective-permute-start | bytes 196616 | tf_op jit(solution)/shard_map/ppermute | solution.py:20
  12.9 2.8 %maximum_convert_fusion = f32[2,64,68,128]{3,2,1,0:T(8,128)S(1)} fusion(bf16[2,64,2,128]{3,2,1,0:T(2,128)(2,1)S(1)} %collective-permute-done.1, bf16[2,64,64,128]{3,2,1,0:T(8,128)(2,1)} %param.2, bf16[2,64,2,128]{3,2,1,0:T(2,128)(2,1)S(1)} %collective-permute-done), kind=kLoop, calls=%fused_computation.14 | loop fusion | flops 6684672 | bytes 6684672 | tf_op jit(solution)/shard_map/convert_element_type | solution.py:113
  15.7 0.3 maximum_convert_fusion.1
  16.0 2.8 %fusion.3 = f32[2,64,64,128]{3,2,1,0:T(8,128)S(1)} fusion(f32[2,68,64,128]{3,2,1,0:T(8,128)S(1)} %maximum_convert_fusion.1, f32[2,64,68,128]{3,2,1,0:T(8,128)S(1)} %maximum_convert_fusion), kind=kLoop, calls=%fused_computation.6 | loop fusion | flops 11534336 | bytes 37748736 | tf_op jit(solution)/shard_map/sub | solution.py:121
  18.8 2.0 %copy-done = f32[2,64,64,128]{3,2,1,0:T(8,128)} copy-done((f32[2,64,64,128]{3,2,1,0:T(8,128)}, f32[2,64,64,128]{3,2,1,0:T(8,128)S(1)}, u32[]{:S(2)}) %copy-start) | copy-done | bytes 4194328
  20.8 1.1 %fusion.8 = f32[2,128,128]{2,1,0:T(8,128)S(1)} fusion(f32[2,4096,128]{2,1,0:T(8,128)S(1)} %bitcast.34), kind=kOutput, calls=%fused_computation.18 | convolution fusion | flops 273678336 | bytes 4325376 | tf_op jit(solution)/shard_map/pcs,pct->pst/dot_general | solution.py:43
  21.9 0.1 copy.6
  22.0 4.5 %convolution_add_fusion.1 = f32[2,128,128]{2,1,0:T(8,128)S(1)} fusion(f32[2,4096,128]{2,1,0:T(8,128)} %bitcast.35, f32[2,128,128]{2,1,0:T(8,128)S(1)} %fusion.8, f32[2,128,128]{1,2,0:T(8,128)S(1)} %copy.6), kind=kOutput, calls=%fused_computation.17 | convolution fusion | flops 270598144 | bytes 4587520 | tf_op jit(solution)/shard_map/pcs,pct->pst/dot_general | solution.py:43
  26.5 0.2 copy-done.1
  26.6 1.2 %convolution_add_fusion = f32[2,128,128]{2,1,0:T(8,128)S(1)} fusion(f32[2,128,128]{2,1,0:T(8,128)S(1)} %convolution_add_fusion.1, f32[2,4096,128]{2,1,0:T(8,128)S(1)} %bitcast.37), kind=kOutput, calls=%fused_computation.16 | convolution fusion | flops 271613952 | bytes 4456448 | tf_op jit(solution)/shard_map/pcs,pct->pst/dot_general | solution.py:43
  27.9 0.8 collective-permute-start.4
  28.7 0.9 %collective-permute-done.4 = f32[136,128]{1,0:T(8,128)S(1)} collective-permute-done((f32[136,128]{1,0:T(8,128)S(1)}, f32[136,128]{1,0:T(8,128)S(1)}, u32[]{:S(2)}, u32[]{:S(2)}) %collective-permute-start.4) | collective-permute-done | bytes 69664 | tf_op jit(solution)/shard_map/ppermute | solution.py:32
  29.7 1.4 %collective-permute-start.5 = (f32[136,128]{1,0:T(8,128)S(1)}, f32[136,128]{1,0:T(8,128)S(1)}, u32[]{:S(2)}, u32[]{:S(2)}) collective-permute-start(f32[136,128]{1,0:T(8,128)S(1)} %fusion.15), channel_id=1, source_target_pairs={{0,2},{1,3},{2,0},{3,1},{4,6},{5,7},{6,4},{7,5},{8,10},{9,11},{10,... | collective-permute-start | bytes 208904 | tf_op jit(solution)/shard_map/ppermute | solution.py:32
  31.1 3.2 %collective-permute-done.5 = f32[136,128]{1,0:T(8,128)S(1)} collective-permute-done((f32[136,128]{1,0:T(8,128)S(1)}, f32[136,128]{1,0:T(8,128)S(1)}, u32[]{:S(2)}, u32[]{:S(2)}) %collective-permute-start.5) | collective-permute-done | bytes 69664 | tf_op jit(solution)/shard_map/ppermute | solution.py:32
  34.3 2.2 %collective-permute-start.6 = (f32[136,128]{1,0:T(8,128)S(1)}, f32[136,128]{1,0:T(8,128)S(1)}, u32[]{:S(2)}, u32[]{:S(2)}) collective-permute-start(f32[136,128]{1,0:T(8,128)S(1)} %add.37), channel_id=1, source_target_pairs={{0,4},{1,5},{2,6},{3,7},{4,0},{5,1},{6,2},{7,3},{8,12},{9,13},{10,... | collective-permute-start | bytes 208904 | tf_op jit(solution)/shard_map/ppermute | solution.py:32
  36.5 3.7 %collective-permute-done.6 = f32[136,128]{1,0:T(8,128)S(1)} collective-permute-done((f32[136,128]{1,0:T(8,128)S(1)}, f32[136,128]{1,0:T(8,128)S(1)}, u32[]{:S(2)}, u32[]{:S(2)}) %collective-permute-start.6) | collective-permute-done | bytes 69664 | tf_op jit(solution)/shard_map/ppermute | solution.py:32
  40.2 0.1 collective-permute-start.7
  40.3 4.3 %collective-permute-done.7 = f32[136,128]{1,0:T(8,128)S(1)} collective-permute-done((f32[136,128]{1,0:T(8,128)S(1)}, f32[136,128]{1,0:T(8,128)S(1)}, u32[]{:S(2)}, u32[]{:S(2)}) %collective-permute-start.7) | collective-permute-done | bytes 69664 | tf_op jit(solution)/shard_map/ppermute | solution.py:32
  44.6 0.5 collective-permute-start.8
  45.1 5.1 %collective-permute-done.8 = f32[136,128]{1,0:T(8,128)S(1)} collective-permute-done((f32[136,128]{1,0:T(8,128)S(1)}, f32[136,128]{1,0:T(8,128)S(1)}, u32[]{:S(2)}, u32[]{:S(2)}) %collective-permute-start.8) | collective-permute-done | bytes 69664 | tf_op jit(solution)/shard_map/ppermute | solution.py:32
  50.2 2.3 %collective-permute-start.9 = (f32[136,128]{1,0:T(8,128)S(1)}, f32[136,128]{1,0:T(8,128)S(1)}, u32[]{:S(2)}, u32[]{:S(2)}) collective-permute-start(f32[136,128]{1,0:T(8,128)S(1)} %add.40), channel_id=1, source_target_pairs={{0,32},{8,40},{16,48},{24,56},{32,0},{40,8},{48,16},{56,24},{64,96... | collective-permute-start | bytes 208904 | tf_op jit(solution)/shard_map/ppermute | solution.py:32
  52.5 6.3 %collective-permute-done.9 = f32[136,128]{1,0:T(8,128)S(1)} collective-permute-done((f32[136,128]{1,0:T(8,128)S(1)}, f32[136,128]{1,0:T(8,128)S(1)}, u32[]{:S(2)}, u32[]{:S(2)}) %collective-permute-start.9) | collective-permute-done | bytes 69664 | tf_op jit(solution)/shard_map/ppermute | solution.py:32
  58.9 4.3 %collective-permute-done.10 = f32[136,128]{1,0:T(8,128)S(1)} collective-permute-done((f32[136,128]{1,0:T(8,128)S(1)}, f32[136,128]{1,0:T(8,128)S(1)}, u32[]{:S(2)}, u32[]{:S(2)}) %collective-permute-start.10) | collective-permute-done | bytes 69664 | tf_op jit(solution)/shard_map/ppermute | solution.py:32
  63.2 1.1 %collective-permute-start.11 = (f32[136,128]{1,0:T(8,128)S(1)}, f32[136,128]{1,0:T(8,128)S(1)}, u32[]{:S(2)}, u32[]{:S(2)}) collective-permute-start(f32[136,128]{1,0:T(8,128)S(1)} %add.42), channel_id=1, source_target_pairs={{0,128},{8,136},{16,144},{24,152},{32,160},{40,168},{48,176},{56,1... | collective-permute-start | bytes 208904 | tf_op jit(solution)/shard_map/ppermute | solution.py:32
  64.3 5.0 %collective-permute-done.11 = f32[136,128]{1,0:T(8,128)S(1)} collective-permute-done((f32[136,128]{1,0:T(8,128)S(1)}, f32[136,128]{1,0:T(8,128)S(1)}, u32[]{:S(2)}, u32[]{:S(2)}) %collective-permute-start.11) | collective-permute-done | bytes 69664 | tf_op jit(solution)/shard_map/ppermute | solution.py:32
  69.5 0.7 maximum_multiply_fusion.g_ref
  70.2 12.8 %shard_map.41 = (f32[2,128,128]{2,1,0:T(8,128)}, f32[2,128,128]{2,1,0:T(8,128)}) custom-call(f32[2,128,128]{2,1,0:T(8,128)} %maximum_multiply_fusion.g_ref), custom_call_target="tpu_custom_call" | custom-call | tf_op jit(solution)/shard_map/pallas_call | solution.py:102
  83.0 6.0 %fusion.18 = f32[2,4096,128]{2,1,0:T(8,128)} fusion(f32[2,4096,128]{2,1,0:T(8,128)} %bitcast.36, f32[2,128,128]{2,1,0:T(8,128)} %get-tuple-element.4), kind=kOutput, calls=%fused_computation.39 | convolution fusion | flops 805306368 | bytes 8519680 | tf_op jit(solution)/shard_map/pcs,pts->pct/dot_general | solution.py:131
  (26 shorter events, 0.7 us)
Async XLA Ops:
  0.6 15.1 %copy-start.2 = (bf16[2,64,64,128]{3,2,1,0:T(8,128)(2,1)S(1)}, bf16[2,64,64,128]{3,2,1,0:T(8,128)(2,1)}, u32[]{:S(2)}) copy-start(bf16[2,64,64,128]{3,2,1,0:T(8,128)(2,1)} %param.3) | copy-start | bytes 6291460
  1.9 10.9 %collective-permute-start = (bf16[2,64,2,128]{3,2,1,0:T(2,128)(2,1)S(1)}, bf16[2,64,2,128]{3,2,1,0:T(2,128)(2,1)S(1)}, u32[]{:S(2)}, u32[]{:S(2)}) collective-permute-start(bf16[2,64,2,128]{3,2,1,0:T(2,128)(2,1)S(1)} %get-tuple-element.6), channel_id=1, source_target_pairs={{0,8},{8,16},{16,24},{24,32},{32,40},{40,48},{48,56},{56,64},{64,7... | collective-permute-start | bytes 196616 | tf_op jit(solution)/shard_map/ppermute | solution.py:18
  3.9 9.0 %collective-permute-start.1 = (bf16[2,64,2,128]{3,2,1,0:T(2,128)(2,1)S(1)}, bf16[2,64,2,128]{3,2,1,0:T(2,128)(2,1)S(1)}, u32[]{:S(2)}, u32[]{:S(2)}) collective-permute-start(bf16[2,64,2,128]{3,2,1,0:T(2,128)(2,1)S(1)} %get-tuple-element.7), channel_id=1, source_target_pairs={{8,0},{16,8},{24,16},{32,24},{40,32},{48,40},{56,48},{64,56},{72,6... | collective-permute-start | bytes 196616 | tf_op jit(solution)/shard_map/ppermute | solution.py:20
  11.0 4.6 %collective-permute-start.2 = (bf16[2,2,64,128]{3,2,1,0:T(8,128)(2,1)S(1)}, bf16[2,2,64,128]{3,2,1,0:T(8,128)(2,1)S(1)}, u32[]{:S(2)}, u32[]{:S(2)}) collective-permute-start(bf16[2,2,64,128]{3,2,1,0:T(8,128)(2,1)S(1)} %get-tuple-element.8), channel_id=1, source_target_pairs={{0,1},{1,2},{2,3},{3,4},{4,5},{5,6},{6,7},{7,0},{8,9},{9,10},{10,1... | collective-permute-start | bytes 196616 | tf_op jit(solution)/shard_map/ppermute | solution.py:18
  11.1 4.6 %collective-permute-start.3 = (bf16[2,2,64,128]{3,2,1,0:T(8,128)(2,1)S(1)}, bf16[2,2,64,128]{3,2,1,0:T(8,128)(2,1)S(1)}, u32[]{:S(2)}, u32[]{:S(2)}) collective-permute-start(bf16[2,2,64,128]{3,2,1,0:T(8,128)(2,1)S(1)} %get-tuple-element.9), channel_id=1, source_target_pairs={{1,0},{2,1},{3,2},{4,3},{5,4},{6,5},{7,6},{0,7},{9,8},{10,9},{11,1... | collective-permute-start | bytes 196616 | tf_op jit(solution)/shard_map/ppermute | solution.py:20
  18.8 2.0 %copy-start = (f32[2,64,64,128]{3,2,1,0:T(8,128)}, f32[2,64,64,128]{3,2,1,0:T(8,128)S(1)}, u32[]{:S(2)}) copy-start(f32[2,64,64,128]{3,2,1,0:T(8,128)S(1)} %fusion.3) | copy-start | bytes 12582916
  22.0 4.6 %copy-start.1 = (f32[2,64,64,128]{3,2,1,0:T(8,128)S(1)}, f32[2,64,64,128]{3,2,1,0:T(8,128)}, u32[]{:S(2)}) copy-start(f32[2,64,64,128]{3,2,1,0:T(8,128)} %copy-done) | copy-start | bytes 12582916
  27.9 1.7 %collective-permute-start.4 = (f32[136,128]{1,0:T(8,128)S(1)}, f32[136,128]{1,0:T(8,128)S(1)}, u32[]{:S(2)}, u32[]{:S(2)}) collective-permute-start(f32[136,128]{1,0:T(8,128)S(1)} %maximum_maximum_fusion), channel_id=1, source_target_pairs={{0,1},{1,0},{2,3},{3,2},{4,5},{5,4},{6,7},{7,6},{8,9},{9,8},{10,11... | collective-permute-start | bytes 208904 | tf_op jit(solution)/shard_map/ppermute | solution.py:32
  29.7 4.5 %collective-permute-start.5 = (f32[136,128]{1,0:T(8,128)S(1)}, f32[136,128]{1,0:T(8,128)S(1)}, u32[]{:S(2)}, u32[]{:S(2)}) collective-permute-start(f32[136,128]{1,0:T(8,128)S(1)} %fusion.15), channel_id=1, source_target_pairs={{0,2},{1,3},{2,0},{3,1},{4,6},{5,7},{6,4},{7,5},{8,10},{9,11},{10,... | collective-permute-start | bytes 208904 | tf_op jit(solution)/shard_map/ppermute | solution.py:32
  34.3 5.9 %collective-permute-start.6 = (f32[136,128]{1,0:T(8,128)S(1)}, f32[136,128]{1,0:T(8,128)S(1)}, u32[]{:S(2)}, u32[]{:S(2)}) collective-permute-start(f32[136,128]{1,0:T(8,128)S(1)} %add.37), channel_id=1, source_target_pairs={{0,4},{1,5},{2,6},{3,7},{4,0},{5,1},{6,2},{7,3},{8,12},{9,13},{10,... | collective-permute-start | bytes 208904 | tf_op jit(solution)/shard_map/ppermute | solution.py:32
  40.2 4.4 %collective-permute-start.7 = (f32[136,128]{1,0:T(8,128)S(1)}, f32[136,128]{1,0:T(8,128)S(1)}, u32[]{:S(2)}, u32[]{:S(2)}) collective-permute-start(f32[136,128]{1,0:T(8,128)S(1)} %add.38), channel_id=1, source_target_pairs={{0,8},{8,0},{16,24},{24,16},{32,40},{40,32},{48,56},{56,48},{64,72... | collective-permute-start | bytes 208904 | tf_op jit(solution)/shard_map/ppermute | solution.py:32
  44.6 5.6 %collective-permute-start.8 = (f32[136,128]{1,0:T(8,128)S(1)}, f32[136,128]{1,0:T(8,128)S(1)}, u32[]{:S(2)}, u32[]{:S(2)}) collective-permute-start(f32[136,128]{1,0:T(8,128)S(1)} %add.39), channel_id=1, source_target_pairs={{0,16},{8,24},{16,0},{24,8},{32,48},{40,56},{48,32},{56,40},{64,80... | collective-permute-start | bytes 208904 | tf_op jit(solution)/shard_map/ppermute | solution.py:32
  50.2 8.6 %collective-permute-start.9 = (f32[136,128]{1,0:T(8,128)S(1)}, f32[136,128]{1,0:T(8,128)S(1)}, u32[]{:S(2)}, u32[]{:S(2)}) collective-permute-start(f32[136,128]{1,0:T(8,128)S(1)} %add.40), channel_id=1, source_target_pairs={{0,32},{8,40},{16,48},{24,56},{32,0},{40,8},{48,16},{56,24},{64,96... | collective-permute-start | bytes 208904 | tf_op jit(solution)/shard_map/ppermute | solution.py:32
  58.8 4.4 %collective-permute-start.10 = (f32[136,128]{1,0:T(8,128)S(1)}, f32[136,128]{1,0:T(8,128)S(1)}, u32[]{:S(2)}, u32[]{:S(2)}) collective-permute-start(f32[136,128]{1,0:T(8,128)S(1)} %add.41), channel_id=1, source_target_pairs={{0,64},{8,72},{16,80},{24,88},{32,96},{40,104},{48,112},{56,120},{... | collective-permute-start | bytes 208904 | tf_op jit(solution)/shard_map/ppermute | solution.py:32
  63.2 6.1 %collective-permute-start.11 = (f32[136,128]{1,0:T(8,128)S(1)}, f32[136,128]{1,0:T(8,128)S(1)}, u32[]{:S(2)}, u32[]{:S(2)}) collective-permute-start(f32[136,128]{1,0:T(8,128)S(1)} %add.42), channel_id=1, source_target_pairs={{0,128},{8,136},{16,144},{24,152},{32,160},{40,168},{48,176},{56,1... | collective-permute-start | bytes 208904 | tf_op jit(solution)/shard_map/ppermute | solution.py:32

commit v6 on v5

--- a/solution.py
+++ b/solution.py
@@ -34,17 +34,26 @@
     return x
 
 
-def split_gram(columns):
-    head32 = lax.reduce_precision(columns, exponent_bits=8, mantissa_bits=7)
-    head = head32.astype(jnp.bfloat16)
-    tail = (columns - head32).astype(jnp.bfloat16)
+def split(values):
+    head32 = lax.reduce_precision(values, exponent_bits=8, mantissa_bits=7)
+    return head32.astype(jnp.bfloat16), (values - head32).astype(jnp.bfloat16)
 
+
+def split_gram(head, tail):
     def dot(a, b):
         return jnp.einsum("pcs,pct->pst", a, b, preferred_element_type=jnp.float32)
 
     cross = dot(head, tail)
     return dot(head, head) + (cross + jnp.swapaxes(cross, 1, 2)) + dot(tail, tail)
 
+
+def split_modes(head, tail, lower_inverse):
+    inv_head, inv_tail = split(lower_inverse)
+
+    def dot(a, b):
+        return jnp.einsum("pcs,pts->pct", a, b, preferred_element_type=jnp.float32)
+
+    return dot(head, inv_head) + (dot(head, inv_tail) + dot(tail, inv_head))
 
 def pack_pair(gram):
     n = gram.shape[-1]
@@ -120,7 +129,8 @@
     )
     vorticity = span_diff / (12.0 * span_step) - stream_diff / 12.0
     columns = vorticity.reshape(planes, rows_x * rows_z, snaps)
-    gram_local = split_gram(columns)
+    head, tail = lax.optimization_barrier(split(columns))
+    gram_local = split_gram(head, tail)
     if planes == 2:
         gram_sum = unpack_pair(butterfly_sum(pack_pair(gram_local), ("gx", "gz")))
     else:
@@ -128,13 +138,7 @@
     total_cells = rows_x * rows_z * lax.axis_size("gz") * lax.axis_size("gx")
     gram = gram_sum / total_cells
     factor_r, lower_inverse = chol_inv(gram)
-    modes = jnp.einsum(
-        "pcs,pts->pct",
-        columns,
-        lower_inverse,
-        precision=lax.Precision.HIGH,
-        preferred_element_type=jnp.float32,
-    )
+    modes = split_modes(head, tail, lower_inverse)
     modes = modes.reshape(planes, rows_x, rows_z, snaps)
     return (modes, factor_r)
 

time: 89.2 us -> 85.5 us (0.959)
  matrix products: 12.7 us -> 7.44 us
    dot_general x3, matrix products: 6.73 us -> 2.34 us  [dot(): return jnp.einsum('pcs,pct->pst', a, b, preferred_element_type=jnp.float32)]
    dot_general x1 -> x3, matrix products: 6 us -> 5.11 us  [dot(): return jnp.einsum('pcs,pts->pct', a, b, preferred_element_type=jnp.float32)]
    unnamed x6 -> x10, local copies, waits for them, and re-layouts: 2.12 us -> 3 us
where the time goes in v6:
time: 85.5 us; the launch traced here: 85.2 us
  waiting for transfers between devices  32.7 us (38%)
  starting transfers between devices  18.4 us (22%)
  Pallas kernels  12.8 us (15%)
  other arithmetic  7.56 us (9%)
  matrix products  7.44 us (9%)
  local copies, waits for them, and re-layouts  5.45 us (6%)
  between operations  0.86 us (1%)
    ppermute x8, waiting for transfers between devices, butterfly_sum(): x = x + lax.ppermute(x, axis, [(i, i ^ step) for i in range(count)])  32.7 us
    pallas_call x1, Pallas kernels, chol_inv(): pl.pallas_call(chol_inv_kernel, out_shape=(jax.ShapeDtypeStruct(gram.shap...  12.8 us
    ppermute x8, starting transfers between devices, butterfly_sum(): x = x + lax.ppermute(x, axis, [(i, i ^ step) for i in range(count)])  8.48 us
    ppermute x2, starting transfers between devices, with_halo(): lax.ppermute(head, axis, [((i + 1) % count, i) for i in range(count)])  7.96 us
    dot_general x3, matrix products, dot(): return jnp.einsum('pcs,pts->pct', a, b, preferred_element_type=jnp.float32)  5.11 us
    unnamed x10, local copies, waits for them, and re-layouts  3 us
    convert_element_type x1, other arithmetic, local(): padded_u = with_halo(u_field, (('gz', 2),), 2).astype(jnp.float32)  2.78 us
    sub x1, other arithmetic, local(): vorticity = span_diff / (12.0 * span_step) - stream_diff / 12.0  2.77 us
  transfers between devices with their start and end apart: 12, of which 8 were waited for; matrix products, arithmetic and copies ran while one was open for 4% of the time, Pallas kernels for 0%

profile of v6, /device:TPU:8, one launch (start us, length us, event | category | flops | bytes accessed | tf_op | source)
XLA Modules:
  0.0 85.2 jit_solution(6248389174605822164)
XLA Ops:
  0.6 1.3 %fusion.18 = (bf16[2,64,2,128]{3,2,1,0:T(2,128)(2,1)S(1)}, bf16[2,64,2,128]{3,2,1,0:T(2,128)(2,1)S(1)}) fusion(bf16[2,64,64,128]{3,2,1,0:T(8,128)(2,1)} %param.2), kind=kLoop, calls=%fused_computation.43 | loop fusion | bytes 262144 | tf_op jit(solution)/shard_map/slice | solution.py:15
  1.9 2.0 %collective-permute-start = (bf16[2,64,2,128]{3,2,1,0:T(2,128)(2,1)S(1)}, bf16[2,64,2,128]{3,2,1,0:T(2,128)(2,1)S(1)}, u32[]{:S(2)}, u32[]{:S(2)}) collective-permute-start(bf16[2,64,2,128]{3,2,1,0:T(2,128)(2,1)S(1)} %get-tuple-element.12), channel_id=1, source_target_pairs={{0,8},{8,16},{16,24},{24,32},{32,40},{40,48},{48,56},{56,64},{64,7... | collective-permute-start | bytes 196616 | tf_op jit(solution)/shard_map/ppermute | solution.py:18
  3.9 6.2 %collective-permute-start.1 = (bf16[2,64,2,128]{3,2,1,0:T(2,128)(2,1)S(1)}, bf16[2,64,2,128]{3,2,1,0:T(2,128)(2,1)S(1)}, u32[]{:S(2)}, u32[]{:S(2)}) collective-permute-start(bf16[2,64,2,128]{3,2,1,0:T(2,128)(2,1)S(1)} %get-tuple-element.13), channel_id=1, source_target_pairs={{8,0},{16,8},{24,16},{32,24},{40,32},{48,40},{56,48},{64,56},{72,6... | collective-permute-start | bytes 196616 | tf_op jit(solution)/shard_map/ppermute | solution.py:20
  10.2 0.9 %fusion.19 = (bf16[2,2,64,128]{3,2,1,0:T(8,128)(2,1)S(1)}, bf16[2,2,64,128]{3,2,1,0:T(8,128)(2,1)S(1)}) fusion(bf16[2,64,64,128]{3,2,1,0:T(8,128)(2,1)} %param.3), kind=kLoop, calls=%fused_computation.44 | loop fusion | bytes 262144 | tf_op jit(solution)/shard_map/slice | solution.py:15
  11.1 1.7 %collective-permute-start.3 = (bf16[2,2,64,128]{3,2,1,0:T(8,128)(2,1)S(1)}, bf16[2,2,64,128]{3,2,1,0:T(8,128)(2,1)S(1)}, u32[]{:S(2)}, u32[]{:S(2)}) collective-permute-start(bf16[2,2,64,128]{3,2,1,0:T(8,128)(2,1)S(1)} %get-tuple-element.15), channel_id=1, source_target_pairs={{1,0},{2,1},{3,2},{4,3},{5,4},{6,5},{7,6},{0,7},{9,8},{10,9},{11,1... | collective-permute-start | bytes 196616 | tf_op jit(solution)/shard_map/ppermute | solution.py:20
  12.9 2.8 %maximum_convert_fusion = f32[2,64,68,128]{3,2,1,0:T(8,128)S(1)} fusion(bf16[2,64,2,128]{3,2,1,0:T(2,128)(2,1)S(1)} %collective-permute-done.1, bf16[2,64,64,128]{3,2,1,0:T(8,128)(2,1)} %param.2, bf16[2,64,2,128]{3,2,1,0:T(2,128)(2,1)S(1)} %collective-permute-done), kind=kLoop, calls=%fused_computation.16 | loop fusion | flops 6684672 | bytes 6684672 | tf_op jit(solution)/shard_map/convert_element_type | solution.py:122
  16.0 2.8 %fusion.4 = f32[2,64,64,128]{3,2,1,0:T(8,128)S(1)} fusion(f32[2,68,64,128]{3,2,1,0:T(8,128)S(1)} %maximum_convert_fusion.1, f32[2,64,68,128]{3,2,1,0:T(8,128)S(1)} %maximum_convert_fusion), kind=kLoop, calls=%fused_computation.8 | loop fusion | flops 11534336 | bytes 37748736 | tf_op jit(solution)/shard_map/sub | solution.py:130
  18.8 0.7 fusion.1
  19.5 1.3 %copy-done = bf16[2,4096,128]{2,1,0:T(8,128)(2,1)} copy-done((bf16[2,4096,128]{2,1,0:T(8,128)(2,1)}, bf16[2,4096,128]{2,1,0:T(8,128)(2,1)S(1)}, u32[]{:S(2)}) %copy-start) | copy-done | bytes 2097176
  20.8 0.8 fusion.20
  21.7 0.8 convolution_add_fusion.2
  22.5 0.8 copy-done.1
  23.3 0.8 convolution_add_fusion.1
  24.2 0.8 collective-permute-start.4
  25.0 0.9 %collective-permute-done.4 = f32[136,128]{1,0:T(8,128)S(1)} collective-permute-done((f32[136,128]{1,0:T(8,128)S(1)}, f32[136,128]{1,0:T(8,128)S(1)}, u32[]{:S(2)}, u32[]{:S(2)}) %collective-permute-start.4) | collective-permute-done | bytes 69664 | tf_op jit(solution)/shard_map/ppermute | solution.py:32
  26.0 1.4 %collective-permute-start.5 = (f32[136,128]{1,0:T(8,128)S(1)}, f32[136,128]{1,0:T(8,128)S(1)}, u32[]{:S(2)}, u32[]{:S(2)}) collective-permute-start(f32[136,128]{1,0:T(8,128)S(1)} %fusion.17), channel_id=1, source_target_pairs={{0,2},{1,3},{2,0},{3,1},{4,6},{5,7},{6,4},{7,5},{8,10},{9,11},{10,... | collective-permute-start | bytes 208904 | tf_op jit(solution)/shard_map/ppermute | solution.py:32
  27.4 3.2 %collective-permute-done.5 = f32[136,128]{1,0:T(8,128)S(1)} collective-permute-done((f32[136,128]{1,0:T(8,128)S(1)}, f32[136,128]{1,0:T(8,128)S(1)}, u32[]{:S(2)}, u32[]{:S(2)}) %collective-permute-start.5) | collective-permute-done | bytes 69664 | tf_op jit(solution)/shard_map/ppermute | solution.py:32
  30.6 2.2 %collective-permute-start.6 = (f32[136,128]{1,0:T(8,128)S(1)}, f32[136,128]{1,0:T(8,128)S(1)}, u32[]{:S(2)}, u32[]{:S(2)}) collective-permute-start(f32[136,128]{1,0:T(8,128)S(1)} %add.43), channel_id=1, source_target_pairs={{0,4},{1,5},{2,6},{3,7},{4,0},{5,1},{6,2},{7,3},{8,12},{9,13},{10,... | collective-permute-start | bytes 208904 | tf_op jit(solution)/shard_map/ppermute | solution.py:32
  32.8 3.7 %collective-permute-done.6 = f32[136,128]{1,0:T(8,128)S(1)} collective-permute-done((f32[136,128]{1,0:T(8,128)S(1)}, f32[136,128]{1,0:T(8,128)S(1)}, u32[]{:S(2)}, u32[]{:S(2)}) %collective-permute-start.6) | collective-permute-done | bytes 69664 | tf_op jit(solution)/shard_map/ppermute | solution.py:32
  36.6 4.3 %collective-permute-done.7 = f32[136,128]{1,0:T(8,128)S(1)} collective-permute-done((f32[136,128]{1,0:T(8,128)S(1)}, f32[136,128]{1,0:T(8,128)S(1)}, u32[]{:S(2)}, u32[]{:S(2)}) %collective-permute-start.7) | collective-permute-done | bytes 69664 | tf_op jit(solution)/shard_map/ppermute | solution.py:32
  41.4 5.1 %collective-permute-done.8 = f32[136,128]{1,0:T(8,128)S(1)} collective-permute-done((f32[136,128]{1,0:T(8,128)S(1)}, f32[136,128]{1,0:T(8,128)S(1)}, u32[]{:S(2)}, u32[]{:S(2)}) %collective-permute-start.8) | collective-permute-done | bytes 69664 | tf_op jit(solution)/shard_map/ppermute | solution.py:32
  46.5 2.3 %collective-permute-start.9 = (f32[136,128]{1,0:T(8,128)S(1)}, f32[136,128]{1,0:T(8,128)S(1)}, u32[]{:S(2)}, u32[]{:S(2)}) collective-permute-start(f32[136,128]{1,0:T(8,128)S(1)} %add.46), channel_id=1, source_target_pairs={{0,32},{8,40},{16,48},{24,56},{32,0},{40,8},{48,16},{56,24},{64,96... | collective-permute-start | bytes 208904 | tf_op jit(solution)/shard_map/ppermute | solution.py:32
  48.7 6.3 %collective-permute-done.9 = f32[136,128]{1,0:T(8,128)S(1)} collective-permute-done((f32[136,128]{1,0:T(8,128)S(1)}, f32[136,128]{1,0:T(8,128)S(1)}, u32[]{:S(2)}, u32[]{:S(2)}) %collective-permute-start.9) | collective-permute-done | bytes 69664 | tf_op jit(solution)/shard_map/ppermute | solution.py:32
  55.2 4.3 %collective-permute-done.10 = f32[136,128]{1,0:T(8,128)S(1)} collective-permute-done((f32[136,128]{1,0:T(8,128)S(1)}, f32[136,128]{1,0:T(8,128)S(1)}, u32[]{:S(2)}, u32[]{:S(2)}) %collective-permute-start.10) | collective-permute-done | bytes 69664 | tf_op jit(solution)/shard_map/ppermute | solution.py:32
  59.5 1.1 %collective-permute-start.11 = (f32[136,128]{1,0:T(8,128)S(1)}, f32[136,128]{1,0:T(8,128)S(1)}, u32[]{:S(2)}, u32[]{:S(2)}) collective-permute-start(f32[136,128]{1,0:T(8,128)S(1)} %add.48), channel_id=1, source_target_pairs={{0,128},{8,136},{16,144},{24,152},{32,160},{40,168},{48,176},{56,1... | collective-permute-start | bytes 208904 | tf_op jit(solution)/shard_map/ppermute | solution.py:32
  60.6 5.0 %collective-permute-done.11 = f32[136,128]{1,0:T(8,128)S(1)} collective-permute-done((f32[136,128]{1,0:T(8,128)S(1)}, f32[136,128]{1,0:T(8,128)S(1)}, u32[]{:S(2)}, u32[]{:S(2)}) %collective-permute-start.11) | collective-permute-done | bytes 69664 | tf_op jit(solution)/shard_map/ppermute | solution.py:32
  65.8 0.7 maximum_multiply_fusion.g_ref
  66.5 12.8 %shard_map.41 = (f32[2,128,128]{2,1,0:T(8,128)}, f32[2,128,128]{2,1,0:T(8,128)}) custom-call(f32[2,128,128]{2,1,0:T(8,128)} %maximum_multiply_fusion.g_ref), custom_call_target="tpu_custom_call" | custom-call | tf_op jit(solution)/shard_map/pallas_call | solution.py:111
  79.2 1.7 %fusion.10 = f32[2,4096,128]{2,1,0:T(8,128)S(1)} fusion(bf16[2,4096,128]{2,1,0:T(8,128)(2,1)S(1)} %get-tuple-element.6, f32[2,128,128]{2,1,0:T(8,128)} %get-tuple-element.8), kind=kOutput, calls=%fused_computation.26 | convolution fusion | flops 268533760 | bytes 6422528 | tf_op jit(solution)/shard_map/pcs,pts->pct/dot_general | solution.py:54
  80.9 0.7 fusion.16
  81.7 0.9 %copy-done.2 = bf16[2,4096,128]{2,1,0:T(8,128)(2,1)S(1)} copy-done((bf16[2,4096,128]{2,1,0:T(8,128)(2,1)S(1)}, bf16[2,4096,128]{2,1,0:T(8,128)(2,1)}, u32[]{:S(2)}) %copy-start.2) | copy-done | bytes 2097176
  82.5 2.7 %fusion = f32[2,4096,128]{2,1,0:T(8,128)} fusion(f32[2,4096,128]{2,1,0:T(8,128)S(1)} %fusion.16, f32[2,4096,128]{2,1,0:T(8,128)S(1)} %fusion.10, bf16[2,4096,128]{2,1,0:T(8,128)(2,1)S(1)} %copy-done.2, f32[2,128,128]{2,1,0:T(8,128)S(1)} %copy-done.4), kind=kOutput, calls=%fused_computation.3 | convolution fusion | flops 270598144 | bytes 14811136 | tf_op jit(solution)/shard_map/pcs,pts->pct/dot_general | solution.py:54
  (33 shorter events, 1.7 us)
Async XLA Ops:
  0.6 15.1 %copy-start.3 = (bf16[2,64,64,128]{3,2,1,0:T(8,128)(2,1)S(1)}, bf16[2,64,64,128]{3,2,1,0:T(8,128)(2,1)}, u32[]{:S(2)}) copy-start(bf16[2,64,64,128]{3,2,1,0:T(8,128)(2,1)} %param.3) | copy-start | bytes 6291460
  1.9 10.9 %collective-permute-start = (bf16[2,64,2,128]{3,2,1,0:T(2,128)(2,1)S(1)}, bf16[2,64,2,128]{3,2,1,0:T(2,128)(2,1)S(1)}, u32[]{:S(2)}, u32[]{:S(2)}) collective-permute-start(bf16[2,64,2,128]{3,2,1,0:T(2,128)(2,1)S(1)} %get-tuple-element.12), channel_id=1, source_target_pairs={{0,8},{8,16},{16,24},{24,32},{32,40},{40,48},{48,56},{56,64},{64,7... | collective-permute-start | bytes 196616 | tf_op jit(solution)/shard_map/ppermute | solution.py:18
  3.9 9.0 %collective-permute-start.1 = (bf16[2,64,2,128]{3,2,1,0:T(2,128)(2,1)S(1)}, bf16[2,64,2,128]{3,2,1,0:T(2,128)(2,1)S(1)}, u32[]{:S(2)}, u32[]{:S(2)}) collective-permute-start(bf16[2,64,2,128]{3,2,1,0:T(2,128)(2,1)S(1)} %get-tuple-element.13), channel_id=1, source_target_pairs={{8,0},{16,8},{24,16},{32,24},{40,32},{48,40},{56,48},{64,56},{72,6... | collective-permute-start | bytes 196616 | tf_op jit(solution)/shard_map/ppermute | solution.py:20
  11.0 4.6 %collective-permute-start.2 = (bf16[2,2,64,128]{3,2,1,0:T(8,128)(2,1)S(1)}, bf16[2,2,64,128]{3,2,1,0:T(8,128)(2,1)S(1)}, u32[]{:S(2)}, u32[]{:S(2)}) collective-permute-start(bf16[2,2,64,128]{3,2,1,0:T(8,128)(2,1)S(1)} %get-tuple-element.14), channel_id=1, source_target_pairs={{0,1},{1,2},{2,3},{3,4},{4,5},{5,6},{6,7},{7,0},{8,9},{9,10},{10,1... | collective-permute-start | bytes 196616 | tf_op jit(solution)/shard_map/ppermute | solution.py:18
  11.1 4.6 %collective-permute-start.3 = (bf16[2,2,64,128]{3,2,1,0:T(8,128)(2,1)S(1)}, bf16[2,2,64,128]{3,2,1,0:T(8,128)(2,1)S(1)}, u32[]{:S(2)}, u32[]{:S(2)}) collective-permute-start(bf16[2,2,64,128]{3,2,1,0:T(8,128)(2,1)S(1)} %get-tuple-element.15), channel_id=1, source_target_pairs={{1,0},{2,1},{3,2},{4,3},{5,4},{6,5},{7,6},{0,7},{9,8},{10,9},{11,1... | collective-permute-start | bytes 196616 | tf_op jit(solution)/shard_map/ppermute | solution.py:20
  19.5 1.3 %copy-start = (bf16[2,4096,128]{2,1,0:T(8,128)(2,1)}, bf16[2,4096,128]{2,1,0:T(8,128)(2,1)S(1)}, u32[]{:S(2)}) copy-start(bf16[2,4096,128]{2,1,0:T(8,128)(2,1)S(1)} %get-tuple-element.7) | copy-start | bytes 6291460
  21.7 1.6 %copy-start.1 = (bf16[2,4096,128]{2,1,0:T(8,128)(2,1)S(1)}, bf16[2,4096,128]{2,1,0:T(8,128)(2,1)}, u32[]{:S(2)}) copy-start(bf16[2,4096,128]{2,1,0:T(8,128)(2,1)} %copy-done) | copy-start | bytes 6291460
  24.2 1.7 %collective-permute-start.4 = (f32[136,128]{1,0:T(8,128)S(1)}, f32[136,128]{1,0:T(8,128)S(1)}, u32[]{:S(2)}, u32[]{:S(2)}) collective-permute-start(f32[136,128]{1,0:T(8,128)S(1)} %maximum_maximum_fusion), channel_id=1, source_target_pairs={{0,1},{1,0},{2,3},{3,2},{4,5},{5,4},{6,7},{7,6},{8,9},{9,8},{10,11... | collective-permute-start | bytes 208904 | tf_op jit(solution)/shard_map/ppermute | solution.py:32
  26.0 4.5 %collective-permute-start.5 = (f32[136,128]{1,0:T(8,128)S(1)}, f32[136,128]{1,0:T(8,128)S(1)}, u32[]{:S(2)}, u32[]{:S(2)}) collective-permute-start(f32[136,128]{1,0:T(8,128)S(1)} %fusion.17), channel_id=1, source_target_pairs={{0,2},{1,3},{2,0},{3,1},{4,6},{5,7},{6,4},{7,5},{8,10},{9,11},{10,... | collective-permute-start | bytes 208904 | tf_op jit(solution)/shard_map/ppermute | solution.py:32
  30.6 5.9 %collective-permute-start.6 = (f32[136,128]{1,0:T(8,128)S(1)}, f32[136,128]{1,0:T(8,128)S(1)}, u32[]{:S(2)}, u32[]{:S(2)}) collective-permute-start(f32[136,128]{1,0:T(8,128)S(1)} %add.43), channel_id=1, source_target_pairs={{0,4},{1,5},{2,6},{3,7},{4,0},{5,1},{6,2},{7,3},{8,12},{9,13},{10,... | collective-permute-start | bytes 208904 | tf_op jit(solution)/shard_map/ppermute | solution.py:32
  36.5 4.4 %collective-permute-start.7 = (f32[136,128]{1,0:T(8,128)S(1)}, f32[136,128]{1,0:T(8,128)S(1)}, u32[]{:S(2)}, u32[]{:S(2)}) collective-permute-start(f32[136,128]{1,0:T(8,128)S(1)} %add.44), channel_id=1, source_target_pairs={{0,8},{8,0},{16,24},{24,16},{32,40},{40,32},{48,56},{56,48},{64,72... | collective-permute-start | bytes 208904 | tf_op jit(solution)/shard_map/ppermute | solution.py:32
  40.9 5.6 %collective-permute-start.8 = (f32[136,128]{1,0:T(8,128)S(1)}, f32[136,128]{1,0:T(8,128)S(1)}, u32[]{:S(2)}, u32[]{:S(2)}) collective-permute-start(f32[136,128]{1,0:T(8,128)S(1)} %add.45), channel_id=1, source_target_pairs={{0,16},{8,24},{16,0},{24,8},{32,48},{40,56},{48,32},{56,40},{64,80... | collective-permute-start | bytes 208904 | tf_op jit(solution)/shard_map/ppermute | solution.py:32
  46.5 8.6 %collective-permute-start.9 = (f32[136,128]{1,0:T(8,128)S(1)}, f32[136,128]{1,0:T(8,128)S(1)}, u32[]{:S(2)}, u32[]{:S(2)}) collective-permute-start(f32[136,128]{1,0:T(8,128)S(1)} %add.46), channel_id=1, source_target_pairs={{0,32},{8,40},{16,48},{24,56},{32,0},{40,8},{48,16},{56,24},{64,96... | collective-permute-start | bytes 208904 | tf_op jit(solution)/shard_map/ppermute | solution.py:32
  55.1 4.4 %collective-permute-start.10 = (f32[136,128]{1,0:T(8,128)S(1)}, f32[136,128]{1,0:T(8,128)S(1)}, u32[]{:S(2)}, u32[]{:S(2)}) collective-permute-start(f32[136,128]{1,0:T(8,128)S(1)} %add.47), channel_id=1, source_target_pairs={{0,64},{8,72},{16,80},{24,88},{32,96},{40,104},{48,112},{56,120},{... | collective-permute-start | bytes 208904 | tf_op jit(solution)/shard_map/ppermute | solution.py:32
  59.5 6.1 %collective-permute-start.11 = (f32[136,128]{1,0:T(8,128)S(1)}, f32[136,128]{1,0:T(8,128)S(1)}, u32[]{:S(2)}, u32[]{:S(2)}) collective-permute-start(f32[136,128]{1,0:T(8,128)S(1)} %add.48), channel_id=1, source_target_pairs={{0,128},{8,136},{16,144},{24,152},{32,160},{40,168},{48,176},{56,1... | collective-permute-start | bytes 208904 | tf_op jit(solution)/shard_map/ppermute | solution.py:32
  79.2 1.7 %copy-start.4 = (f32[2,128,128]{2,1,0:T(8,128)S(1)}, f32[2,128,128]{2,1,0:T(8,128)}, u32[]{:S(2)}) copy-start(f32[2,128,128]{2,1,0:T(8,128)} %get-tuple-element.8) | copy-start | bytes 393220
  80.9 1.6 %copy-start.2 = (bf16[2,4096,128]{2,1,0:T(8,128)(2,1)S(1)}, bf16[2,4096,128]{2,1,0:T(8,128)(2,1)}, u32[]{:S(2)}) copy-start(bf16[2,4096,128]{2,1,0:T(8,128)(2,1)} %copy-done) | copy-start | bytes 6291460

commit v7 on v6

--- a/solution.py
+++ b/solution.py
@@ -47,13 +47,10 @@
     return dot(head, head) + (cross + jnp.swapaxes(cross, 1, 2)) + dot(tail, tail)
 
 
-def split_modes(head, tail, lower_inverse):
+def split_modes(stacked, lower_inverse):
     inv_head, inv_tail = split(lower_inverse)
-
-    def dot(a, b):
-        return jnp.einsum("pcs,pts->pct", a, b, preferred_element_type=jnp.float32)
-
-    return dot(head, inv_head) + (dot(head, inv_tail) + dot(tail, inv_head))
+    weights = jnp.concatenate([inv_head, inv_head, inv_tail], axis=2)
+    return jnp.einsum("pcs,pts->pct", stacked, weights, preferred_element_type=jnp.float32)
 
 def pack_pair(gram):
     n = gram.shape[-1]
@@ -129,8 +126,9 @@
     )
     vorticity = span_diff / (12.0 * span_step) - stream_diff / 12.0
     columns = vorticity.reshape(planes, rows_x * rows_z, snaps)
-    head, tail = lax.optimization_barrier(split(columns))
-    gram_local = split_gram(head, tail)
+    head, tail = split(columns)
+    stacked = lax.optimization_barrier(jnp.concatenate([head, tail, head], axis=2))
+    gram_local = split_gram(stacked[..., :snaps], stacked[..., snaps:2 * snaps])
     if planes == 2:
         gram_sum = unpack_pair(butterfly_sum(pack_pair(gram_local), ("gx", "gz")))
     else:
@@ -138,7 +136,7 @@
     total_cells = rows_x * rows_z * lax.axis_size("gz") * lax.axis_size("gx")
     gram = gram_sum / total_cells
     factor_r, lower_inverse = chol_inv(gram)
-    modes = split_modes(head, tail, lower_inverse)
+    modes = split_modes(stacked, lower_inverse)
     modes = modes.reshape(planes, rows_x, rows_z, snaps)
     return (modes, factor_r)
 

time: 85.5 us -> 89.9 us (1.051)
  matrix products: 7.44 us -> 11.2 us
  other arithmetic: 7.56 us -> 9.38 us
  local copies, waits for them, and re-layouts: 5.45 us -> 4.3 us
    dot_general x3, matrix products: 2.34 us -> 4.57 us  [dot(): return jnp.einsum('pcs,pct->pst', a, b, preferred_element_type=jnp.float32)]
    dot_general x3 -> x1, matrix products: 5.11 us -> 6.6 us  [split_modes(): jnp.einsum('pcs,pts->pct', stacked, weights, preferred_element_type=jnp.f...]
    unnamed x10 -> x4, local copies, waits for them, and re-layouts: 3 us -> 1.85 us
    convert_element_type x1 -> x2, other arithmetic: 0.65 us -> 1.58 us  [split(): return (head32.astype(jnp.bfloat16), (values - head32).astype(jnp.bfloat16))]
where the time goes in v7:
time: 89.9 us; the launch traced here: 89.6 us
  waiting for transfers between devices  33 us (37%)
  starting transfers between devices  18.1 us (20%)
  Pallas kernels  12.8 us (14%)
  matrix products  11.2 us (12%)
  other arithmetic  9.38 us (10%)
  local copies, waits for them, and re-layouts  4.3 us (5%)
    ppermute x8, waiting for transfers between devices, butterfly_sum(): x = x + lax.ppermute(x, axis, [(i, i ^ step) for i in range(count)])  33 us
    pallas_call x1, Pallas kernels, chol_inv(): pl.pallas_call(chol_inv_kernel, out_shape=(jax.ShapeDtypeStruct(gram.shap...  12.8 us
    ppermute x8, starting transfers between devices, butterfly_sum(): x = x + lax.ppermute(x, axis, [(i, i ^ step) for i in range(count)])  8.15 us
    ppermute x2, starting transfers between devices, with_halo(): lax.ppermute(head, axis, [((i + 1) % count, i) for i in range(count)])  7.96 us
    dot_general x1, matrix products, split_modes(): jnp.einsum('pcs,pts->pct', stacked, weights, preferred_element_type=jnp.f...  6.6 us
    dot_general x3, matrix products, dot(): return jnp.einsum('pcs,pct->pst', a, b, preferred_element_type=jnp.float32)  4.57 us
    convert_element_type x1, other arithmetic, local(): padded_u = with_halo(u_field, (('gz', 2),), 2).astype(jnp.float32)  2.78 us
    sub x1, other arithmetic, local(): vorticity = span_diff / (12.0 * span_step) - stream_diff / 12.0  2.77 us
  transfers between devices with their start and end apart: 12, of which 8 were waited for; matrix products, arithmetic and copies ran while one was open for 4% of the time, Pallas kernels for 0%

profile of v7, /device:TPU:8, one launch (start us, length us, event | category | flops | bytes accessed | tf_op | source)
XLA Modules:
  0.0 89.6 jit_solution(4958006087193108688)
XLA Ops:
  0.6 1.3 %fusion.34 = (bf16[2,64,2,128]{3,2,1,0:T(2,128)(2,1)S(1)}, bf16[2,64,2,128]{3,2,1,0:T(2,128)(2,1)S(1)}) fusion(bf16[2,64,64,128]{3,2,1,0:T(8,128)(2,1)} %param.2), kind=kLoop, calls=%fused_computation.54 | loop fusion | bytes 262144 | tf_op jit(solution)/shard_map/slice | solution.py:15
  1.9 2.0 %collective-permute-start = (bf16[2,64,2,128]{3,2,1,0:T(2,128)(2,1)S(1)}, bf16[2,64,2,128]{3,2,1,0:T(2,128)(2,1)S(1)}, u32[]{:S(2)}, u32[]{:S(2)}) collective-permute-start(bf16[2,64,2,128]{3,2,1,0:T(2,128)(2,1)S(1)} %get-tuple-element.8), channel_id=1, source_target_pairs={{0,8},{8,16},{16,24},{24,32},{32,40},{40,48},{48,56},{56,64},{64,7... | collective-permute-start | bytes 196616 | tf_op jit(solution)/shard_map/ppermute | solution.py:18
  3.9 6.2 %collective-permute-start.1 = (bf16[2,64,2,128]{3,2,1,0:T(2,128)(2,1)S(1)}, bf16[2,64,2,128]{3,2,1,0:T(2,128)(2,1)S(1)}, u32[]{:S(2)}, u32[]{:S(2)}) collective-permute-start(bf16[2,64,2,128]{3,2,1,0:T(2,128)(2,1)S(1)} %get-tuple-element.9), channel_id=1, source_target_pairs={{8,0},{16,8},{24,16},{32,24},{40,32},{48,40},{56,48},{64,56},{72,6... | collective-permute-start | bytes 196616 | tf_op jit(solution)/shard_map/ppermute | solution.py:20
  10.2 0.9 fusion.35
  11.1 1.7 %collective-permute-start.3 = (bf16[2,2,64,128]{3,2,1,0:T(8,128)(2,1)S(1)}, bf16[2,2,64,128]{3,2,1,0:T(8,128)(2,1)S(1)}, u32[]{:S(2)}, u32[]{:S(2)}) collective-permute-start(bf16[2,2,64,128]{3,2,1,0:T(8,128)(2,1)S(1)} %get-tuple-element.11), channel_id=1, source_target_pairs={{1,0},{2,1},{3,2},{4,3},{5,4},{6,5},{7,6},{0,7},{9,8},{10,9},{11,1... | collective-permute-start | bytes 196616 | tf_op jit(solution)/shard_map/ppermute | solution.py:20
  12.9 2.8 %maximum_convert_fusion = f32[2,64,68,128]{3,2,1,0:T(8,128)S(1)} fusion(bf16[2,64,2,128]{3,2,1,0:T(2,128)(2,1)S(1)} %collective-permute-done.1, bf16[2,64,64,128]{3,2,1,0:T(8,128)(2,1)} %param.2, bf16[2,64,2,128]{3,2,1,0:T(2,128)(2,1)S(1)} %collective-permute-done), kind=kLoop, calls=%fused_computation.15 | loop fusion | flops 6684672 | bytes 6684672 | tf_op jit(solution)/shard_map/convert_element_type | solution.py:119
  15.7 0.3 maximum_convert_fusion.1
  16.0 2.8 %fusion.3 = f32[2,64,64,128]{3,2,1,0:T(8,128)S(1)} fusion(f32[2,68,64,128]{3,2,1,0:T(8,128)S(1)} %maximum_convert_fusion.1, f32[2,64,68,128]{3,2,1,0:T(8,128)S(1)} %maximum_convert_fusion), kind=kLoop, calls=%fused_computation.7 | loop fusion | flops 11534336 | bytes 37748736 | tf_op jit(solution)/shard_map/sub | solution.py:127
  18.8 0.7 fusion
  19.5 0.9 pad_maximum_fusion
  20.4 0.8 fusion.10
  21.2 1.8 %copy-done = bf16[2,4096,384]{2,1,0:T(8,128)(2,1)} copy-done((bf16[2,4096,384]{2,1,0:T(8,128)(2,1)}, bf16[2,4096,384]{2,1,0:T(8,128)(2,1)S(1)}, u32[]{:S(2)}) %copy-start) | copy-done | bytes 6291480
  23.0 0.8 fusion.8
  23.9 3.0 %fusion.18 = f32[2,128,128]{2,1,0:T(8,128)S(1)} fusion(f32[2,128,128]{2,1,0:T(8,128)S(1)} %fusion.8, bf16[2,4096,384]{2,1,0:T(8,128)(2,1)} %copy-done, f32[2,128,128]{2,1,0:T(8,128)S(1)} %fusion.10, f32[2,128,128]{1,2,0:T(8,128)S(1)} %copy.6), kind=kOutput, calls=%fused_computation.25 | convolution fusion | flops 268533760 | bytes 2621440 | tf_op jit(solution)/shard_map/pcs,pct->pst/dot_general | solution.py:44
  27.0 0.8 collective-permute-start.4
  27.9 0.9 %collective-permute-done.4 = f32[136,128]{1,0:T(8,128)S(1)} collective-permute-done((f32[136,128]{1,0:T(8,128)S(1)}, f32[136,128]{1,0:T(8,128)S(1)}, u32[]{:S(2)}, u32[]{:S(2)}) %collective-permute-start.4) | collective-permute-done | bytes 69664 | tf_op jit(solution)/shard_map/ppermute | solution.py:32
  28.9 1.4 %collective-permute-start.5 = (f32[136,128]{1,0:T(8,128)S(1)}, f32[136,128]{1,0:T(8,128)S(1)}, u32[]{:S(2)}, u32[]{:S(2)}) collective-permute-start(f32[136,128]{1,0:T(8,128)S(1)} %fusion.33), channel_id=1, source_target_pairs={{0,2},{1,3},{2,0},{3,1},{4,6},{5,7},{6,4},{7,5},{8,10},{9,11},{10,... | collective-permute-start | bytes 208904 | tf_op jit(solution)/shard_map/ppermute | solution.py:32
  30.2 3.2 %collective-permute-done.5 = f32[136,128]{1,0:T(8,128)S(1)} collective-permute-done((f32[136,128]{1,0:T(8,128)S(1)}, f32[136,128]{1,0:T(8,128)S(1)}, u32[]{:S(2)}, u32[]{:S(2)}) %collective-permute-start.5) | collective-permute-done | bytes 69664 | tf_op jit(solution)/shard_map/ppermute | solution.py:32
  33.4 2.2 %collective-permute-start.6 = (f32[136,128]{1,0:T(8,128)S(1)}, f32[136,128]{1,0:T(8,128)S(1)}, u32[]{:S(2)}, u32[]{:S(2)}) collective-permute-start(f32[136,128]{1,0:T(8,128)S(1)} %add.37), channel_id=1, source_target_pairs={{0,4},{1,5},{2,6},{3,7},{4,0},{5,1},{6,2},{7,3},{8,12},{9,13},{10,... | collective-permute-start | bytes 208904 | tf_op jit(solution)/shard_map/ppermute | solution.py:32
  35.6 3.7 %collective-permute-done.6 = f32[136,128]{1,0:T(8,128)S(1)} collective-permute-done((f32[136,128]{1,0:T(8,128)S(1)}, f32[136,128]{1,0:T(8,128)S(1)}, u32[]{:S(2)}, u32[]{:S(2)}) %collective-permute-start.6) | collective-permute-done | bytes 69664 | tf_op jit(solution)/shard_map/ppermute | solution.py:32
  39.4 4.3 %collective-permute-done.7 = f32[136,128]{1,0:T(8,128)S(1)} collective-permute-done((f32[136,128]{1,0:T(8,128)S(1)}, f32[136,128]{1,0:T(8,128)S(1)}, u32[]{:S(2)}, u32[]{:S(2)}) %collective-permute-start.7) | collective-permute-done | bytes 69664 | tf_op jit(solution)/shard_map/ppermute | solution.py:32
  43.7 0.5 collective-permute-start.8
  44.2 5.1 %collective-permute-done.8 = f32[136,128]{1,0:T(8,128)S(1)} collective-permute-done((f32[136,128]{1,0:T(8,128)S(1)}, f32[136,128]{1,0:T(8,128)S(1)}, u32[]{:S(2)}, u32[]{:S(2)}) %collective-permute-start.8) | collective-permute-done | bytes 69664 | tf_op jit(solution)/shard_map/ppermute | solution.py:32
  49.3 2.3 %collective-permute-start.9 = (f32[136,128]{1,0:T(8,128)S(1)}, f32[136,128]{1,0:T(8,128)S(1)}, u32[]{:S(2)}, u32[]{:S(2)}) collective-permute-start(f32[136,128]{1,0:T(8,128)S(1)} %add.40), channel_id=1, source_target_pairs={{0,32},{8,40},{16,48},{24,56},{32,0},{40,8},{48,16},{56,24},{64,96... | collective-permute-start | bytes 208904 | tf_op jit(solution)/shard_map/ppermute | solution.py:32
  51.6 6.3 %collective-permute-done.9 = f32[136,128]{1,0:T(8,128)S(1)} collective-permute-done((f32[136,128]{1,0:T(8,128)S(1)}, f32[136,128]{1,0:T(8,128)S(1)}, u32[]{:S(2)}, u32[]{:S(2)}) %collective-permute-start.9) | collective-permute-done | bytes 69664 | tf_op jit(solution)/shard_map/ppermute | solution.py:32
  58.2 4.3 %collective-permute-done.10 = f32[136,128]{1,0:T(8,128)S(1)} collective-permute-done((f32[136,128]{1,0:T(8,128)S(1)}, f32[136,128]{1,0:T(8,128)S(1)}, u32[]{:S(2)}, u32[]{:S(2)}) %collective-permute-start.10) | collective-permute-done | bytes 69664 | tf_op jit(solution)/shard_map/ppermute | solution.py:32
  62.5 0.6 collective-permute-start.11
  63.1 5.3 %collective-permute-done.11 = f32[136,128]{1,0:T(8,128)S(1)} collective-permute-done((f32[136,128]{1,0:T(8,128)S(1)}, f32[136,128]{1,0:T(8,128)S(1)}, u32[]{:S(2)}, u32[]{:S(2)}) %collective-permute-start.11) | collective-permute-done | bytes 69664 | tf_op jit(solution)/shard_map/ppermute | solution.py:32
  68.7 0.7 maximum_multiply_fusion.g_ref
  69.3 12.8 %shard_map.41 = (f32[2,128,128]{2,1,0:T(8,128)}, f32[2,128,128]{2,1,0:T(8,128)}) custom-call(f32[2,128,128]{2,1,0:T(8,128)} %maximum_multiply_fusion.g_ref), custom_call_target="tpu_custom_call" | custom-call | tf_op jit(solution)/shard_map/pallas_call | solution.py:108
  82.1 0.9 %reduce-precision_convert_fusion.1 = (bf16[2,128,128]{2,1,0:T(8,128)(2,1)S(1)}, bf16[2,128,128]{2,1,0:T(8,128)(2,1)S(1)}) fusion(f32[2,128,128]{2,1,0:T(8,128)} %get-tuple-element.4), kind=kLoop, calls=%fused_computation.33 | loop fusion | flops 131072 | bytes 262144 | tf_op jit(solution)/shard_map/convert_element_type | solution.py:39
  83.0 6.6 %fusion.21 = f32[2,4096,128]{2,1,0:T(8,128)} fusion(bf16[2,4096,384]{2,1,0:T(8,128)(2,1)} %copy-done, bf16[2,128,128]{2,1,0:T(8,128)(2,1)S(1)} %get-tuple-element.15, bf16[2,128,128]{2,1,0:T(8,128)(2,1)S(1)} %get-tuple-element.14), kind=kOutput, calls=%fused_computation.26 | convolution fusion | flops 805896192 | bytes 10616832 | tf_op jit(solution)/shard_map/pcs,pts->pct/dot_general | solution.py:53
  (27 shorter events, 1.0 us)
Async XLA Ops:
  0.6 15.1 %copy-start.1 = (bf16[2,64,64,128]{3,2,1,0:T(8,128)(2,1)S(1)}, bf16[2,64,64,128]{3,2,1,0:T(8,128)(2,1)}, u32[]{:S(2)}) copy-start(bf16[2,64,64,128]{3,2,1,0:T(8,128)(2,1)} %param.3) | copy-start | bytes 6291460
  1.9 10.9 %collective-permute-start = (bf16[2,64,2,128]{3,2,1,0:T(2,128)(2,1)S(1)}, bf16[2,64,2,128]{3,2,1,0:T(2,128)(2,1)S(1)}, u32[]{:S(2)}, u32[]{:S(2)}) collective-permute-start(bf16[2,64,2,128]{3,2,1,0:T(2,128)(2,1)S(1)} %get-tuple-element.8), channel_id=1, source_target_pairs={{0,8},{8,16},{16,24},{24,32},{32,40},{40,48},{48,56},{56,64},{64,7... | collective-permute-start | bytes 196616 | tf_op jit(solution)/shard_map/ppermute | solution.py:18
  3.9 9.0 %collective-permute-start.1 = (bf16[2,64,2,128]{3,2,1,0:T(2,128)(2,1)S(1)}, bf16[2,64,2,128]{3,2,1,0:T(2,128)(2,1)S(1)}, u32[]{:S(2)}, u32[]{:S(2)}) collective-permute-start(bf16[2,64,2,128]{3,2,1,0:T(2,128)(2,1)S(1)} %get-tuple-element.9), channel_id=1, source_target_pairs={{8,0},{16,8},{24,16},{32,24},{40,32},{48,40},{56,48},{64,56},{72,6... | collective-permute-start | bytes 196616 | tf_op jit(solution)/shard_map/ppermute | solution.py:20
  11.0 4.6 %collective-permute-start.2 = (bf16[2,2,64,128]{3,2,1,0:T(8,128)(2,1)S(1)}, bf16[2,2,64,128]{3,2,1,0:T(8,128)(2,1)S(1)}, u32[]{:S(2)}, u32[]{:S(2)}) collective-permute-start(bf16[2,2,64,128]{3,2,1,0:T(8,128)(2,1)S(1)} %get-tuple-element.10), channel_id=1, source_target_pairs={{0,1},{1,2},{2,3},{3,4},{4,5},{5,6},{6,7},{7,0},{8,9},{9,10},{10,1... | collective-permute-start | bytes 196616 | tf_op jit(solution)/shard_map/ppermute | solution.py:18
  11.1 4.6 %collective-permute-start.3 = (bf16[2,2,64,128]{3,2,1,0:T(8,128)(2,1)S(1)}, bf16[2,2,64,128]{3,2,1,0:T(8,128)(2,1)S(1)}, u32[]{:S(2)}, u32[]{:S(2)}) collective-permute-start(bf16[2,2,64,128]{3,2,1,0:T(8,128)(2,1)S(1)} %get-tuple-element.11), channel_id=1, source_target_pairs={{1,0},{2,1},{3,2},{4,3},{5,4},{6,5},{7,6},{0,7},{9,8},{10,9},{11,1... | collective-permute-start | bytes 196616 | tf_op jit(solution)/shard_map/ppermute | solution.py:20
  20.4 2.7 %copy-start = (bf16[2,4096,384]{2,1,0:T(8,128)(2,1)}, bf16[2,4096,384]{2,1,0:T(8,128)(2,1)S(1)}, u32[]{:S(2)}) copy-start(bf16[2,4096,384]{2,1,0:T(8,128)(2,1)S(1)} %pad_maximum_fusion) | copy-start | bytes 18874372
  27.0 1.7 %collective-permute-start.4 = (f32[136,128]{1,0:T(8,128)S(1)}, f32[136,128]{1,0:T(8,128)S(1)}, u32[]{:S(2)}, u32[]{:S(2)}) collective-permute-start(f32[136,128]{1,0:T(8,128)S(1)} %maximum_maximum_fusion), channel_id=1, source_target_pairs={{0,1},{1,0},{2,3},{3,2},{4,5},{5,4},{6,7},{7,6},{8,9},{9,8},{10,11... | collective-permute-start | bytes 208904 | tf_op jit(solution)/shard_map/ppermute | solution.py:32
  28.9 4.5 %collective-permute-start.5 = (f32[136,128]{1,0:T(8,128)S(1)}, f32[136,128]{1,0:T(8,128)S(1)}, u32[]{:S(2)}, u32[]{:S(2)}) collective-permute-start(f32[136,128]{1,0:T(8,128)S(1)} %fusion.33), channel_id=1, source_target_pairs={{0,2},{1,3},{2,0},{3,1},{4,6},{5,7},{6,4},{7,5},{8,10},{9,11},{10,... | collective-permute-start | bytes 208904 | tf_op jit(solution)/shard_map/ppermute | solution.py:32
  33.4 5.9 %collective-permute-start.6 = (f32[136,128]{1,0:T(8,128)S(1)}, f32[136,128]{1,0:T(8,128)S(1)}, u32[]{:S(2)}, u32[]{:S(2)}) collective-permute-start(f32[136,128]{1,0:T(8,128)S(1)} %add.37), channel_id=1, source_target_pairs={{0,4},{1,5},{2,6},{3,7},{4,0},{5,1},{6,2},{7,3},{8,12},{9,13},{10,... | collective-permute-start | bytes 208904 | tf_op jit(solution)/shard_map/ppermute | solution.py:32
  39.3 4.4 %collective-permute-start.7 = (f32[136,128]{1,0:T(8,128)S(1)}, f32[136,128]{1,0:T(8,128)S(1)}, u32[]{:S(2)}, u32[]{:S(2)}) collective-permute-start(f32[136,128]{1,0:T(8,128)S(1)} %add.38), channel_id=1, source_target_pairs={{0,8},{8,0},{16,24},{24,16},{32,40},{40,32},{48,56},{56,48},{64,72... | collective-permute-start | bytes 208904 | tf_op jit(solution)/shard_map/ppermute | solution.py:32
  43.7 5.6 %collective-permute-start.8 = (f32[136,128]{1,0:T(8,128)S(1)}, f32[136,128]{1,0:T(8,128)S(1)}, u32[]{:S(2)}, u32[]{:S(2)}) collective-permute-start(f32[136,128]{1,0:T(8,128)S(1)} %add.39), channel_id=1, source_target_pairs={{0,16},{8,24},{16,0},{24,8},{32,48},{40,56},{48,32},{56,40},{64,80... | collective-permute-start | bytes 208904 | tf_op jit(solution)/shard_map/ppermute | solution.py:32
  49.3 8.6 %collective-permute-start.9 = (f32[136,128]{1,0:T(8,128)S(1)}, f32[136,128]{1,0:T(8,128)S(1)}, u32[]{:S(2)}, u32[]{:S(2)}) collective-permute-start(f32[136,128]{1,0:T(8,128)S(1)} %add.40), channel_id=1, source_target_pairs={{0,32},{8,40},{16,48},{24,56},{32,0},{40,8},{48,16},{56,24},{64,96... | collective-permute-start | bytes 208904 | tf_op jit(solution)/shard_map/ppermute | solution.py:32
  57.9 4.6 %collective-permute-start.10 = (f32[136,128]{1,0:T(8,128)S(1)}, f32[136,128]{1,0:T(8,128)S(1)}, u32[]{:S(2)}, u32[]{:S(2)}) collective-permute-start(f32[136,128]{1,0:T(8,128)S(1)} %add.41), channel_id=1, source_target_pairs={{0,64},{8,72},{16,80},{24,88},{32,96},{40,104},{48,112},{56,120},{... | collective-permute-start | bytes 208904 | tf_op jit(solution)/shard_map/ppermute | solution.py:32
  62.5 5.9 %collective-permute-start.11 = (f32[136,128]{1,0:T(8,128)S(1)}, f32[136,128]{1,0:T(8,128)S(1)}, u32[]{:S(2)}, u32[]{:S(2)}) collective-permute-start(f32[136,128]{1,0:T(8,128)S(1)} %add.42), channel_id=1, source_target_pairs={{0,128},{8,136},{16,144},{24,152},{32,160},{40,168},{48,176},{56,1... | collective-permute-start | bytes 208904 | tf_op jit(solution)/shard_map/ppermute | solution.py:32

commit v8 on v6

--- a/solution.py
+++ b/solution.py
@@ -94,8 +94,8 @@
             rowj = pivot[p]
             root = jnp.sqrt(rowj[:, j:j + 1])
             inv = lax.rsqrt(rowj[:, j:j + 1])
-            lrow = jnp.where(lane > j, rowj * inv, jnp.where(lane == j, root, 0.0))
-            rt_ref[p, j:j + 1, :] = lrow
+            lrow = rowj * inv
+            rt_ref[p, j:j + 1, :] = jnp.where(lane > j, lrow, jnp.where(lane == j, root, 0.0))
             if j + 1 < n:
                 nxt = s_ref[p, j + 1:j + 2, :]
                 pivot[p] = nxt - (nxt[:, j:j + 1] * inv) * lrow

time: 85.5 us -> 85.2 us (level)
  no operation moved by 1% of the time
where the time goes in v8:
time: 85.2 us; the launch traced here: 84.9 us
  waiting for transfers between devices  32.7 us (38%)
  starting transfers between devices  18.4 us (22%)
  Pallas kernels  12.4 us (15%)
  other arithmetic  7.56 us (9%)
  matrix products  7.45 us (9%)
  local copies, waits for them, and re-layouts  5.45 us (6%)
  between operations  0.86 us (1%)
    ppermute x8, waiting for transfers between devices, butterfly_sum(): x = x + lax.ppermute(x, axis, [(i, i ^ step) for i in range(count)])  32.7 us
    pallas_call x1, Pallas kernels, chol_inv(): pl.pallas_call(chol_inv_kernel, out_shape=(jax.ShapeDtypeStruct(gram.shap...  12.4 us
    ppermute x8, starting transfers between devices, butterfly_sum(): x = x + lax.ppermute(x, axis, [(i, i ^ step) for i in range(count)])  8.48 us
    ppermute x2, starting transfers between devices, with_halo(): lax.ppermute(head, axis, [((i + 1) % count, i) for i in range(count)])  7.96 us
    dot_general x3, matrix products, dot(): return jnp.einsum('pcs,pts->pct', a, b, preferred_element_type=jnp.float32)  5.11 us
    unnamed x10, local copies, waits for them, and re-layouts  3 us
    convert_element_type x1, other arithmetic, local(): padded_u = with_halo(u_field, (('gz', 2),), 2).astype(jnp.float32)  2.78 us
    sub x1, other arithmetic, local(): vorticity = span_diff / (12.0 * span_step) - stream_diff / 12.0  2.77 us
  transfers between devices with their start and end apart: 12, of which 8 were waited for; matrix products, arithmetic and copies ran while one was open for 4% of the time, Pallas kernels for 0%

profile of v8, /device:TPU:8, one launch (start us, length us, event | category | flops | bytes accessed | tf_op | source)
XLA Modules:
  0.0 84.9 jit_solution(17525469618680502048)
XLA Ops:
  0.6 1.3 %fusion.18 = (bf16[2,64,2,128]{3,2,1,0:T(2,128)(2,1)S(1)}, bf16[2,64,2,128]{3,2,1,0:T(2,128)(2,1)S(1)}) fusion(bf16[2,64,64,128]{3,2,1,0:T(8,128)(2,1)} %param.2), kind=kLoop, calls=%fused_computation.43 | loop fusion | bytes 262144 | tf_op jit(solution)/shard_map/slice | solution.py:15
  1.9 2.0 %collective-permute-start = (bf16[2,64,2,128]{3,2,1,0:T(2,128)(2,1)S(1)}, bf16[2,64,2,128]{3,2,1,0:T(2,128)(2,1)S(1)}, u32[]{:S(2)}, u32[]{:S(2)}) collective-permute-start(bf16[2,64,2,128]{3,2,1,0:T(2,128)(2,1)S(1)} %get-tuple-element.12), channel_id=1, source_target_pairs={{0,8},{8,16},{16,24},{24,32},{32,40},{40,48},{48,56},{56,64},{64,7... | collective-permute-start | bytes 196616 | tf_op jit(solution)/shard_map/ppermute | solution.py:18
  3.9 6.2 %collective-permute-start.1 = (bf16[2,64,2,128]{3,2,1,0:T(2,128)(2,1)S(1)}, bf16[2,64,2,128]{3,2,1,0:T(2,128)(2,1)S(1)}, u32[]{:S(2)}, u32[]{:S(2)}) collective-permute-start(bf16[2,64,2,128]{3,2,1,0:T(2,128)(2,1)S(1)} %get-tuple-element.13), channel_id=1, source_target_pairs={{8,0},{16,8},{24,16},{32,24},{40,32},{48,40},{56,48},{64,56},{72,6... | collective-permute-start | bytes 196616 | tf_op jit(solution)/shard_map/ppermute | solution.py:20
  10.2 0.9 %fusion.19 = (bf16[2,2,64,128]{3,2,1,0:T(8,128)(2,1)S(1)}, bf16[2,2,64,128]{3,2,1,0:T(8,128)(2,1)S(1)}) fusion(bf16[2,64,64,128]{3,2,1,0:T(8,128)(2,1)} %param.3), kind=kLoop, calls=%fused_computation.44 | loop fusion | bytes 262144 | tf_op jit(solution)/shard_map/slice | solution.py:15
  11.1 1.7 %collective-permute-start.3 = (bf16[2,2,64,128]{3,2,1,0:T(8,128)(2,1)S(1)}, bf16[2,2,64,128]{3,2,1,0:T(8,128)(2,1)S(1)}, u32[]{:S(2)}, u32[]{:S(2)}) collective-permute-start(bf16[2,2,64,128]{3,2,1,0:T(8,128)(2,1)S(1)} %get-tuple-element.15), channel_id=1, source_target_pairs={{1,0},{2,1},{3,2},{4,3},{5,4},{6,5},{7,6},{0,7},{9,8},{10,9},{11,1... | collective-permute-start | bytes 196616 | tf_op jit(solution)/shard_map/ppermute | solution.py:20
  12.9 2.8 %maximum_convert_fusion = f32[2,64,68,128]{3,2,1,0:T(8,128)S(1)} fusion(bf16[2,64,2,128]{3,2,1,0:T(2,128)(2,1)S(1)} %collective-permute-done.1, bf16[2,64,64,128]{3,2,1,0:T(8,128)(2,1)} %param.2, bf16[2,64,2,128]{3,2,1,0:T(2,128)(2,1)S(1)} %collective-permute-done), kind=kLoop, calls=%fused_computation.16 | loop fusion | flops 6684672 | bytes 6684672 | tf_op jit(solution)/shard_map/convert_element_type | solution.py:122
  16.0 2.8 %fusion.4 = f32[2,64,64,128]{3,2,1,0:T(8,128)S(1)} fusion(f32[2,68,64,128]{3,2,1,0:T(8,128)S(1)} %maximum_convert_fusion.1, f32[2,64,68,128]{3,2,1,0:T(8,128)S(1)} %maximum_convert_fusion), kind=kLoop, calls=%fused_computation.8 | loop fusion | flops 11534336 | bytes 37748736 | tf_op jit(solution)/shard_map/sub | solution.py:130
  18.8 0.7 fusion.1
  19.5 1.3 %copy-done = bf16[2,4096,128]{2,1,0:T(8,128)(2,1)} copy-done((bf16[2,4096,128]{2,1,0:T(8,128)(2,1)}, bf16[2,4096,128]{2,1,0:T(8,128)(2,1)S(1)}, u32[]{:S(2)}) %copy-start) | copy-done | bytes 2097176
  20.8 0.8 fusion.20
  21.7 0.8 convolution_add_fusion.2
  22.5 0.8 copy-done.1
  23.3 0.8 convolution_add_fusion.1
  24.2 0.8 collective-permute-start.4
  25.0 0.9 %collective-permute-done.4 = f32[136,128]{1,0:T(8,128)S(1)} collective-permute-done((f32[136,128]{1,0:T(8,128)S(1)}, f32[136,128]{1,0:T(8,128)S(1)}, u32[]{:S(2)}, u32[]{:S(2)}) %collective-permute-start.4) | collective-permute-done | bytes 69664 | tf_op jit(solution)/shard_map/ppermute | solution.py:32
  26.0 1.4 %collective-permute-start.5 = (f32[136,128]{1,0:T(8,128)S(1)}, f32[136,128]{1,0:T(8,128)S(1)}, u32[]{:S(2)}, u32[]{:S(2)}) collective-permute-start(f32[136,128]{1,0:T(8,128)S(1)} %fusion.17), channel_id=1, source_target_pairs={{0,2},{1,3},{2,0},{3,1},{4,6},{5,7},{6,4},{7,5},{8,10},{9,11},{10,... | collective-permute-start | bytes 208904 | tf_op jit(solution)/shard_map/ppermute | solution.py:32
  27.4 3.2 %collective-permute-done.5 = f32[136,128]{1,0:T(8,128)S(1)} collective-permute-done((f32[136,128]{1,0:T(8,128)S(1)}, f32[136,128]{1,0:T(8,128)S(1)}, u32[]{:S(2)}, u32[]{:S(2)}) %collective-permute-start.5) | collective-permute-done | bytes 69664 | tf_op jit(solution)/shard_map/ppermute | solution.py:32
  30.6 2.2 %collective-permute-start.6 = (f32[136,128]{1,0:T(8,128)S(1)}, f32[136,128]{1,0:T(8,128)S(1)}, u32[]{:S(2)}, u32[]{:S(2)}) collective-permute-start(f32[136,128]{1,0:T(8,128)S(1)} %add.43), channel_id=1, source_target_pairs={{0,4},{1,5},{2,6},{3,7},{4,0},{5,1},{6,2},{7,3},{8,12},{9,13},{10,... | collective-permute-start | bytes 208904 | tf_op jit(solution)/shard_map/ppermute | solution.py:32
  32.8 3.7 %collective-permute-done.6 = f32[136,128]{1,0:T(8,128)S(1)} collective-permute-done((f32[136,128]{1,0:T(8,128)S(1)}, f32[136,128]{1,0:T(8,128)S(1)}, u32[]{:S(2)}, u32[]{:S(2)}) %collective-permute-start.6) | collective-permute-done | bytes 69664 | tf_op jit(solution)/shard_map/ppermute | solution.py:32
  36.6 4.3 %collective-permute-done.7 = f32[136,128]{1,0:T(8,128)S(1)} collective-permute-done((f32[136,128]{1,0:T(8,128)S(1)}, f32[136,128]{1,0:T(8,128)S(1)}, u32[]{:S(2)}, u32[]{:S(2)}) %collective-permute-start.7) | collective-permute-done | bytes 69664 | tf_op jit(solution)/shard_map/ppermute | solution.py:32
  41.4 5.1 %collective-permute-done.8 = f32[136,128]{1,0:T(8,128)S(1)} collective-permute-done((f32[136,128]{1,0:T(8,128)S(1)}, f32[136,128]{1,0:T(8,128)S(1)}, u32[]{:S(2)}, u32[]{:S(2)}) %collective-permute-start.8) | collective-permute-done | bytes 69664 | tf_op jit(solution)/shard_map/ppermute | solution.py:32
  46.5 2.3 %collective-permute-start.9 = (f32[136,128]{1,0:T(8,128)S(1)}, f32[136,128]{1,0:T(8,128)S(1)}, u32[]{:S(2)}, u32[]{:S(2)}) collective-permute-start(f32[136,128]{1,0:T(8,128)S(1)} %add.46), channel_id=1, source_target_pairs={{0,32},{8,40},{16,48},{24,56},{32,0},{40,8},{48,16},{56,24},{64,96... | collective-permute-start | bytes 208904 | tf_op jit(solution)/shard_map/ppermute | solution.py:32
  48.7 6.3 %collective-permute-done.9 = f32[136,128]{1,0:T(8,128)S(1)} collective-permute-done((f32[136,128]{1,0:T(8,128)S(1)}, f32[136,128]{1,0:T(8,128)S(1)}, u32[]{:S(2)}, u32[]{:S(2)}) %collective-permute-start.9) | collective-permute-done | bytes 69664 | tf_op jit(solution)/shard_map/ppermute | solution.py:32
  55.2 4.3 %collective-permute-done.10 = f32[136,128]{1,0:T(8,128)S(1)} collective-permute-done((f32[136,128]{1,0:T(8,128)S(1)}, f32[136,128]{1,0:T(8,128)S(1)}, u32[]{:S(2)}, u32[]{:S(2)}) %collective-permute-start.10) | collective-permute-done | bytes 69664 | tf_op jit(solution)/shard_map/ppermute | solution.py:32
  59.5 1.1 %collective-permute-start.11 = (f32[136,128]{1,0:T(8,128)S(1)}, f32[136,128]{1,0:T(8,128)S(1)}, u32[]{:S(2)}, u32[]{:S(2)}) collective-permute-start(f32[136,128]{1,0:T(8,128)S(1)} %add.48), channel_id=1, source_target_pairs={{0,128},{8,136},{16,144},{24,152},{32,160},{40,168},{48,176},{56,1... | collective-permute-start | bytes 208904 | tf_op jit(solution)/shard_map/ppermute | solution.py:32
  60.6 5.0 %collective-permute-done.11 = f32[136,128]{1,0:T(8,128)S(1)} collective-permute-done((f32[136,128]{1,0:T(8,128)S(1)}, f32[136,128]{1,0:T(8,128)S(1)}, u32[]{:S(2)}, u32[]{:S(2)}) %collective-permute-start.11) | collective-permute-done | bytes 69664 | tf_op jit(solution)/shard_map/ppermute | solution.py:32
  65.8 0.7 maximum_multiply_fusion.g_ref
  66.5 12.4 %shard_map.41 = (f32[2,128,128]{2,1,0:T(8,128)}, f32[2,128,128]{2,1,0:T(8,128)}) custom-call(f32[2,128,128]{2,1,0:T(8,128)} %maximum_multiply_fusion.g_ref), custom_call_target="tpu_custom_call" | custom-call | tf_op jit(solution)/shard_map/pallas_call | solution.py:111
  78.9 1.7 %fusion.10 = f32[2,4096,128]{2,1,0:T(8,128)S(1)} fusion(bf16[2,4096,128]{2,1,0:T(8,128)(2,1)S(1)} %get-tuple-element.6, f32[2,128,128]{2,1,0:T(8,128)} %get-tuple-element.8), kind=kOutput, calls=%fused_computation.26 | convolution fusion | flops 268533760 | bytes 6422528 | tf_op jit(solution)/shard_map/pcs,pts->pct/dot_general | solution.py:54
  80.6 0.7 fusion.16
  81.3 0.9 %copy-done.2 = bf16[2,4096,128]{2,1,0:T(8,128)(2,1)S(1)} copy-done((bf16[2,4096,128]{2,1,0:T(8,128)(2,1)S(1)}, bf16[2,4096,128]{2,1,0:T(8,128)(2,1)}, u32[]{:S(2)}) %copy-start.2) | copy-done | bytes 2097176
  82.2 2.7 %fusion = f32[2,4096,128]{2,1,0:T(8,128)} fusion(f32[2,4096,128]{2,1,0:T(8,128)S(1)} %fusion.16, f32[2,4096,128]{2,1,0:T(8,128)S(1)} %fusion.10, bf16[2,4096,128]{2,1,0:T(8,128)(2,1)S(1)} %copy-done.2, f32[2,128,128]{2,1,0:T(8,128)S(1)} %copy-done.4), kind=kOutput, calls=%fused_computation.3 | convolution fusion | flops 270598144 | bytes 14811136 | tf_op jit(solution)/shard_map/pcs,pts->pct/dot_general | solution.py:54
  (33 shorter events, 1.7 us)
Async XLA Ops:
  0.6 15.1 %copy-start.3 = (bf16[2,64,64,128]{3,2,1,0:T(8,128)(2,1)S(1)}, bf16[2,64,64,128]{3,2,1,0:T(8,128)(2,1)}, u32[]{:S(2)}) copy-start(bf16[2,64,64,128]{3,2,1,0:T(8,128)(2,1)} %param.3) | copy-start | bytes 6291460
  1.9 10.9 %collective-permute-start = (bf16[2,64,2,128]{3,2,1,0:T(2,128)(2,1)S(1)}, bf16[2,64,2,128]{3,2,1,0:T(2,128)(2,1)S(1)}, u32[]{:S(2)}, u32[]{:S(2)}) collective-permute-start(bf16[2,64,2,128]{3,2,1,0:T(2,128)(2,1)S(1)} %get-tuple-element.12), channel_id=1, source_target_pairs={{0,8},{8,16},{16,24},{24,32},{32,40},{40,48},{48,56},{56,64},{64,7... | collective-permute-start | bytes 196616 | tf_op jit(solution)/shard_map/ppermute | solution.py:18
  3.9 9.0 %collective-permute-start.1 = (bf16[2,64,2,128]{3,2,1,0:T(2,128)(2,1)S(1)}, bf16[2,64,2,128]{3,2,1,0:T(2,128)(2,1)S(1)}, u32[]{:S(2)}, u32[]{:S(2)}) collective-permute-start(bf16[2,64,2,128]{3,2,1,0:T(2,128)(2,1)S(1)} %get-tuple-element.13), channel_id=1, source_target_pairs={{8,0},{16,8},{24,16},{32,24},{40,32},{48,40},{56,48},{64,56},{72,6... | collective-permute-start | bytes 196616 | tf_op jit(solution)/shard_map/ppermute | solution.py:20
  11.0 4.6 %collective-permute-start.2 = (bf16[2,2,64,128]{3,2,1,0:T(8,128)(2,1)S(1)}, bf16[2,2,64,128]{3,2,1,0:T(8,128)(2,1)S(1)}, u32[]{:S(2)}, u32[]{:S(2)}) collective-permute-start(bf16[2,2,64,128]{3,2,1,0:T(8,128)(2,1)S(1)} %get-tuple-element.14), channel_id=1, source_target_pairs={{0,1},{1,2},{2,3},{3,4},{4,5},{5,6},{6,7},{7,0},{8,9},{9,10},{10,1... | collective-permute-start | bytes 196616 | tf_op jit(solution)/shard_map/ppermute | solution.py:18
  11.1 4.6 %collective-permute-start.3 = (bf16[2,2,64,128]{3,2,1,0:T(8,128)(2,1)S(1)}, bf16[2,2,64,128]{3,2,1,0:T(8,128)(2,1)S(1)}, u32[]{:S(2)}, u32[]{:S(2)}) collective-permute-start(bf16[2,2,64,128]{3,2,1,0:T(8,128)(2,1)S(1)} %get-tuple-element.15), channel_id=1, source_target_pairs={{1,0},{2,1},{3,2},{4,3},{5,4},{6,5},{7,6},{0,7},{9,8},{10,9},{11,1... | collective-permute-start | bytes 196616 | tf_op jit(solution)/shard_map/ppermute | solution.py:20
  19.5 1.3 %copy-start = (bf16[2,4096,128]{2,1,0:T(8,128)(2,1)}, bf16[2,4096,128]{2,1,0:T(8,128)(2,1)S(1)}, u32[]{:S(2)}) copy-start(bf16[2,4096,128]{2,1,0:T(8,128)(2,1)S(1)} %get-tuple-element.7) | copy-start | bytes 6291460
  21.7 1.6 %copy-start.1 = (bf16[2,4096,128]{2,1,0:T(8,128)(2,1)S(1)}, bf16[2,4096,128]{2,1,0:T(8,128)(2,1)}, u32[]{:S(2)}) copy-start(bf16[2,4096,128]{2,1,0:T(8,128)(2,1)} %copy-done) | copy-start | bytes 6291460
  24.2 1.7 %collective-permute-start.4 = (f32[136,128]{1,0:T(8,128)S(1)}, f32[136,128]{1,0:T(8,128)S(1)}, u32[]{:S(2)}, u32[]{:S(2)}) collective-permute-start(f32[136,128]{1,0:T(8,128)S(1)} %maximum_maximum_fusion), channel_id=1, source_target_pairs={{0,1},{1,0},{2,3},{3,2},{4,5},{5,4},{6,7},{7,6},{8,9},{9,8},{10,11... | collective-permute-start | bytes 208904 | tf_op jit(solution)/shard_map/ppermute | solution.py:32
  26.0 4.5 %collective-permute-start.5 = (f32[136,128]{1,0:T(8,128)S(1)}, f32[136,128]{1,0:T(8,128)S(1)}, u32[]{:S(2)}, u32[]{:S(2)}) collective-permute-start(f32[136,128]{1,0:T(8,128)S(1)} %fusion.17), channel_id=1, source_target_pairs={{0,2},{1,3},{2,0},{3,1},{4,6},{5,7},{6,4},{7,5},{8,10},{9,11},{10,... | collective-permute-start | bytes 208904 | tf_op jit(solution)/shard_map/ppermute | solution.py:32
  30.6 5.9 %collective-permute-start.6 = (f32[136,128]{1,0:T(8,128)S(1)}, f32[136,128]{1,0:T(8,128)S(1)}, u32[]{:S(2)}, u32[]{:S(2)}) collective-permute-start(f32[136,128]{1,0:T(8,128)S(1)} %add.43), channel_id=1, source_target_pairs={{0,4},{1,5},{2,6},{3,7},{4,0},{5,1},{6,2},{7,3},{8,12},{9,13},{10,... | collective-permute-start | bytes 208904 | tf_op jit(solution)/shard_map/ppermute | solution.py:32
  36.5 4.4 %collective-permute-start.7 = (f32[136,128]{1,0:T(8,128)S(1)}, f32[136,128]{1,0:T(8,128)S(1)}, u32[]{:S(2)}, u32[]{:S(2)}) collective-permute-start(f32[136,128]{1,0:T(8,128)S(1)} %add.44), channel_id=1, source_target_pairs={{0,8},{8,0},{16,24},{24,16},{32,40},{40,32},{48,56},{56,48},{64,72... | collective-permute-start | bytes 208904 | tf_op jit(solution)/shard_map/ppermute | solution.py:32
  40.9 5.6 %collective-permute-start.8 = (f32[136,128]{1,0:T(8,128)S(1)}, f32[136,128]{1,0:T(8,128)S(1)}, u32[]{:S(2)}, u32[]{:S(2)}) collective-permute-start(f32[136,128]{1,0:T(8,128)S(1)} %add.45), channel_id=1, source_target_pairs={{0,16},{8,24},{16,0},{24,8},{32,48},{40,56},{48,32},{56,40},{64,80... | collective-permute-start | bytes 208904 | tf_op jit(solution)/shard_map/ppermute | solution.py:32
  46.5 8.6 %collective-permute-start.9 = (f32[136,128]{1,0:T(8,128)S(1)}, f32[136,128]{1,0:T(8,128)S(1)}, u32[]{:S(2)}, u32[]{:S(2)}) collective-permute-start(f32[136,128]{1,0:T(8,128)S(1)} %add.46), channel_id=1, source_target_pairs={{0,32},{8,40},{16,48},{24,56},{32,0},{40,8},{48,16},{56,24},{64,96... | collective-permute-start | bytes 208904 | tf_op jit(solution)/shard_map/ppermute | solution.py:32
  55.1 4.4 %collective-permute-start.10 = (f32[136,128]{1,0:T(8,128)S(1)}, f32[136,128]{1,0:T(8,128)S(1)}, u32[]{:S(2)}, u32[]{:S(2)}) collective-permute-start(f32[136,128]{1,0:T(8,128)S(1)} %add.47), channel_id=1, source_target_pairs={{0,64},{8,72},{16,80},{24,88},{32,96},{40,104},{48,112},{56,120},{... | collective-permute-start | bytes 208904 | tf_op jit(solution)/shard_map/ppermute | solution.py:32
  59.5 6.1 %collective-permute-start.11 = (f32[136,128]{1,0:T(8,128)S(1)}, f32[136,128]{1,0:T(8,128)S(1)}, u32[]{:S(2)}, u32[]{:S(2)}) collective-permute-start(f32[136,128]{1,0:T(8,128)S(1)} %add.48), channel_id=1, source_target_pairs={{0,128},{8,136},{16,144},{24,152},{32,160},{40,168},{48,176},{56,1... | collective-permute-start | bytes 208904 | tf_op jit(solution)/shard_map/ppermute | solution.py:32
  78.9 1.7 %copy-start.4 = (f32[2,128,128]{2,1,0:T(8,128)S(1)}, f32[2,128,128]{2,1,0:T(8,128)}, u32[]{:S(2)}) copy-start(f32[2,128,128]{2,1,0:T(8,128)} %get-tuple-element.8) | copy-start | bytes 393220
  80.6 1.6 %copy-start.2 = (bf16[2,4096,128]{2,1,0:T(8,128)(2,1)S(1)}, bf16[2,4096,128]{2,1,0:T(8,128)(2,1)}, u32[]{:S(2)}) copy-start(bf16[2,4096,128]{2,1,0:T(8,128)(2,1)} %copy-done) | copy-start | bytes 6291460

commit v9 on v8

--- a/solution.py
+++ b/solution.py
@@ -24,15 +24,32 @@
     return cells
 
 
+def ring_stages(size):
+    stages, step = [], 1
+    while step < size:
+        if step * 2 == size and size > 2:
+            stages.append([size - 1 - p for p in range(size)])
+        else:
+            stages.append([p ^ step for p in range(size)])
+        step *= 2
+    return stages
+
+
+def axis_stages(count, inner):
+    if count % inner:
+        inner = count
+    outer = count // inner
+    stages = [[i - i % inner + perm[i % inner] for i in range(count)] for perm in ring_stages(inner)]
+    stages += [[perm[i // inner] * inner + i % inner for i in range(count)] for perm in ring_stages(outer)]
+    return stages
+
+
 def butterfly_sum(x, axes):
-    for axis in axes:
+    for axis, inner in axes:
         count = lax.axis_size(axis)
-        step = 1
-        while step < count:
-            x = x + lax.ppermute(x, axis, [(i, i ^ step) for i in range(count)])
-            step *= 2
+        for partner in axis_stages(count, inner):
+            x = x + lax.ppermute(x, axis, [(i, partner[i]) for i in range(count)])
     return x
-
 
 def split(values):
     head32 = lax.reduce_precision(values, exponent_bits=8, mantissa_bits=7)
@@ -132,9 +149,9 @@
     head, tail = lax.optimization_barrier(split(columns))
     gram_local = split_gram(head, tail)
     if planes == 2:
-        gram_sum = unpack_pair(butterfly_sum(pack_pair(gram_local), ("gx", "gz")))
+        gram_sum = unpack_pair(butterfly_sum(pack_pair(gram_local), (("gx", 2), ("gz", 8))))
     else:
-        gram_sum = butterfly_sum(gram_local, ("gx", "gz"))
+        gram_sum = butterfly_sum(gram_local, (("gx", 2), ("gz", 8)))
     total_cells = rows_x * rows_z * lax.axis_size("gz") * lax.axis_size("gx")
     gram = gram_sum / total_cells
     factor_r, lower_inverse = chol_inv(gram)

time: 85.2 us -> 82.3 us (0.966); the launches traced: 84.9 us -> 80.7 us
  waiting for transfers between devices: 32.7 us -> 29.6 us
  starting transfers between devices: 18.4 us -> 17.5 us
    ppermute x8, waiting for transfers between devices: 32.7 us -> 29.6 us  [butterfly_sum(): x = x + lax.ppermute(x, axis, [(i, partner[i]) for i in range(count)])]
    ppermute x8, starting transfers between devices: 8.48 us -> 7.5 us  [butterfly_sum(): x = x + lax.ppermute(x, axis, [(i, partner[i]) for i in range(count)])]
  transfers between devices with their start and end apart: 12 -> 12, of which waited for: 8 -> 8; matrix products, arithmetic and copies ran while one was open for 4% -> 5% of each run, Pallas kernels for 0% -> 0%
where the time goes in v9:
time: 82.3 us; the launch traced here: 80.7 us
  waiting for transfers between devices  29.6 us (36%)
  starting transfers between devices  17.5 us (21%)
  Pallas kernels  12.4 us (15%)
  other arithmetic  7.56 us (9%)
  matrix products  7.44 us (9%)
  local copies, waits for them, and re-layouts  5.45 us (7%)
  between operations  0.86 us (1%)
    ppermute x8, waiting for transfers between devices, butterfly_sum(): x = x + lax.ppermute(x, axis, [(i, partner[i]) for i in range(count)])  29.6 us
    pallas_call x1, Pallas kernels, chol_inv(): pl.pallas_call(chol_inv_kernel, out_shape=(jax.ShapeDtypeStruct(gram.shap...  12.4 us
    ppermute x2, starting transfers between devices, with_halo(): lax.ppermute(head, axis, [((i + 1) % count, i) for i in range(count)])  7.96 us
    ppermute x8, starting transfers between devices, butterfly_sum(): x = x + lax.ppermute(x, axis, [(i, partner[i]) for i in range(count)])  7.5 us
    dot_general x3, matrix products, dot(): return jnp.einsum('pcs,pts->pct', a, b, preferred_element_type=jnp.float32)  5.11 us
    unnamed x10, local copies, waits for them, and re-layouts  3 us
    convert_element_type x1, other arithmetic, local(): padded_u = with_halo(u_field, (('gz', 2),), 2).astype(jnp.float32)  2.78 us
    sub x1, other arithmetic, local(): vorticity = span_diff / (12.0 * span_step) - stream_diff / 12.0  2.77 us
  transfers between devices with their start and end apart: 12, of which 8 were waited for; matrix products, arithmetic and copies ran while one was open for 5% of the time, Pallas kernels for 0%

profile of v9, /device:TPU:8, one launch (start us, length us, event | category | flops | bytes accessed | tf_op | source)
XLA Modules:
  0.0 80.7 jit_solution(17279025413273606235)
XLA Ops:
  0.6 1.3 %fusion.18 = (bf16[2,64,2,128]{3,2,1,0:T(2,128)(2,1)S(1)}, bf16[2,64,2,128]{3,2,1,0:T(2,128)(2,1)S(1)}) fusion(bf16[2,64,64,128]{3,2,1,0:T(8,128)(2,1)} %param.2), kind=kLoop, calls=%fused_computation.43 | loop fusion | bytes 262144 | tf_op jit(solution)/shard_map/slice | solution.py:15
  1.9 2.0 %collective-permute-start = (bf16[2,64,2,128]{3,2,1,0:T(2,128)(2,1)S(1)}, bf16[2,64,2,128]{3,2,1,0:T(2,128)(2,1)S(1)}, u32[]{:S(2)}, u32[]{:S(2)}) collective-permute-start(bf16[2,64,2,128]{3,2,1,0:T(2,128)(2,1)S(1)} %get-tuple-element.12), channel_id=1, source_target_pairs={{0,8},{8,16},{16,24},{24,32},{32,40},{40,48},{48,56},{56,64},{64,7... | collective-permute-start | bytes 196616 | tf_op jit(solution)/shard_map/ppermute | solution.py:18
  3.9 6.2 %collective-permute-start.1 = (bf16[2,64,2,128]{3,2,1,0:T(2,128)(2,1)S(1)}, bf16[2,64,2,128]{3,2,1,0:T(2,128)(2,1)S(1)}, u32[]{:S(2)}, u32[]{:S(2)}) collective-permute-start(bf16[2,64,2,128]{3,2,1,0:T(2,128)(2,1)S(1)} %get-tuple-element.13), channel_id=1, source_target_pairs={{8,0},{16,8},{24,16},{32,24},{40,32},{48,40},{56,48},{64,56},{72,6... | collective-permute-start | bytes 196616 | tf_op jit(solution)/shard_map/ppermute | solution.py:20
  10.2 0.9 %fusion.19 = (bf16[2,2,64,128]{3,2,1,0:T(8,128)(2,1)S(1)}, bf16[2,2,64,128]{3,2,1,0:T(8,128)(2,1)S(1)}) fusion(bf16[2,64,64,128]{3,2,1,0:T(8,128)(2,1)} %param.3), kind=kLoop, calls=%fused_computation.44 | loop fusion | bytes 262144 | tf_op jit(solution)/shard_map/slice | solution.py:15
  11.1 1.7 %collective-permute-start.3 = (bf16[2,2,64,128]{3,2,1,0:T(8,128)(2,1)S(1)}, bf16[2,2,64,128]{3,2,1,0:T(8,128)(2,1)S(1)}, u32[]{:S(2)}, u32[]{:S(2)}) collective-permute-start(bf16[2,2,64,128]{3,2,1,0:T(8,128)(2,1)S(1)} %get-tuple-element.15), channel_id=1, source_target_pairs={{1,0},{2,1},{3,2},{4,3},{5,4},{6,5},{7,6},{0,7},{9,8},{10,9},{11,1... | collective-permute-start | bytes 196616 | tf_op jit(solution)/shard_map/ppermute | solution.py:20
  12.9 2.8 %maximum_convert_fusion = f32[2,64,68,128]{3,2,1,0:T(8,128)S(1)} fusion(bf16[2,64,2,128]{3,2,1,0:T(2,128)(2,1)S(1)} %collective-permute-done.1, bf16[2,64,64,128]{3,2,1,0:T(8,128)(2,1)} %param.2, bf16[2,64,2,128]{3,2,1,0:T(2,128)(2,1)S(1)} %collective-permute-done), kind=kLoop, calls=%fused_computation.16 | loop fusion | flops 6684672 | bytes 6684672 | tf_op jit(solution)/shard_map/convert_element_type | solution.py:139
  16.0 2.8 %fusion.4 = f32[2,64,64,128]{3,2,1,0:T(8,128)S(1)} fusion(f32[2,68,64,128]{3,2,1,0:T(8,128)S(1)} %maximum_convert_fusion.1, f32[2,64,68,128]{3,2,1,0:T(8,128)S(1)} %maximum_convert_fusion), kind=kLoop, calls=%fused_computation.8 | loop fusion | flops 11534336 | bytes 37748736 | tf_op jit(solution)/shard_map/sub | solution.py:147
  18.8 0.7 fusion.1
  19.5 1.3 %copy-done = bf16[2,4096,128]{2,1,0:T(8,128)(2,1)} copy-done((bf16[2,4096,128]{2,1,0:T(8,128)(2,1)}, bf16[2,4096,128]{2,1,0:T(8,128)(2,1)S(1)}, u32[]{:S(2)}) %copy-start) | copy-done | bytes 2097176
  20.8 0.8 fusion.20
  21.7 0.8 convolution_add_fusion.2
  22.5 0.8 copy-done.1
  23.3 0.8 convolution_add_fusion.1
  24.2 0.8 %collective-permute-start.4 = (f32[136,128]{1,0:T(8,128)S(1)}, f32[136,128]{1,0:T(8,128)S(1)}, u32[]{:S(2)}, u32[]{:S(2)}) collective-permute-start(f32[136,128]{1,0:T(8,128)S(1)} %maximum_maximum_fusion), channel_id=1, source_target_pairs={{0,1},{1,0},{2,3},{3,2},{4,5},{5,4},{6,7},{7,6},{8,9},{9,8},{10,11... | collective-permute-start | bytes 208904 | tf_op jit(solution)/shard_map/ppermute | solution.py:51
  25.0 0.9 %collective-permute-done.4 = f32[136,128]{1,0:T(8,128)S(1)} collective-permute-done((f32[136,128]{1,0:T(8,128)S(1)}, f32[136,128]{1,0:T(8,128)S(1)}, u32[]{:S(2)}, u32[]{:S(2)}) %collective-permute-start.4) | collective-permute-done | bytes 69664 | tf_op jit(solution)/shard_map/ppermute | solution.py:51
  26.0 1.4 %collective-permute-start.5 = (f32[136,128]{1,0:T(8,128)S(1)}, f32[136,128]{1,0:T(8,128)S(1)}, u32[]{:S(2)}, u32[]{:S(2)}) collective-permute-start(f32[136,128]{1,0:T(8,128)S(1)} %fusion.17), channel_id=1, source_target_pairs={{0,2},{1,3},{2,0},{3,1},{4,6},{5,7},{6,4},{7,5},{8,10},{9,11},{10,... | collective-permute-start | bytes 208904 | tf_op jit(solution)/shard_map/ppermute | solution.py:51
  27.4 3.2 %collective-permute-done.5 = f32[136,128]{1,0:T(8,128)S(1)} collective-permute-done((f32[136,128]{1,0:T(8,128)S(1)}, f32[136,128]{1,0:T(8,128)S(1)}, u32[]{:S(2)}, u32[]{:S(2)}) %collective-permute-start.5) | collective-permute-done | bytes 69664 | tf_op jit(solution)/shard_map/ppermute | solution.py:51
  30.6 1.4 %collective-permute-start.6 = (f32[136,128]{1,0:T(8,128)S(1)}, f32[136,128]{1,0:T(8,128)S(1)}, u32[]{:S(2)}, u32[]{:S(2)}) collective-permute-start(f32[136,128]{1,0:T(8,128)S(1)} %add.43), channel_id=1, source_target_pairs={{0,6},{1,7},{2,4},{3,5},{4,2},{5,3},{6,0},{7,1},{8,14},{9,15},{10,... | collective-permute-start | bytes 208904 | tf_op jit(solution)/shard_map/ppermute | solution.py:51
  31.9 3.0 %collective-permute-done.6 = f32[136,128]{1,0:T(8,128)S(1)} collective-permute-done((f32[136,128]{1,0:T(8,128)S(1)}, f32[136,128]{1,0:T(8,128)S(1)}, u32[]{:S(2)}, u32[]{:S(2)}) %collective-permute-start.6) | collective-permute-done | bytes 69664 | tf_op jit(solution)/shard_map/ppermute | solution.py:51
  35.1 4.3 %collective-permute-done.7 = f32[136,128]{1,0:T(8,128)S(1)} collective-permute-done((f32[136,128]{1,0:T(8,128)S(1)}, f32[136,128]{1,0:T(8,128)S(1)}, u32[]{:S(2)}, u32[]{:S(2)}) %collective-permute-start.7) | collective-permute-done | bytes 69664 | tf_op jit(solution)/shard_map/ppermute | solution.py:51
  39.8 5.0 %collective-permute-done.8 = f32[136,128]{1,0:T(8,128)S(1)} collective-permute-done((f32[136,128]{1,0:T(8,128)S(1)}, f32[136,128]{1,0:T(8,128)S(1)}, u32[]{:S(2)}, u32[]{:S(2)}) %collective-permute-start.8) | collective-permute-done | bytes 69664 | tf_op jit(solution)/shard_map/ppermute | solution.py:51
  44.9 1.0 %collective-permute-start.9 = (f32[136,128]{1,0:T(8,128)S(1)}, f32[136,128]{1,0:T(8,128)S(1)}, u32[]{:S(2)}, u32[]{:S(2)}) collective-permute-start(f32[136,128]{1,0:T(8,128)S(1)} %add.46), channel_id=1, source_target_pairs={{0,56},{8,48},{16,40},{24,32},{32,24},{40,16},{48,8},{56,0},{64,12... | collective-permute-start | bytes 208904 | tf_op jit(solution)/shard_map/ppermute | solution.py:51
  45.9 5.3 %collective-permute-done.9 = f32[136,128]{1,0:T(8,128)S(1)} collective-permute-done((f32[136,128]{1,0:T(8,128)S(1)}, f32[136,128]{1,0:T(8,128)S(1)}, u32[]{:S(2)}, u32[]{:S(2)}) %collective-permute-start.9) | collective-permute-done | bytes 69664 | tf_op jit(solution)/shard_map/ppermute | solution.py:51
  51.3 4.3 %collective-permute-done.10 = f32[136,128]{1,0:T(8,128)S(1)} collective-permute-done((f32[136,128]{1,0:T(8,128)S(1)}, f32[136,128]{1,0:T(8,128)S(1)}, u32[]{:S(2)}, u32[]{:S(2)}) %collective-permute-start.10) | collective-permute-done | bytes 69664 | tf_op jit(solution)/shard_map/ppermute | solution.py:51
  55.6 2.3 %collective-permute-start.11 = (f32[136,128]{1,0:T(8,128)S(1)}, f32[136,128]{1,0:T(8,128)S(1)}, u32[]{:S(2)}, u32[]{:S(2)}) collective-permute-start(f32[136,128]{1,0:T(8,128)S(1)} %add.48), channel_id=1, source_target_pairs={{0,192},{8,200},{16,208},{24,216},{32,224},{40,232},{48,240},{56,2... | collective-permute-start | bytes 208904 | tf_op jit(solution)/shard_map/ppermute | solution.py:51
  57.9 3.5 %collective-permute-done.11 = f32[136,128]{1,0:T(8,128)S(1)} collective-permute-done((f32[136,128]{1,0:T(8,128)S(1)}, f32[136,128]{1,0:T(8,128)S(1)}, u32[]{:S(2)}, u32[]{:S(2)}) %collective-permute-start.11) | collective-permute-done | bytes 69664 | tf_op jit(solution)/shard_map/ppermute | solution.py:51
  61.7 0.7 maximum_multiply_fusion.g_ref
  62.3 12.4 %shard_map.41 = (f32[2,128,128]{2,1,0:T(8,128)}, f32[2,128,128]{2,1,0:T(8,128)}) custom-call(f32[2,128,128]{2,1,0:T(8,128)} %maximum_multiply_fusion.g_ref), custom_call_target="tpu_custom_call" | custom-call | tf_op jit(solution)/shard_map/pallas_call | solution.py:128
  74.7 1.7 %fusion.10 = f32[2,4096,128]{2,1,0:T(8,128)S(1)} fusion(bf16[2,4096,128]{2,1,0:T(8,128)(2,1)S(1)} %get-tuple-element.6, f32[2,128,128]{2,1,0:T(8,128)} %get-tuple-element.8), kind=kOutput, calls=%fused_computation.26 | convolution fusion | flops 268533760 | bytes 6422528 | tf_op jit(solution)/shard_map/pcs,pts->pct/dot_general | solution.py:71
  76.4 0.7 fusion.16
  77.1 0.9 %copy-done.2 = bf16[2,4096,128]{2,1,0:T(8,128)(2,1)S(1)} copy-done((bf16[2,4096,128]{2,1,0:T(8,128)(2,1)S(1)}, bf16[2,4096,128]{2,1,0:T(8,128)(2,1)}, u32[]{:S(2)}) %copy-start.2) | copy-done | bytes 2097176
  78.0 2.7 %fusion = f32[2,4096,128]{2,1,0:T(8,128)} fusion(f32[2,4096,128]{2,1,0:T(8,128)S(1)} %fusion.16, f32[2,4096,128]{2,1,0:T(8,128)S(1)} %fusion.10, bf16[2,4096,128]{2,1,0:T(8,128)(2,1)S(1)} %copy-done.2, f32[2,128,128]{2,1,0:T(8,128)S(1)} %copy-done.4), kind=kOutput, calls=%fused_computation.3 | convolution fusion | flops 270598144 | bytes 14811136 | tf_op jit(solution)/shard_map/pcs,pts->pct/dot_general | solution.py:71
  (33 shorter events, 1.7 us)
Async XLA Ops:
  0.6 15.1 %copy-start.3 = (bf16[2,64,64,128]{3,2,1,0:T(8,128)(2,1)S(1)}, bf16[2,64,64,128]{3,2,1,0:T(8,128)(2,1)}, u32[]{:S(2)}) copy-start(bf16[2,64,64,128]{3,2,1,0:T(8,128)(2,1)} %param.3) | copy-start | bytes 6291460
  1.9 10.9 %collective-permute-start = (bf16[2,64,2,128]{3,2,1,0:T(2,128)(2,1)S(1)}, bf16[2,64,2,128]{3,2,1,0:T(2,128)(2,1)S(1)}, u32[]{:S(2)}, u32[]{:S(2)}) collective-permute-start(bf16[2,64,2,128]{3,2,1,0:T(2,128)(2,1)S(1)} %get-tuple-element.12), channel_id=1, source_target_pairs={{0,8},{8,16},{16,24},{24,32},{32,40},{40,48},{48,56},{56,64},{64,7... | collective-permute-start | bytes 196616 | tf_op jit(solution)/shard_map/ppermute | solution.py:18
  3.9 9.0 %collective-permute-start.1 = (bf16[2,64,2,128]{3,2,1,0:T(2,128)(2,1)S(1)}, bf16[2,64,2,128]{3,2,1,0:T(2,128)(2,1)S(1)}, u32[]{:S(2)}, u32[]{:S(2)}) collective-permute-start(bf16[2,64,2,128]{3,2,1,0:T(2,128)(2,1)S(1)} %get-tuple-element.13), channel_id=1, source_target_pairs={{8,0},{16,8},{24,16},{32,24},{40,32},{48,40},{56,48},{64,56},{72,6... | collective-permute-start | bytes 196616 | tf_op jit(solution)/shard_map/ppermute | solution.py:20
  11.0 4.6 %collective-permute-start.2 = (bf16[2,2,64,128]{3,2,1,0:T(8,128)(2,1)S(1)}, bf16[2,2,64,128]{3,2,1,0:T(8,128)(2,1)S(1)}, u32[]{:S(2)}, u32[]{:S(2)}) collective-permute-start(bf16[2,2,64,128]{3,2,1,0:T(8,128)(2,1)S(1)} %get-tuple-element.14), channel_id=1, source_target_pairs={{0,1},{1,2},{2,3},{3,4},{4,5},{5,6},{6,7},{7,0},{8,9},{9,10},{10,1... | collective-permute-start | bytes 196616 | tf_op jit(solution)/shard_map/ppermute | solution.py:18
  11.1 4.6 %collective-permute-start.3 = (bf16[2,2,64,128]{3,2,1,0:T(8,128)(2,1)S(1)}, bf16[2,2,64,128]{3,2,1,0:T(8,128)(2,1)S(1)}, u32[]{:S(2)}, u32[]{:S(2)}) collective-permute-start(bf16[2,2,64,128]{3,2,1,0:T(8,128)(2,1)S(1)} %get-tuple-element.15), channel_id=1, source_target_pairs={{1,0},{2,1},{3,2},{4,3},{5,4},{6,5},{7,6},{0,7},{9,8},{10,9},{11,1... | collective-permute-start | bytes 196616 | tf_op jit(solution)/shard_map/ppermute | solution.py:20
  19.5 1.3 %copy-start = (bf16[2,4096,128]{2,1,0:T(8,128)(2,1)}, bf16[2,4096,128]{2,1,0:T(8,128)(2,1)S(1)}, u32[]{:S(2)}) copy-start(bf16[2,4096,128]{2,1,0:T(8,128)(2,1)S(1)} %get-tuple-element.7) | copy-start | bytes 6291460
  21.7 1.6 %copy-start.1 = (bf16[2,4096,128]{2,1,0:T(8,128)(2,1)S(1)}, bf16[2,4096,128]{2,1,0:T(8,128)(2,1)}, u32[]{:S(2)}) copy-start(bf16[2,4096,128]{2,1,0:T(8,128)(2,1)} %copy-done) | copy-start | bytes 6291460
  24.2 1.7 %collective-permute-start.4 = (f32[136,128]{1,0:T(8,128)S(1)}, f32[136,128]{1,0:T(8,128)S(1)}, u32[]{:S(2)}, u32[]{:S(2)}) collective-permute-start(f32[136,128]{1,0:T(8,128)S(1)} %maximum_maximum_fusion), channel_id=1, source_target_pairs={{0,1},{1,0},{2,3},{3,2},{4,5},{5,4},{6,7},{7,6},{8,9},{9,8},{10,11... | collective-permute-start | bytes 208904 | tf_op jit(solution)/shard_map/ppermute | solution.py:51
  26.0 4.5 %collective-permute-start.5 = (f32[136,128]{1,0:T(8,128)S(1)}, f32[136,128]{1,0:T(8,128)S(1)}, u32[]{:S(2)}, u32[]{:S(2)}) collective-permute-start(f32[136,128]{1,0:T(8,128)S(1)} %fusion.17), channel_id=1, source_target_pairs={{0,2},{1,3},{2,0},{3,1},{4,6},{5,7},{6,4},{7,5},{8,10},{9,11},{10,... | collective-permute-start | bytes 208904 | tf_op jit(solution)/shard_map/ppermute | solution.py:51
  30.6 4.4 %collective-permute-start.6 = (f32[136,128]{1,0:T(8,128)S(1)}, f32[136,128]{1,0:T(8,128)S(1)}, u32[]{:S(2)}, u32[]{:S(2)}) collective-permute-start(f32[136,128]{1,0:T(8,128)S(1)} %add.43), channel_id=1, source_target_pairs={{0,6},{1,7},{2,4},{3,5},{4,2},{5,3},{6,0},{7,1},{8,14},{9,15},{10,... | collective-permute-start | bytes 208904 | tf_op jit(solution)/shard_map/ppermute | solution.py:51
  35.0 4.4 %collective-permute-start.7 = (f32[136,128]{1,0:T(8,128)S(1)}, f32[136,128]{1,0:T(8,128)S(1)}, u32[]{:S(2)}, u32[]{:S(2)}) collective-permute-start(f32[136,128]{1,0:T(8,128)S(1)} %add.44), channel_id=1, source_target_pairs={{0,8},{8,0},{16,24},{24,16},{32,40},{40,32},{48,56},{56,48},{64,72... | collective-permute-start | bytes 208904 | tf_op jit(solution)/shard_map/ppermute | solution.py:51
  39.4 5.5 %collective-permute-start.8 = (f32[136,128]{1,0:T(8,128)S(1)}, f32[136,128]{1,0:T(8,128)S(1)}, u32[]{:S(2)}, u32[]{:S(2)}) collective-permute-start(f32[136,128]{1,0:T(8,128)S(1)} %add.45), channel_id=1, source_target_pairs={{0,16},{8,24},{16,0},{24,8},{32,48},{40,56},{48,32},{56,40},{64,80... | collective-permute-start | bytes 208904 | tf_op jit(solution)/shard_map/ppermute | solution.py:51
  44.9 6.4 %collective-permute-start.9 = (f32[136,128]{1,0:T(8,128)S(1)}, f32[136,128]{1,0:T(8,128)S(1)}, u32[]{:S(2)}, u32[]{:S(2)}) collective-permute-start(f32[136,128]{1,0:T(8,128)S(1)} %add.46), channel_id=1, source_target_pairs={{0,56},{8,48},{16,40},{24,32},{32,24},{40,16},{48,8},{56,0},{64,12... | collective-permute-start | bytes 208904 | tf_op jit(solution)/shard_map/ppermute | solution.py:51
  51.2 4.4 %collective-permute-start.10 = (f32[136,128]{1,0:T(8,128)S(1)}, f32[136,128]{1,0:T(8,128)S(1)}, u32[]{:S(2)}, u32[]{:S(2)}) collective-permute-start(f32[136,128]{1,0:T(8,128)S(1)} %add.47), channel_id=1, source_target_pairs={{0,64},{8,72},{16,80},{24,88},{32,96},{40,104},{48,112},{56,120},{... | collective-permute-start | bytes 208904 | tf_op jit(solution)/shard_map/ppermute | solution.py:51
  55.6 5.8 %collective-permute-start.11 = (f32[136,128]{1,0:T(8,128)S(1)}, f32[136,128]{1,0:T(8,128)S(1)}, u32[]{:S(2)}, u32[]{:S(2)}) collective-permute-start(f32[136,128]{1,0:T(8,128)S(1)} %add.48), channel_id=1, source_target_pairs={{0,192},{8,200},{16,208},{24,216},{32,224},{40,232},{48,240},{56,2... | collective-permute-start | bytes 208904 | tf_op jit(solution)/shard_map/ppermute | solution.py:51
  74.7 1.7 %copy-start.4 = (f32[2,128,128]{2,1,0:T(8,128)S(1)}, f32[2,128,128]{2,1,0:T(8,128)}, u32[]{:S(2)}) copy-start(f32[2,128,128]{2,1,0:T(8,128)} %get-tuple-element.8) | copy-start | bytes 393220
  76.4 1.6 %copy-start.2 = (bf16[2,4096,128]{2,1,0:T(8,128)(2,1)S(1)}, bf16[2,4096,128]{2,1,0:T(8,128)(2,1)}, u32[]{:S(2)}) copy-start(bf16[2,4096,128]{2,1,0:T(8,128)(2,1)} %copy-done) | copy-start | bytes 6291460

commit v10 on v9

--- a/solution.py
+++ b/solution.py
@@ -27,7 +27,9 @@
 def ring_stages(size):
     stages, step = [], 1
     while step < size:
-        if step * 2 == size and size > 2:
+        if step * 2 == size and size == 8:
+            stages.append([6, 7, 4, 5, 2, 3, 0, 1])
+        elif step * 2 == size and size > 2:
             stages.append([size - 1 - p for p in range(size)])
         else:
             stages.append([p ^ step for p in range(size)])

time: 82.3 us -> 82.3 us (level)
  waiting for transfers between devices: 29.6 us -> 32.1 us
  starting transfers between devices: 17.5 us -> 15.2 us
    ppermute x8, waiting for transfers between devices: 29.6 us -> 32.1 us  [butterfly_sum(): x = x + lax.ppermute(x, axis, [(i, partner[i]) for i in range(count)])]
    ppermute x8, starting transfers between devices: 7.5 us -> 5.23 us  [butterfly_sum(): x = x + lax.ppermute(x, axis, [(i, partner[i]) for i in range(count)])]
where the time goes in v10:
time: 82.3 us; the launch traced here: 81 us
  waiting for transfers between devices  32.1 us (39%)
  starting transfers between devices  15.2 us (18%)
  Pallas kernels  12.4 us (15%)
  other arithmetic  7.56 us (9%)
  matrix products  7.45 us (9%)
  local copies, waits for them, and re-layouts  5.45 us (7%)
  between operations  0.86 us (1%)
    ppermute x8, waiting for transfers between devices, butterfly_sum(): x = x + lax.ppermute(x, axis, [(i, partner[i]) for i in range(count)])  32.1 us
    pallas_call x1, Pallas kernels, chol_inv(): pl.pallas_call(chol_inv_kernel, out_shape=(jax.ShapeDtypeStruct(gram.shap...  12.4 us
    ppermute x2, starting transfers between devices, with_halo(): lax.ppermute(head, axis, [((i + 1) % count, i) for i in range(count)])  7.96 us
    ppermute x8, starting transfers between devices, butterfly_sum(): x = x + lax.ppermute(x, axis, [(i, partner[i]) for i in range(count)])  5.23 us
    dot_general x3, matrix products, dot(): return jnp.einsum('pcs,pts->pct', a, b, preferred_element_type=jnp.float32)  5.11 us
    unnamed x10, local copies, waits for them, and re-layouts  3 us
    convert_element_type x1, other arithmetic, local(): padded_u = with_halo(u_field, (('gz', 2),), 2).astype(jnp.float32)  2.78 us
    sub x1, other arithmetic, local(): vorticity = span_diff / (12.0 * span_step) - stream_diff / 12.0  2.77 us
  transfers between devices with their start and end apart: 12, of which 8 were waited for; matrix products, arithmetic and copies ran while one was open for 5% of the time, Pallas kernels for 0%

profile of v10, /device:TPU:8, one launch (start us, length us, event | category | flops | bytes accessed | tf_op | source)
XLA Modules:
  0.0 81.0 jit_solution(13172290052646210815)
XLA Ops:
  0.6 1.3 %fusion.18 = (bf16[2,64,2,128]{3,2,1,0:T(2,128)(2,1)S(1)}, bf16[2,64,2,128]{3,2,1,0:T(2,128)(2,1)S(1)}) fusion(bf16[2,64,64,128]{3,2,1,0:T(8,128)(2,1)} %param.2), kind=kLoop, calls=%fused_computation.43 | loop fusion | bytes 262144 | tf_op jit(solution)/shard_map/slice | solution.py:15
  1.9 2.0 %collective-permute-start = (bf16[2,64,2,128]{3,2,1,0:T(2,128)(2,1)S(1)}, bf16[2,64,2,128]{3,2,1,0:T(2,128)(2,1)S(1)}, u32[]{:S(2)}, u32[]{:S(2)}) collective-permute-start(bf16[2,64,2,128]{3,2,1,0:T(2,128)(2,1)S(1)} %get-tuple-element.12), channel_id=1, source_target_pairs={{0,8},{8,16},{16,24},{24,32},{32,40},{40,48},{48,56},{56,64},{64,7... | collective-permute-start | bytes 196616 | tf_op jit(solution)/shard_map/ppermute | solution.py:18
  3.9 6.2 %collective-permute-start.1 = (bf16[2,64,2,128]{3,2,1,0:T(2,128)(2,1)S(1)}, bf16[2,64,2,128]{3,2,1,0:T(2,128)(2,1)S(1)}, u32[]{:S(2)}, u32[]{:S(2)}) collective-permute-start(bf16[2,64,2,128]{3,2,1,0:T(2,128)(2,1)S(1)} %get-tuple-element.13), channel_id=1, source_target_pairs={{8,0},{16,8},{24,16},{32,24},{40,32},{48,40},{56,48},{64,56},{72,6... | collective-permute-start | bytes 196616 | tf_op jit(solution)/shard_map/ppermute | solution.py:20
  10.2 0.9 %fusion.19 = (bf16[2,2,64,128]{3,2,1,0:T(8,128)(2,1)S(1)}, bf16[2,2,64,128]{3,2,1,0:T(8,128)(2,1)S(1)}) fusion(bf16[2,64,64,128]{3,2,1,0:T(8,128)(2,1)} %param.3), kind=kLoop, calls=%fused_computation.44 | loop fusion | bytes 262144 | tf_op jit(solution)/shard_map/slice | solution.py:15
  11.1 1.7 %collective-permute-start.3 = (bf16[2,2,64,128]{3,2,1,0:T(8,128)(2,1)S(1)}, bf16[2,2,64,128]{3,2,1,0:T(8,128)(2,1)S(1)}, u32[]{:S(2)}, u32[]{:S(2)}) collective-permute-start(bf16[2,2,64,128]{3,2,1,0:T(8,128)(2,1)S(1)} %get-tuple-element.15), channel_id=1, source_target_pairs={{1,0},{2,1},{3,2},{4,3},{5,4},{6,5},{7,6},{0,7},{9,8},{10,9},{11,1... | collective-permute-start | bytes 196616 | tf_op jit(solution)/shard_map/ppermute | solution.py:20
  12.9 2.8 %maximum_convert_fusion = f32[2,64,68,128]{3,2,1,0:T(8,128)S(1)} fusion(bf16[2,64,2,128]{3,2,1,0:T(2,128)(2,1)S(1)} %collective-permute-done.1, bf16[2,64,64,128]{3,2,1,0:T(8,128)(2,1)} %param.2, bf16[2,64,2,128]{3,2,1,0:T(2,128)(2,1)S(1)} %collective-permute-done), kind=kLoop, calls=%fused_computation.16 | loop fusion | flops 6684672 | bytes 6684672 | tf_op jit(solution)/shard_map/convert_element_type | solution.py:141
  16.0 2.8 %fusion.4 = f32[2,64,64,128]{3,2,1,0:T(8,128)S(1)} fusion(f32[2,68,64,128]{3,2,1,0:T(8,128)S(1)} %maximum_convert_fusion.1, f32[2,64,68,128]{3,2,1,0:T(8,128)S(1)} %maximum_convert_fusion), kind=kLoop, calls=%fused_computation.8 | loop fusion | flops 11534336 | bytes 37748736 | tf_op jit(solution)/shard_map/sub | solution.py:149
  18.8 0.7 fusion.1
  19.5 1.3 %copy-done = bf16[2,4096,128]{2,1,0:T(8,128)(2,1)} copy-done((bf16[2,4096,128]{2,1,0:T(8,128)(2,1)}, bf16[2,4096,128]{2,1,0:T(8,128)(2,1)S(1)}, u32[]{:S(2)}) %copy-start) | copy-done | bytes 2097176
  20.8 0.8 fusion.20
  21.7 0.8 convolution_add_fusion.2
  22.5 0.8 copy-done.1
  23.3 0.8 convolution_add_fusion.1
  24.2 0.8 %collective-permute-start.4 = (f32[136,128]{1,0:T(8,128)S(1)}, f32[136,128]{1,0:T(8,128)S(1)}, u32[]{:S(2)}, u32[]{:S(2)}) collective-permute-start(f32[136,128]{1,0:T(8,128)S(1)} %maximum_maximum_fusion), channel_id=1, source_target_pairs={{0,1},{1,0},{2,3},{3,2},{4,5},{5,4},{6,7},{7,6},{8,9},{9,8},{10,11... | collective-permute-start | bytes 208904 | tf_op jit(solution)/shard_map/ppermute | solution.py:53
  25.0 0.9 %collective-permute-done.4 = f32[136,128]{1,0:T(8,128)S(1)} collective-permute-done((f32[136,128]{1,0:T(8,128)S(1)}, f32[136,128]{1,0:T(8,128)S(1)}, u32[]{:S(2)}, u32[]{:S(2)}) %collective-permute-start.4) | collective-permute-done | bytes 69664 | tf_op jit(solution)/shard_map/ppermute | solution.py:53
  26.0 1.4 %collective-permute-start.5 = (f32[136,128]{1,0:T(8,128)S(1)}, f32[136,128]{1,0:T(8,128)S(1)}, u32[]{:S(2)}, u32[]{:S(2)}) collective-permute-start(f32[136,128]{1,0:T(8,128)S(1)} %fusion.17), channel_id=1, source_target_pairs={{0,2},{1,3},{2,0},{3,1},{4,6},{5,7},{6,4},{7,5},{8,10},{9,11},{10,... | collective-permute-start | bytes 208904 | tf_op jit(solution)/shard_map/ppermute | solution.py:53
  27.4 3.2 %collective-permute-done.5 = f32[136,128]{1,0:T(8,128)S(1)} collective-permute-done((f32[136,128]{1,0:T(8,128)S(1)}, f32[136,128]{1,0:T(8,128)S(1)}, u32[]{:S(2)}, u32[]{:S(2)}) %collective-permute-start.5) | collective-permute-done | bytes 69664 | tf_op jit(solution)/shard_map/ppermute | solution.py:53
  30.6 1.4 %collective-permute-start.6 = (f32[136,128]{1,0:T(8,128)S(1)}, f32[136,128]{1,0:T(8,128)S(1)}, u32[]{:S(2)}, u32[]{:S(2)}) collective-permute-start(f32[136,128]{1,0:T(8,128)S(1)} %add.43), channel_id=1, source_target_pairs={{0,6},{1,7},{2,4},{3,5},{4,2},{5,3},{6,0},{7,1},{8,14},{9,15},{10,... | collective-permute-start | bytes 208904 | tf_op jit(solution)/shard_map/ppermute | solution.py:53
  31.9 3.0 %collective-permute-done.6 = f32[136,128]{1,0:T(8,128)S(1)} collective-permute-done((f32[136,128]{1,0:T(8,128)S(1)}, f32[136,128]{1,0:T(8,128)S(1)}, u32[]{:S(2)}, u32[]{:S(2)}) %collective-permute-start.6) | collective-permute-done | bytes 69664 | tf_op jit(solution)/shard_map/ppermute | solution.py:53
  35.1 4.3 %collective-permute-done.7 = f32[136,128]{1,0:T(8,128)S(1)} collective-permute-done((f32[136,128]{1,0:T(8,128)S(1)}, f32[136,128]{1,0:T(8,128)S(1)}, u32[]{:S(2)}, u32[]{:S(2)}) %collective-permute-start.7) | collective-permute-done | bytes 69664 | tf_op jit(solution)/shard_map/ppermute | solution.py:53
  39.4 0.5 collective-permute-start.8
  39.8 5.1 %collective-permute-done.8 = f32[136,128]{1,0:T(8,128)S(1)} collective-permute-done((f32[136,128]{1,0:T(8,128)S(1)}, f32[136,128]{1,0:T(8,128)S(1)}, u32[]{:S(2)}, u32[]{:S(2)}) %collective-permute-start.8) | collective-permute-done | bytes 69664 | tf_op jit(solution)/shard_map/ppermute | solution.py:53
  45.2 6.3 %collective-permute-done.9 = f32[136,128]{1,0:T(8,128)S(1)} collective-permute-done((f32[136,128]{1,0:T(8,128)S(1)}, f32[136,128]{1,0:T(8,128)S(1)}, u32[]{:S(2)}, u32[]{:S(2)}) %collective-permute-start.9) | collective-permute-done | bytes 69664 | tf_op jit(solution)/shard_map/ppermute | solution.py:53
  51.6 4.3 %collective-permute-done.10 = f32[136,128]{1,0:T(8,128)S(1)} collective-permute-done((f32[136,128]{1,0:T(8,128)S(1)}, f32[136,128]{1,0:T(8,128)S(1)}, u32[]{:S(2)}, u32[]{:S(2)}) %collective-permute-start.10) | collective-permute-done | bytes 69664 | tf_op jit(solution)/shard_map/ppermute | solution.py:53
  55.9 0.8 %collective-permute-start.11 = (f32[136,128]{1,0:T(8,128)S(1)}, f32[136,128]{1,0:T(8,128)S(1)}, u32[]{:S(2)}, u32[]{:S(2)}) collective-permute-start(f32[136,128]{1,0:T(8,128)S(1)} %add.48), channel_id=1, source_target_pairs={{0,192},{8,200},{16,208},{24,216},{32,224},{40,232},{48,240},{56,2... | collective-permute-start | bytes 208904 | tf_op jit(solution)/shard_map/ppermute | solution.py:53
  56.7 5.0 %collective-permute-done.11 = f32[136,128]{1,0:T(8,128)S(1)} collective-permute-done((f32[136,128]{1,0:T(8,128)S(1)}, f32[136,128]{1,0:T(8,128)S(1)}, u32[]{:S(2)}, u32[]{:S(2)}) %collective-permute-start.11) | collective-permute-done | bytes 69664 | tf_op jit(solution)/shard_map/ppermute | solution.py:53
  61.9 0.7 maximum_multiply_fusion.g_ref
  62.6 12.4 %shard_map.41 = (f32[2,128,128]{2,1,0:T(8,128)}, f32[2,128,128]{2,1,0:T(8,128)}) custom-call(f32[2,128,128]{2,1,0:T(8,128)} %maximum_multiply_fusion.g_ref), custom_call_target="tpu_custom_call" | custom-call | tf_op jit(solution)/shard_map/pallas_call | solution.py:130
  75.0 1.7 %fusion.10 = f32[2,4096,128]{2,1,0:T(8,128)S(1)} fusion(bf16[2,4096,128]{2,1,0:T(8,128)(2,1)S(1)} %get-tuple-element.6, f32[2,128,128]{2,1,0:T(8,128)} %get-tuple-element.8), kind=kOutput, calls=%fused_computation.26 | convolution fusion | flops 268533760 | bytes 6422528 | tf_op jit(solution)/shard_map/pcs,pts->pct/dot_general | solution.py:73
  76.7 0.7 fusion.16
  77.4 0.9 %copy-done.2 = bf16[2,4096,128]{2,1,0:T(8,128)(2,1)S(1)} copy-done((bf16[2,4096,128]{2,1,0:T(8,128)(2,1)S(1)}, bf16[2,4096,128]{2,1,0:T(8,128)(2,1)}, u32[]{:S(2)}) %copy-start.2) | copy-done | bytes 2097176
  78.3 2.7 %fusion = f32[2,4096,128]{2,1,0:T(8,128)} fusion(f32[2,4096,128]{2,1,0:T(8,128)S(1)} %fusion.16, f32[2,4096,128]{2,1,0:T(8,128)S(1)} %fusion.10, bf16[2,4096,128]{2,1,0:T(8,128)(2,1)S(1)} %copy-done.2, f32[2,128,128]{2,1,0:T(8,128)S(1)} %copy-done.4), kind=kOutput, calls=%fused_computation.3 | convolution fusion | flops 270598144 | bytes 14811136 | tf_op jit(solution)/shard_map/pcs,pts->pct/dot_general | solution.py:73
  (33 shorter events, 1.4 us)
Async XLA Ops:
  0.6 15.1 %copy-start.3 = (bf16[2,64,64,128]{3,2,1,0:T(8,128)(2,1)S(1)}, bf16[2,64,64,128]{3,2,1,0:T(8,128)(2,1)}, u32[]{:S(2)}) copy-start(bf16[2,64,64,128]{3,2,1,0:T(8,128)(2,1)} %param.3) | copy-start | bytes 6291460
  1.9 10.9 %collective-permute-start = (bf16[2,64,2,128]{3,2,1,0:T(2,128)(2,1)S(1)}, bf16[2,64,2,128]{3,2,1,0:T(2,128)(2,1)S(1)}, u32[]{:S(2)}, u32[]{:S(2)}) collective-permute-start(bf16[2,64,2,128]{3,2,1,0:T(2,128)(2,1)S(1)} %get-tuple-element.12), channel_id=1, source_target_pairs={{0,8},{8,16},{16,24},{24,32},{32,40},{40,48},{48,56},{56,64},{64,7... | collective-permute-start | bytes 196616 | tf_op jit(solution)/shard_map/ppermute | solution.py:18
  3.9 9.0 %collective-permute-start.1 = (bf16[2,64,2,128]{3,2,1,0:T(2,128)(2,1)S(1)}, bf16[2,64,2,128]{3,2,1,0:T(2,128)(2,1)S(1)}, u32[]{:S(2)}, u32[]{:S(2)}) collective-permute-start(bf16[2,64,2,128]{3,2,1,0:T(2,128)(2,1)S(1)} %get-tuple-element.13), channel_id=1, source_target_pairs={{8,0},{16,8},{24,16},{32,24},{40,32},{48,40},{56,48},{64,56},{72,6... | collective-permute-start | bytes 196616 | tf_op jit(solution)/shard_map/ppermute | solution.py:20
  11.0 4.6 %collective-permute-start.2 = (bf16[2,2,64,128]{3,2,1,0:T(8,128)(2,1)S(1)}, bf16[2,2,64,128]{3,2,1,0:T(8,128)(2,1)S(1)}, u32[]{:S(2)}, u32[]{:S(2)}) collective-permute-start(bf16[2,2,64,128]{3,2,1,0:T(8,128)(2,1)S(1)} %get-tuple-element.14), channel_id=1, source_target_pairs={{0,1},{1,2},{2,3},{3,4},{4,5},{5,6},{6,7},{7,0},{8,9},{9,10},{10,1... | collective-permute-start | bytes 196616 | tf_op jit(solution)/shard_map/ppermute | solution.py:18
  11.1 4.6 %collective-permute-start.3 = (bf16[2,2,64,128]{3,2,1,0:T(8,128)(2,1)S(1)}, bf16[2,2,64,128]{3,2,1,0:T(8,128)(2,1)S(1)}, u32[]{:S(2)}, u32[]{:S(2)}) collective-permute-start(bf16[2,2,64,128]{3,2,1,0:T(8,128)(2,1)S(1)} %get-tuple-element.15), channel_id=1, source_target_pairs={{1,0},{2,1},{3,2},{4,3},{5,4},{6,5},{7,6},{0,7},{9,8},{10,9},{11,1... | collective-permute-start | bytes 196616 | tf_op jit(solution)/shard_map/ppermute | solution.py:20
  19.5 1.3 %copy-start = (bf16[2,4096,128]{2,1,0:T(8,128)(2,1)}, bf16[2,4096,128]{2,1,0:T(8,128)(2,1)S(1)}, u32[]{:S(2)}) copy-start(bf16[2,4096,128]{2,1,0:T(8,128)(2,1)S(1)} %get-tuple-element.7) | copy-start | bytes 6291460
  21.7 1.6 %copy-start.1 = (bf16[2,4096,128]{2,1,0:T(8,128)(2,1)S(1)}, bf16[2,4096,128]{2,1,0:T(8,128)(2,1)}, u32[]{:S(2)}) copy-start(bf16[2,4096,128]{2,1,0:T(8,128)(2,1)} %copy-done) | copy-start | bytes 6291460
  24.2 1.7 %collective-permute-start.4 = (f32[136,128]{1,0:T(8,128)S(1)}, f32[136,128]{1,0:T(8,128)S(1)}, u32[]{:S(2)}, u32[]{:S(2)}) collective-permute-start(f32[136,128]{1,0:T(8,128)S(1)} %maximum_maximum_fusion), channel_id=1, source_target_pairs={{0,1},{1,0},{2,3},{3,2},{4,5},{5,4},{6,7},{7,6},{8,9},{9,8},{10,11... | collective-permute-start | bytes 208904 | tf_op jit(solution)/shard_map/ppermute | solution.py:53
  26.0 4.5 %collective-permute-start.5 = (f32[136,128]{1,0:T(8,128)S(1)}, f32[136,128]{1,0:T(8,128)S(1)}, u32[]{:S(2)}, u32[]{:S(2)}) collective-permute-start(f32[136,128]{1,0:T(8,128)S(1)} %fusion.17), channel_id=1, source_target_pairs={{0,2},{1,3},{2,0},{3,1},{4,6},{5,7},{6,4},{7,5},{8,10},{9,11},{10,... | collective-permute-start | bytes 208904 | tf_op jit(solution)/shard_map/ppermute | solution.py:53
  30.6 4.4 %collective-permute-start.6 = (f32[136,128]{1,0:T(8,128)S(1)}, f32[136,128]{1,0:T(8,128)S(1)}, u32[]{:S(2)}, u32[]{:S(2)}) collective-permute-start(f32[136,128]{1,0:T(8,128)S(1)} %add.43), channel_id=1, source_target_pairs={{0,6},{1,7},{2,4},{3,5},{4,2},{5,3},{6,0},{7,1},{8,14},{9,15},{10,... | collective-permute-start | bytes 208904 | tf_op jit(solution)/shard_map/ppermute | solution.py:53
  35.0 4.4 %collective-permute-start.7 = (f32[136,128]{1,0:T(8,128)S(1)}, f32[136,128]{1,0:T(8,128)S(1)}, u32[]{:S(2)}, u32[]{:S(2)}) collective-permute-start(f32[136,128]{1,0:T(8,128)S(1)} %add.44), channel_id=1, source_target_pairs={{0,8},{8,0},{16,24},{24,16},{32,40},{40,32},{48,56},{56,48},{64,72... | collective-permute-start | bytes 208904 | tf_op jit(solution)/shard_map/ppermute | solution.py:53
  39.4 5.6 %collective-permute-start.8 = (f32[136,128]{1,0:T(8,128)S(1)}, f32[136,128]{1,0:T(8,128)S(1)}, u32[]{:S(2)}, u32[]{:S(2)}) collective-permute-start(f32[136,128]{1,0:T(8,128)S(1)} %add.45), channel_id=1, source_target_pairs={{0,16},{8,24},{16,0},{24,8},{32,48},{40,56},{48,32},{56,40},{64,80... | collective-permute-start | bytes 208904 | tf_op jit(solution)/shard_map/ppermute | solution.py:53
  45.0 6.5 %collective-permute-start.9 = (f32[136,128]{1,0:T(8,128)S(1)}, f32[136,128]{1,0:T(8,128)S(1)}, u32[]{:S(2)}, u32[]{:S(2)}) collective-permute-start(f32[136,128]{1,0:T(8,128)S(1)} %add.46), channel_id=1, source_target_pairs={{0,48},{8,56},{16,32},{24,40},{32,16},{40,24},{48,0},{56,8},{64,11... | collective-permute-start | bytes 208904 | tf_op jit(solution)/shard_map/ppermute | solution.py:53
  51.5 4.4 %collective-permute-start.10 = (f32[136,128]{1,0:T(8,128)S(1)}, f32[136,128]{1,0:T(8,128)S(1)}, u32[]{:S(2)}, u32[]{:S(2)}) collective-permute-start(f32[136,128]{1,0:T(8,128)S(1)} %add.47), channel_id=1, source_target_pairs={{0,64},{8,72},{16,80},{24,88},{32,96},{40,104},{48,112},{56,120},{... | collective-permute-start | bytes 208904 | tf_op jit(solution)/shard_map/ppermute | solution.py:53
  55.9 5.8 %collective-permute-start.11 = (f32[136,128]{1,0:T(8,128)S(1)}, f32[136,128]{1,0:T(8,128)S(1)}, u32[]{:S(2)}, u32[]{:S(2)}) collective-permute-start(f32[136,128]{1,0:T(8,128)S(1)} %add.48), channel_id=1, source_target_pairs={{0,192},{8,200},{16,208},{24,216},{32,224},{40,232},{48,240},{56,2... | collective-permute-start | bytes 208904 | tf_op jit(solution)/shard_map/ppermute | solution.py:53
  75.0 1.7 %copy-start.4 = (f32[2,128,128]{2,1,0:T(8,128)S(1)}, f32[2,128,128]{2,1,0:T(8,128)}, u32[]{:S(2)}) copy-start(f32[2,128,128]{2,1,0:T(8,128)} %get-tuple-element.8) | copy-start | bytes 393220
  76.7 1.6 %copy-start.2 = (bf16[2,4096,128]{2,1,0:T(8,128)(2,1)S(1)}, bf16[2,4096,128]{2,1,0:T(8,128)(2,1)}, u32[]{:S(2)}) copy-start(bf16[2,4096,128]{2,1,0:T(8,128)(2,1)} %copy-done) | copy-start | bytes 6291460
